TPU v7x, 256 devices: a whole 4x4x8 slice. The times are simulated.
256 devices in a mesh: member: 8 (over x, y_hi), space: 32 (over y_lo, z, core).
Axes of the slice: x: 4, y: 4 (y_hi: 2, y_lo: 2; y = y_hi * 2 + y_lo), z: 8, core: 2. Of those that a mesh axis runs over, the one named last changes fastest.
Arguments:
- ensemble: bfloat16 [256, 48, 16384], P('member', None, 'space')
- inflation: float32 [256, 128], P('member'), may hold values from 0.5 to 2
- weights: bfloat16 [128, 256, 256], P('space')
- region_ids: int32 [16384], P('space'), may hold values from 0 to 127, as said below
- extinction: float32 [48], replicated, may hold values from 0.1 to 2
- obs_cols: int32 [4096], P('space'), may hold values from 0 to 16383, as said below
Outputs:
- analysis: bfloat16 [256, 48, 16384], P('member', None, 'space')
- obs_analysis: float32 [256, 4096], P('member', 'space')
Inputs may be any that keep to these rules, and one draw needn't show every extreme that they name: `region_ids`: region r belongs to index r // 4 of space. Each block of 512 columns held by one index of space holds exactly 16 columns of the regions of every index of space. `obs_cols`: each observation's column lies in the block of 512 columns held by the same index of space as the observation.
All inputs are finite; a program needn't handle non-finite values.
Results may differ from a plain program's by a relative error of at most 0.0047.
Values may be sent and summed in bfloat16 or wider, within the bound.
No kernel may reach another device: no remote copies, remote signals or barrier semaphores. Data moves between devices by JAX's collectives and lax.ppermute only.
A program may use at most 64 MiB of HBM per device.

v0:
```python
import jax
import jax.numpy as jnp
from jax import lax
from jax.sharding import PartitionSpec as P


def local(ensemble, inflation, weights, region_ids, extinction, obs_cols):
    n_space = lax.axis_size("space")
    n_member = lax.axis_size("member")
    local_members = ensemble.shape[0]
    tracers = ensemble.shape[1]
    columns = ensemble.shape[2]
    members = local_members * n_member
    reg_count = weights.shape[0]
    all_regions = inflation.shape[1]
    send_cols = columns // n_space
    slot_cols = send_cols // n_member
    own_cols = n_space * slot_cols
    owner = region_ids // reg_count
    owner_hot = (owner[:, None] == jnp.arange(n_space, dtype=jnp.int32)[None, :]).astype(jnp.int32)
    before = jnp.cumsum(owner_hot, axis=0) - owner_hot
    rank_in = jnp.sum(before * owner_hot, axis=1)
    position = owner * send_cols + rank_in
    ordering = (
        jnp.zeros((columns,), jnp.int32).at[position].set(jnp.arange(columns, dtype=jnp.int32))
    )
    labels_all = jnp.take(region_ids % reg_count, ordering).reshape(n_space, n_member, slot_cols)
    my_labels = lax.dynamic_index_in_dim(labels_all, lax.axis_index("member"), 1, keepdims=False)
    got_labels = lax.all_to_all(
        my_labels, "space", split_axis=0, concat_axis=0, tiled=True
    ).reshape(own_cols)
    summed = lax.psum(jnp.sum(ensemble, axis=0, dtype=jnp.float32), "member")
    mean = summed / members
    region_hot = (jnp.arange(all_regions, dtype=jnp.int32)[:, None] == region_ids[None, :]).astype(
        jnp.float32
    )
    factor = jnp.dot(inflation, region_hot, precision=lax.Precision.HIGHEST)
    outgoing = ((ensemble.astype(jnp.float32) - mean[None]) * factor[:, None, :]).astype(
        jnp.bfloat16
    )
    rows_major = jnp.transpose(outgoing, (2, 0, 1)).reshape(columns, local_members * tracers)
    payload = jnp.take(rows_major, ordering, axis=0).reshape(
        n_space, n_member, slot_cols, local_members * tracers
    )
    received = lax.all_to_all(
        lax.all_to_all(payload, "member", split_axis=1, concat_axis=3, tiled=True),
        "space",
        split_axis=0,
        concat_axis=0,
        tiled=True,
    )
    gathered = received.reshape(own_cols, members, tracers)
    accum = jnp.zeros((own_cols, members, tracers), jnp.float32)
    for region in range(reg_count):
        partial_prod = jnp.einsum(
            "jk,cjt->ckt", weights[region], gathered, preferred_element_type=jnp.float32
        )
        accum = accum + jnp.where((got_labels == region)[:, None, None], partial_prod, 0.0)
    increment = accum.astype(jnp.bfloat16)
    result_rows = increment
    result_rows = result_rows.reshape(n_space, 1, slot_cols, members * tracers)
    halfway = lax.all_to_all(result_rows, "space", split_axis=0, concat_axis=0, tiled=True)
    returned = lax.all_to_all(halfway, "member", split_axis=3, concat_axis=1, tiled=True)
    restored = jnp.take(returned.reshape(columns, local_members * tracers), position, axis=0)
    restored = jnp.transpose(restored.reshape(columns, local_members, tracers), (1, 2, 0))
    analysis = (mean[None] + restored.astype(jnp.float32)).astype(jnp.bfloat16)
    local_index = obs_cols - lax.axis_index("space") * columns
    picked = jnp.take(analysis, local_index, axis=2).astype(jnp.float32)
    obs_analysis = jnp.einsum("t,kto->ko", extinction, picked, precision=lax.Precision.HIGHEST)
    return (analysis, obs_analysis)


def solution(mesh):
    in_specs = (
        P("member", None, "space"),
        P("member", None),
        P("space", None, None),
        P("space"),
        P(),
        P("space"),
    )
    out_specs = (P("member", None, "space"), P("member", "space"))
    return jax.shard_map(local, mesh=mesh, in_specs=in_specs, out_specs=out_specs, check_vma=False)
```

profile of v0, /device:TPU:1, one launch (start us, length us, event | category | flops | bytes accessed | tf_op | source)
XLA Modules:
  0.0 388.2 jit_solution(15727001249137828852)
XLA Ops:
  7.2 7.2 %copy.60 = bf16[32,48,512]{1,0,2:T(8,128)(2,1)} copy(bf16[32,48,512]{2,1,0:T(8,128)(2,1)} %param.8) | data formatting | bytes 3145728 | tf_op args[0]
  14.5 4.8 %convert_reduce_fusion = f32[48,512]{0,1:T(8,128)} fusion(bf16[32,48,512]{1,0,2:T(8,128)(2,1)} %copy.60), kind=kLoop, calls=%fused_computation.6 | loop fusion | flops 1548288 | bytes 1671168 | tf_op jit(solution)/shard_map/reduce_sum | solution.py:32
  27.2 80.2 %all-reduce.2.cloned.1.call-done = f32[48,512]{0,1:T(8,128)} async-done(((f32[48,512]{0,1:T(8,128)}), f32[48,512]{0,1:T(8,128)}) %all-reduce.2.cloned.1.call-update) | async-done | bytes 98320 | tf_op jit(solution)/shard_map/psum | solution.py:32
  108.3 5.8 %fusion.3 = bf16[512,32,48]{2,1,0:T(8,128)(2,1)} fusion(bf16[32,48,512]{1,0,2:T(8,128)(2,1)} %copy.60, f32[32,512]{0,1:T(8,128)S(1)} %copy.62, f32[48,512]{0,1:T(8,128)S(1)} %broadcast_multiply_fusion), kind=kLoop, calls=%fused_computation.11 | loop fusion | flops 3145728 | bytes 3309568 | tf_op jit(solution)/shard_map/transpose | solution.py:41
  114.1 4.4 %copy.63 = bf16[512,32,48]{0,2,1:T(8,128)(2,1)S(1)} copy(bf16[512,32,48]{2,1,0:T(8,128)(2,1)} %fusion.3) | data formatting | bytes 3145728 | tf_op jit(solution)/shard_map/transpose | solution.py:41
  126.9 3.6 all-to-all-start.1
  131.2 16.8 %all-to-all-done.1 = bf16[32,8,2,1536]{3,2,0,1:T(2,128)(2,1)S(1)} async-done(((bf16[32,8,2,1536]{3,2,0,1:T(2,128)(2,1)}), bf16[32,8,2,1536]{3,2,0,1:T(2,128)(2,1)S(1)}, u32[]{:S(2)}, u32[]{:S(2)}) %all-to-all-start.1) | async-done | bytes 1572896 | tf_op jit(solution)/shard_map/all_to_all | solution.py:46
  148.0 13.4 %all-to-all-start = ((s32[32,1,2]{2,1,0:T(1,128)}), s32[32,1,2]{2,1,0:T(1,128)S(1)}, u32[]{:S(2)}, u32[]{:S(2)}) async-start(s32[32,1,2]{2,1,0:T(1,128)} %constant_dynamic-slice_fusion), calls=%async_computation | async-start | bytes 32768 | tf_op jit(solution)/shard_map/all_to_all | solution.py:29
  164.8 4.4 %all-to-all-done = s32[32,1,2]{2,1,0:T(1,128)S(1)} async-done(((s32[32,1,2]{2,1,0:T(1,128)}), s32[32,1,2]{2,1,0:T(1,128)S(1)}, u32[]{:S(2)}, u32[]{:S(2)}) %all-to-all-start) | async-done | bytes 288 | tf_op jit(solution)/shard_map/all_to_all | solution.py:29
  169.2 4.4 %all-to-all-start.2 = ((bf16[32,1,2,12288]{3,2,1,0:T(2,128)(2,1)}), bf16[32,1,2,12288]{3,2,1,0:T(2,128)(2,1)S(1)}, u32[]{:S(2)}, u32[]{:S(2)}) async-start(bf16[32,1,2,12288]{3,2,1,0:T(2,128)(2,1)} %reshape.160), calls=%async_computation.2 | async-start | bytes 3145728 | tf_op jit(solution)/shard_map/all_to_all | solution.py:45
  174.3 37.7 %all-to-all-done.2 = bf16[32,1,2,12288]{3,2,1,0:T(2,128)(2,1)S(1)} async-done(((bf16[32,1,2,12288]{3,2,1,0:T(2,128)(2,1)}), bf16[32,1,2,12288]{3,2,1,0:T(2,128)(2,1)S(1)}, u32[]{:S(2)}, u32[]{:S(2)}) %all-to-all-start.2) | async-done | bytes 1572896 | tf_op jit(solution)/shard_map/all_to_all | solution.py:45
  212.1 5.2 %reshape.101 = bf16[64,256,48]{2,1,0:T(8,128)(2,1)} reshape(bf16[32,1,2,12288]{3,2,1,0:T(2,128)(2,1)S(1)} %all-to-all-done.2) | data formatting | bytes 3145728 | tf_op jit(solution)/shard_map/reshape | solution.py:52
  217.2 3.6 fusion.10
  228.9 9.3 %reshape.102 = bf16[32,1,2,12288]{3,2,0,1:T(2,128)(2,1)S(1)} reshape(bf16[64,256,48]{2,1,0:T(8,128)(2,1)} %copy.72) | data formatting | bytes 3145728 | tf_op jit(solution)/shard_map/reshape | solution.py:61
  238.2 44.1 %all_to_all.49 = bf16[32,1,2,12288]{3,2,1,0:T(2,128)(2,1)S(1)} all-to-all(bf16[32,1,2,12288]{3,2,1,0:T(2,128)(2,1)S(1)} %bitcast.79), channel_id=1, replica_groups=mesh['member'=8,'space'=32] {'space'}, dimensions={0} | all-to-all | bytes 3145728 | tf_op jit(solution)/shard_map/all_to_all | solution.py:62
  282.3 11.1 %copy.74 = bf16[32,1,2,12288]{0,2,1,3:T(2,128)(2,1)} copy(bf16[32,1,2,12288]{3,2,1,0:T(2,128)(2,1)S(1)} %all_to_all.49) | data formatting | bytes 3145728 | tf_op jit(solution)/shard_map/all_to_all | solution.py:62
  293.4 9.5 %reshape.168 = bf16[8,2,49152]{2,1,0:T(2,128)(2,1)} reshape(bf16[12288,1,2,32]{3,2,1,0:T(2,128)(2,1)} %bitcast.74) | data formatting | bytes 3145728
  302.9 4.5 %all-to-all-start.4 = ((bf16[8,2,49152]{2,1,0:T(2,128)(2,1)}), bf16[8,2,49152]{2,1,0:T(2,128)(2,1)S(1)}, u32[]{:S(2)}, u32[]{:S(2)}) async-start(bf16[8,2,49152]{2,1,0:T(2,128)(2,1)} %reshape.168), calls=%async_computation.4 | async-start | bytes 3145728 | tf_op jit(solution)/shard_map/all_to_all | solution.py:63
  307.4 20.9 %all-to-all-done.4 = bf16[8,2,49152]{2,1,0:T(2,128)(2,1)S(1)} async-done(((bf16[8,2,49152]{2,1,0:T(2,128)(2,1)}), bf16[8,2,49152]{2,1,0:T(2,128)(2,1)S(1)}, u32[]{:S(2)}, u32[]{:S(2)}) %all-to-all-start.4) | async-done | bytes 1572896 | tf_op jit(solution)/shard_map/all_to_all | solution.py:63
  328.4 5.4 %reshape.169 = bf16[12288,1,2,32]{3,2,1,0:T(2,128)(2,1)} reshape(bf16[8,2,49152]{2,1,0:T(2,128)(2,1)S(1)} %all-to-all-done.4) | data formatting | bytes 3145728
  333.8 14.4 %copy.75 = bf16[32,1,2,8,1536]{4,2,3,0,1:T(2,128)(2,1)S(1)} copy(bf16[32,1,2,8,1536]{0,2,4,3,1:T(2,128)(2,1)} %bitcast.75) | data formatting | bytes 3145728 | tf_op jit(solution)/shard_map/all_to_all | solution.py:63
  356.0 8.8 %copy.77 = f32[512,32,48]{2,1,0:T(8,128)} copy(f32[512,32,48]{0,2,1:T(8,128)} %bitcast.76) | data formatting | bytes 6291456 | tf_op jit(solution)/shard_map/convert_element_type | solution.py:66
  364.7 6.5 %fusion.2 = bf16[32,48,512]{1,0,2:T(8,128)(2,1)} fusion(f32[512,32,48]{2,1,0:T(8,128)} %copy.77, f32[48,512]{0,1:T(8,128)S(1)} %broadcast_multiply_fusion), kind=kLoop, calls=%fused_computation.10 | loop fusion | flops 1572864 | bytes 4816896 | tf_op jit(solution)/shard_map/convert_element_type | solution.py:66
  371.3 5.4 %copy.78 = bf16[32,48,512]{2,1,0:T(8,128)(2,1)} copy(bf16[32,48,512]{1,0,2:T(8,128)(2,1)} %fusion.2) | data formatting | bytes 3145728
  (61 shorter events, 42.4 us)
Async XLA Ops:
  7.2 16.2 %copy-start = (f32[32,128]{1,0:T(8,128)S(1)}, f32[32,128]{1,0:T(8,128)}, u32[]{:S(2)}) copy-start(f32[32,128]{1,0:T(8,128)} %param.9) | copy-start | bytes 49156
  7.2 100.2 %all-reduce.2.cloned.1.call-start = ((), (), s32[]{:S(2)}) async-start(), calls=%async_computation.5 | async-start | bytes 524288 | tf_op jit(solution)/shard_map/psum | solution.py:32
  14.5 4.8 %copy-start.4 = (s32[512]{0:T(512)S(1)}, s32[512]{0:T(512)}, u32[]{:S(2)}) copy-start(s32[512]{0:T(512)} %param.11) | copy-start | bytes 6148
  126.9 21.1 %all-to-all-start.1 = ((bf16[32,8,2,1536]{3,2,0,1:T(2,128)(2,1)}), bf16[32,8,2,1536]{3,2,0,1:T(2,128)(2,1)S(1)}, u32[]{:S(2)}, u32[]{:S(2)}) async-start(bf16[32,8,2,1536]{3,2,0,1:T(2,128)(2,1)} %copy.65), calls=%async_computation.1 | async-start | bytes 3145728 | tf_op jit(solution)/shard_map/all_to_all | solution.py:46
  148.0 21.2 %all-to-all-start = ((s32[32,1,2]{2,1,0:T(1,128)}), s32[32,1,2]{2,1,0:T(1,128)S(1)}, u32[]{:S(2)}, u32[]{:S(2)}) async-start(s32[32,1,2]{2,1,0:T(1,128)} %constant_dynamic-slice_fusion), calls=%async_computation | async-start | bytes 32768 | tf_op jit(solution)/shard_map/all_to_all | solution.py:29
  169.2 42.8 %all-to-all-start.2 = ((bf16[32,1,2,12288]{3,2,1,0:T(2,128)(2,1)}), bf16[32,1,2,12288]{3,2,1,0:T(2,128)(2,1)S(1)}, u32[]{:S(2)}, u32[]{:S(2)}) async-start(bf16[32,1,2,12288]{3,2,1,0:T(2,128)(2,1)} %reshape.160), calls=%async_computation.2 | async-start | bytes 3145728 | tf_op jit(solution)/shard_map/all_to_all | solution.py:45
  173.6 43.6 %copy-start.3 = (bf16[4,256,256]{2,1,0:T(8,128)(2,1)S(1)}, bf16[4,256,256]{2,1,0:T(8,128)(2,1)}, u32[]{:S(2)}) copy-start(bf16[4,256,256]{2,1,0:T(8,128)(2,1)} %param.10) | copy-start | bytes 1572868
  217.2 3.6 copy-start.2
  302.9 4.5 %copy-start.6 = (s32[128]{0:T(128)S(1)}, s32[128]{0:T(128)}, u32[]{:S(2)}) copy-start(s32[128]{0:T(128)} %param.13) | copy-start | bytes 1540
  302.9 25.5 %all-to-all-start.4 = ((bf16[8,2,49152]{2,1,0:T(2,128)(2,1)}), bf16[8,2,49152]{2,1,0:T(2,128)(2,1)S(1)}, u32[]{:S(2)}, u32[]{:S(2)}) async-start(bf16[8,2,49152]{2,1,0:T(2,128)(2,1)} %reshape.168), calls=%async_computation.4 | async-start | bytes 3145728 | tf_op jit(solution)/shard_map/all_to_all | solution.py:63
  371.3 8.5 %copy-start.5 = (f32[48]{0:T(128)S(1)}, f32[48]{0:T(128)}, u32[]{:S(2)}) copy-start(f32[48]{0:T(128)} %param.12) | copy-start | bytes 580
  371.3 10.1 %copy-start.1 = (f32[32,128]{1,0:T(8,128)S(1)}, f32[32,128]{1,0:T(8,128)}, u32[]{:S(2)}) copy-start(f32[32,128]{1,0:T(8,128)} %param.9) | copy-start | bytes 49156
Sparse Core Ops, SparseCore 0:
  19.4 87.9 all-reduce.1
where the time goes:
time: 391 us; the launch traced here: 388 us
  waiting for transfers between devices  160 us (41%)
  local copies, waits for them, and re-layouts  110 us (28%)
  blocking collectives  44.1 us (11%)
  starting transfers between devices  26 us (7%)
  other arithmetic  23.1 us (6%)
  between operations  14.4 us (4%)
  matrix products  10.2 us (3%)
    psum x1, waiting for transfers between devices, local(): summed = lax.psum(jnp.sum(ensemble, axis=0, dtype=jnp.float32), 'member')  80.2 us
    all_to_all x1, blocking collectives, local(): lax.all_to_all(result_rows, 'space', split_axis=0, concat_axis=0, tiled=T...  44.1 us
    all_to_all x1, waiting for transfers between devices, local(): lax.all_to_all(lax.all_to_all(payload, 'member', split_axis=1, concat_axi...  37.7 us
    unnamed x18, local copies, waits for them, and re-layouts  27.6 us
    all_to_all x1, waiting for transfers between devices, local(): lax.all_to_all(halfway, 'member', split_axis=3, concat_axis=1, tiled=True)  20.9 us
    all_to_all x1, waiting for transfers between devices, local(): lax.all_to_all(payload, 'member', split_axis=1, concat_axis=3, tiled=True)  16.8 us
    all_to_all x1, local copies, waits for them, and re-layouts, local(): lax.all_to_all(halfway, 'member', split_axis=3, concat_axis=1, tiled=True)  14.4 us
    all_to_all x1, starting transfers between devices, local(): lax.all_to_all(my_labels, 'space', split_axis=0, concat_axis=0, tiled=True)  13.4 us
  transfers between devices with their start and end apart: 5, of which 5 were waited for; matrix products, arithmetic and copies ran while one was open for 3% of the time, Pallas kernels for 0%

commit v1 on v0

v1 whole, which is shorter than its diff:
```python
import jax
import jax.numpy as jnp
from jax import lax
from jax.sharding import PartitionSpec as P


def _split3(x):
    hi = lax.reduce_precision(x, exponent_bits=8, mantissa_bits=7)
    r1 = x - hi
    mid = lax.reduce_precision(r1, exponent_bits=8, mantissa_bits=7)
    lo = r1 - mid
    return hi.astype(jnp.bfloat16), mid.astype(jnp.bfloat16), lo.astype(jnp.bfloat16)


def local(ensemble, inflation, weights, region_ids, extinction, obs_cols):
    n_space = lax.axis_size("space")
    n_member = lax.axis_size("member")
    local_members = ensemble.shape[0]
    tracers = ensemble.shape[1]
    columns = ensemble.shape[2]
    members = local_members * n_member
    reg_count = weights.shape[0]
    all_regions = inflation.shape[1]
    send_cols = columns // n_space
    slot_cols = send_cols // n_member
    own_cols = n_space * slot_cols
    row_len = local_members * tracers
    extra_len = 128
    owner = region_ids // reg_count
    owner_hot = (owner[:, None] == jnp.arange(n_space, dtype=jnp.int32)[None, :]).astype(jnp.int32)
    before = jnp.cumsum(owner_hot, axis=0) - owner_hot
    rank_in = jnp.sum(before * owner_hot, axis=1)
    position = owner * send_cols + rank_in
    ordering = (
        jnp.zeros((columns,), jnp.int32).at[position].set(jnp.arange(columns, dtype=jnp.int32))
    )
    region_hot = (jnp.arange(all_regions, dtype=jnp.int32)[:, None] == region_ids[None, :]).astype(
        jnp.float32
    )
    factor = jnp.dot(inflation, region_hot, precision=lax.Precision.HIGHEST)
    f_hi, f_mid, f_lo = _split3(factor.T)
    label = (region_ids % reg_count).astype(jnp.bfloat16)[:, None]
    pad = jnp.zeros((columns, extra_len - 3 * local_members - 1), jnp.bfloat16)
    extra = jnp.concatenate([f_hi, f_mid, f_lo, label, pad], axis=1)
    rows_major = jnp.transpose(ensemble, (2, 0, 1)).reshape(columns, row_len)
    rows = jnp.concatenate([rows_major, extra], axis=1)
    width = row_len + extra_len
    payload = jnp.take(rows, ordering, axis=0).reshape(n_space, n_member, slot_cols, width)
    received = lax.all_to_all(
        lax.all_to_all(payload, "member", split_axis=1, concat_axis=3, tiled=True),
        "space",
        split_axis=0,
        concat_axis=0,
        tiled=True,
    )
    gathered = received.reshape(own_cols, n_member, width)
    ens_part = gathered[:, :, :row_len].reshape(own_cols, members, tracers)
    ext = gathered[:, :, row_len:].astype(jnp.float32)
    lm = local_members
    fac = ((ext[:, :, 0:lm] + ext[:, :, lm:2 * lm]) + ext[:, :, 2 * lm:3 * lm]).reshape(
        own_cols, members
    )
    got_labels = ext[:, 0, 3 * lm].astype(jnp.int32)
    ens32 = ens_part.astype(jnp.float32)
    mean = jnp.sum(ens32, axis=1) / members
    anomaly = ((ens32 - mean[:, None, :]) * fac[:, :, None]).astype(jnp.bfloat16)
    accum = jnp.zeros((own_cols, members, tracers), jnp.float32)
    for region in range(reg_count):
        partial_prod = jnp.einsum(
            "jk,cjt->ckt", weights[region], anomaly, preferred_element_type=jnp.float32
        )
        accum = accum + jnp.where((got_labels == region)[:, None, None], partial_prod, 0.0)
    increment = accum.astype(jnp.bfloat16)
    result_rows = (mean[:, None, :] + increment.astype(jnp.float32)).astype(jnp.bfloat16)
    result_rows = result_rows.reshape(n_space, 1, slot_cols, members * tracers)
    halfway = lax.all_to_all(result_rows, "space", split_axis=0, concat_axis=0, tiled=True)
    returned = lax.all_to_all(halfway, "member", split_axis=3, concat_axis=1, tiled=True)
    restored = jnp.take(returned.reshape(columns, local_members * tracers), position, axis=0)
    analysis = jnp.transpose(restored.reshape(columns, local_members, tracers), (1, 2, 0))
    local_index = obs_cols - lax.axis_index("space") * columns
    picked = jnp.take(analysis, local_index, axis=2).astype(jnp.float32)
    obs_analysis = jnp.einsum("t,kto->ko", extinction, picked, precision=lax.Precision.HIGHEST)
    return (analysis, obs_analysis)


def solution(mesh):
    in_specs = (
        P("member", None, "space"),
        P("member", None),
        P("space", None, None),
        P("space"),
        P(),
        P("space"),
    )
    out_specs = (P("member", None, "space"), P("member", "space"))
    return jax.shard_map(local, mesh=mesh, in_specs=in_specs, out_specs=out_specs, check_vma=False)
```

time: 391 us -> 320 us (0.82)
  waiting for transfers between devices: 160 us -> 21 us
  blocking collectives: 44.1 us -> 126 us
  starting transfers between devices: 26 us -> 3.97 us
  local copies, waits for them, and re-layouts: 110 us -> 129 us
  between operations: 14.4 us -> 0.99 us
    all_to_all x0 -> x2, blocking collectives: none -> 82.4 us  [the longest x1 52.3 us: local(): lax.all_to_all(lax.all_to_all(payload, 'member', split_axis=1, concat_axi...]
    psum x1 -> x0, waiting for transfers between devices: 80.2 us -> none  [local(): summed = lax.psum(jnp.sum(ensemble, axis=0, dtype=jnp.float32), 'member')]
    all_to_all x3 -> x0, waiting for transfers between devices: 58.9 us -> none  [the longest x1 37.7 us: local(): lax.all_to_all(lax.all_to_all(payload, 'member', split_axis=1, concat_axi...]
    all_to_all x3 -> x0, starting transfers between devices: 21.4 us -> none  [the longest x1 13.4 us: local(): lax.all_to_all(my_labels, 'space', split_axis=0, concat_axis=0, tiled=True)]
    mul x0 -> x3, local copies, waits for them, and re-layouts: none -> 13.7 us  [local(): (ens32 - mean[:, None, :]) * fac[:, :, None]]
    add x1 -> x3, local copies, waits for them, and re-layouts: 3.16 us -> 13 us  [the longest x2 12.8 us: local(): mean[:, None, :] + increment.astype(jnp.float32)]
    unnamed x18 -> x25, local copies, waits for them, and re-layouts: 27.6 us -> 20.4 us
    gather x1 -> x3, local copies, waits for them, and re-layouts: 2.94 us -> 9.39 us  [local(): jnp.take(returned.reshape(columns, local_members * tracers), position, ax...]
  transfers between devices with their start and end apart: 5 -> 1, of which waited for: 5 -> 1; matrix products, arithmetic and copies ran while one was open for 3% -> 0% of each run, Pallas kernels for 0% -> 0%
where the time goes in v1:
time: 320 us; the launch traced here: 317 us
  local copies, waits for them, and re-layouts  129 us (40%)
  blocking collectives  126 us (39%)
  other arithmetic  23.7 us (7%)
  waiting for transfers between devices  21 us (7%)
  matrix products  11.8 us (4%)
  starting transfers between devices  3.97 us (1%)
    all_to_all x1, blocking collectives, local(): lax.all_to_all(lax.all_to_all(payload, 'member', split_axis=1, concat_axi...  52.3 us
    all_to_all x1, blocking collectives, local(): lax.all_to_all(result_rows, 'space', split_axis=0, concat_axis=0, tiled=T...  44 us
    all_to_all x1, blocking collectives, local(): lax.all_to_all(payload, 'member', split_axis=1, concat_axis=3, tiled=True)  30 us
    all_to_all x1, waiting for transfers between devices, local(): lax.all_to_all(halfway, 'member', split_axis=3, concat_axis=1, tiled=True)  21 us
    unnamed x25, local copies, waits for them, and re-layouts  20.4 us
    all_to_all x1, local copies, waits for them, and re-layouts, local(): lax.all_to_all(halfway, 'member', split_axis=3, concat_axis=1, tiled=True)  14.4 us
    mul x3, local copies, waits for them, and re-layouts, local(): (ens32 - mean[:, None, :]) * fac[:, :, None]  13.7 us
    add x2, local copies, waits for them, and re-layouts, local(): mean[:, None, :] + increment.astype(jnp.float32)  12.8 us
  transfers between devices with their start and end apart: 1, of which 1 were waited for; matrix products, arithmetic and copies ran while one was open for 0% of the time, Pallas kernels for 0%

profile of v1, /device:TPU:1, one launch (start us, length us, event | category | flops | bytes accessed | tf_op | source)
XLA Modules:
  0.0 317.2 jit_solution(428694375917716117)
XLA Ops:
  18.2 30.0 %all_to_all.43 = bf16[32,8,2,1664]{3,0,2,1:T(8,128)(2,1)S(1)} all-to-all(bf16[32,8,2,1664]{3,0,2,1:T(8,128)(2,1)S(1)} %copy_select_fusion), channel_id=1, replica_groups=mesh['member'=8,'space'=32] {'member'}, dimensions={1} | all-to-all | bytes 3407872 | tf_op jit(solution)/shard_map/all_to_all | solution.py:50
  49.6 52.3 %all_to_all.44 = bf16[32,1,2,13312]{3,2,1,0:T(2,128)(2,1)} all-to-all(bf16[32,1,2,13312]{3,2,1,0:T(2,128)(2,1)S(1)} %reshape.130), channel_id=1, replica_groups=mesh['member'=8,'space'=32] {'space'}, dimensions={0} | all-to-all | bytes 3407872 | tf_op jit(solution)/shard_map/all_to_all | solution.py:49
  101.9 4.2 %reshape.84 = bf16[64,8,1664]{2,1,0:T(8,128)(2,1)S(1)} reshape(bf16[32,1,2,13312]{3,2,1,0:T(2,128)(2,1)} %all_to_all.44) | data formatting | bytes 3407872 | tf_op jit(solution)/shard_map/reshape | solution.py:56
  106.2 4.7 %compare_reduce_fusion.3 = (pred[64]{0:T(512)(128)(4,1)S(1)}, pred[64]{0:T(512)(128)(4,1)S(1)}, pred[64]{0:T(512)(128)(4,1)S(1)}, pred[64]{0:T(512)(128)(4,1)S(1)}) fusion(f32[64,8,128]{2,1,0:T(8,128)S(1)} %slice_convert_fusion.1), kind=kLoop, calls=%fused_computation.34 | loop fusion | flops 320 | bytes 512 | tf_op jit(solution)/shard_map/eq | solution.py:72
  113.5 7.5 %reshape.87 = f32[64,256,48]{2,1,0:T(8,128)} reshape(f32[64,8,1536]{2,1,0:T(8,128)} %slice_convert_fusion) | data formatting | bytes 6291456 | tf_op jit(solution)/shard_map/convert_element_type | solution.py:64
  121.0 4.5 %reduce_sum.19 = f32[64,48]{1,0:T(8,128)S(1)} reduce(f32[64,256,48]{2,1,0:T(8,128)} %reshape.87, f32[]{:T(128)} %constant.89.clone.1), dimensions={1}, to_apply=%region_4.5 | reduce | flops 783360 | bytes 3158020 | tf_op jit(solution)/shard_map/reduce_sum | solution.py:65
  125.6 4.6 %mul.32 = f32[64,256,48]{2,1,0:T(8,128)} broadcast(f32[64,256]{1,0:T(8,128)S(1)} %copy.90), dimensions={0,1} | broadcast | bytes 3211264 | tf_op jit(solution)/shard_map/mul | solution.py:66
  130.1 9.0 %mul.33 = f32[64,8,1536]{2,1,0:T(8,128)} reshape(f32[64,256,48]{2,1,0:T(8,128)} %mul.32) | data formatting | bytes 6291456 | tf_op jit(solution)/shard_map/mul | solution.py:66
  139.2 3.8 %add.69 = f32[64,256,48]{2,1,0:T(8,128)} broadcast(f32[64,48]{1,0:T(8,128)S(1)} %broadcast_multiply_fusion), dimensions={0,2} | broadcast | bytes 3158016 | tf_op jit(solution)/shard_map/add | solution.py:74
  142.9 9.1 %add.70 = f32[64,8,1536]{2,1,0:T(8,128)} reshape(f32[64,256,48]{2,1,0:T(8,128)} %add.69) | data formatting | bytes 6291456 | tf_op jit(solution)/shard_map/add | solution.py:74
  152.0 3.6 %multiply_convert_fusion = bf16[64,8,1536]{2,1,0:T(8,128)(2,1)S(1)} fusion(f32[64,8,1536]{2,1,0:T(8,128)} %mul.33, f32[64,8,1536]{2,1,0:T(8,128)} %add.70, bf16[64,8,1664]{2,1,0:T(8,128)(2,1)S(1)} %reshape.84), kind=kLoop, calls=%fused_computation.7 | loop fusion | flops 3145728 | bytes 9437184 | tf_op jit(solution)/shard_map/convert_element_type | solution.py:66
  155.7 5.5 %convert_element_type.71 = bf16[64,256,48]{2,1,0:T(8,128)(2,1)} reshape(bf16[64,8,1536]{2,1,0:T(8,128)(2,1)S(1)} %multiply_convert_fusion) | data formatting | bytes 3145728 | tf_op jit(solution)/shard_map/convert_element_type | solution.py:66
  161.2 3.6 %fusion.5 = f32[64,48,256]{2,1,0:T(8,128)S(1)} fusion(bf16[64,256,48]{2,1,0:T(8,128)(2,1)} %convert_element_type.71, bf16[4,256,256]{2,1,0:T(8,128)(2,1)S(1)} %copy-done.3), kind=kOutput, calls=%fused_computation.20 | convolution fusion | flops 402653184 | bytes 4849664 | tf_op jit(solution)/shard_map/jk,cjt->ckt/dot_general | solution.py:69
  173.7 9.3 %reshape.85 = bf16[32,1,2,12288]{3,2,0,1:T(2,128)(2,1)S(1)} reshape(bf16[64,256,48]{2,1,0:T(8,128)(2,1)} %copy.95) | data formatting | bytes 3145728 | tf_op jit(solution)/shard_map/reshape | solution.py:75
  183.0 44.0 %all_to_all.45 = bf16[32,1,2,12288]{3,2,1,0:T(2,128)(2,1)S(1)} all-to-all(bf16[32,1,2,12288]{3,2,1,0:T(2,128)(2,1)S(1)} %bitcast.75), channel_id=1, replica_groups=mesh['member'=8,'space'=32] {'space'}, dimensions={0} | all-to-all | bytes 3145728 | tf_op jit(solution)/shard_map/all_to_all | solution.py:76
  227.0 11.1 %copy.97 = bf16[32,1,2,12288]{0,2,1,3:T(2,128)(2,1)} copy(bf16[32,1,2,12288]{3,2,1,0:T(2,128)(2,1)S(1)} %all_to_all.45) | data formatting | bytes 3145728 | tf_op jit(solution)/shard_map/all_to_all | solution.py:76
  238.0 9.5 %reshape.138 = bf16[8,2,49152]{2,1,0:T(2,128)(2,1)} reshape(bf16[12288,1,2,32]{3,2,1,0:T(2,128)(2,1)} %bitcast.72) | data formatting | bytes 3145728
  247.6 4.0 %all-to-all-start.3 = ((bf16[8,2,49152]{2,1,0:T(2,128)(2,1)}), bf16[8,2,49152]{2,1,0:T(2,128)(2,1)S(1)}, u32[]{:S(2)}, u32[]{:S(2)}) async-start(bf16[8,2,49152]{2,1,0:T(2,128)(2,1)} %reshape.138), calls=%async_computation.3 | async-start | bytes 3145728 | tf_op jit(solution)/shard_map/all_to_all | solution.py:77
  251.6 21.0 %all-to-all-done.3 = bf16[8,2,49152]{2,1,0:T(2,128)(2,1)S(1)} async-done(((bf16[8,2,49152]{2,1,0:T(2,128)(2,1)}), bf16[8,2,49152]{2,1,0:T(2,128)(2,1)S(1)}, u32[]{:S(2)}, u32[]{:S(2)}) %all-to-all-start.3) | async-done | bytes 1572896 | tf_op jit(solution)/shard_map/all_to_all | solution.py:77
  272.6 5.4 %reshape.139 = bf16[12288,1,2,32]{3,2,1,0:T(2,128)(2,1)} reshape(bf16[8,2,49152]{2,1,0:T(2,128)(2,1)S(1)} %all-to-all-done.3) | data formatting | bytes 3145728
  278.0 14.4 %copy.98 = bf16[32,1,2,8,1536]{4,2,3,0,1:T(2,128)(2,1)S(1)} copy(bf16[32,1,2,8,1536]{0,2,4,3,1:T(2,128)(2,1)} %bitcast.73) | data formatting | bytes 3145728 | tf_op jit(solution)/shard_map/all_to_all | solution.py:77
  296.0 6.5 %copy.100 = bf16[512,32,48]{2,1,0:T(8,128)(2,1)} copy(bf16[512,32,48]{0,2,1:T(8,128)(2,1)S(1)} %bitcast.76) | data formatting | bytes 3145728 | tf_op jit(solution)/shard_map/jit(_take)/gather | solution.py:78
  302.5 4.5 %select_bitcast_fusion = bf16[32,48,512]{1,0,2:T(8,128)(2,1)} fusion(bf16[512,32,48]{2,1,0:T(8,128)(2,1)} %copy.100, pred[512]{0:T(512)(128)(4,1)S(1)} %copy-done.8), kind=kLoop, calls=%fused_computation.4 | loop fusion | flops 786432 | bytes 3146240 | tf_op jit(solution)/shard_map/transpose | solution.py:79
  307.1 5.4 %copy.101 = bf16[32,48,512]{2,1,0:T(8,128)(2,1)} copy(bf16[32,48,512]{1,0,2:T(8,128)(2,1)} %select_bitcast_fusion) | data formatting | bytes 3145728
  (69 shorter events, 38.6 us)
Async XLA Ops:
  0.6 6.9 %copy-start = (f32[32,128]{1,0:T(8,128)S(1)}, f32[32,128]{1,0:T(8,128)}, u32[]{:S(2)}) copy-start(f32[32,128]{1,0:T(8,128)} %param.7) | copy-start | bytes 49156
  3.5 2.5 copy-start.6
  10.2 4.5 %copy-start.5 = (s32[1024]{0:T(1024)S(1)}, s32[1024]{0:T(1024)}, u32[]{:S(2)}) copy-start(s32[1024]{0:T(1024)} %pad_clamp_fusion.2) | copy-start | bytes 12292
  17.0 0.7 copy-start.4
  155.7 5.5 %copy-start.3 = (bf16[4,256,256]{2,1,0:T(8,128)(2,1)S(1)}, bf16[4,256,256]{2,1,0:T(8,128)(2,1)}, u32[]{:S(2)}) copy-start(bf16[4,256,256]{2,1,0:T(8,128)(2,1)} %param.8) | copy-start | bytes 1572868
  161.1 3.6 %copy-start.2 = (bf16[64,256,48]{2,1,0:T(8,128)(2,1)S(1)}, bf16[64,256,48]{2,1,0:T(8,128)(2,1)}, u32[]{:S(2)}) copy-start(bf16[64,256,48]{2,1,0:T(8,128)(2,1)} %convert_element_type.71) | copy-start | bytes 4718596
  247.5 4.0 %copy-start.7 = (s32[512]{0:T(512)S(1)}, s32[512]{0:T(512)}, u32[]{:S(2)}) copy-start(s32[512]{0:T(512)} %copy-done.6) | copy-start | bytes 6148
  247.5 4.0 %copy-start.10 = (s32[128]{0:T(128)S(1)}, s32[128]{0:T(128)}, u32[]{:S(2)}) copy-start(s32[128]{0:T(128)} %param.11) | copy-start | bytes 1540
  247.6 25.0 %all-to-all-start.3 = ((bf16[8,2,49152]{2,1,0:T(2,128)(2,1)}), bf16[8,2,49152]{2,1,0:T(2,128)(2,1)S(1)}, u32[]{:S(2)}, u32[]{:S(2)}) async-start(bf16[8,2,49152]{2,1,0:T(2,128)(2,1)} %reshape.138), calls=%async_computation.3 | async-start | bytes 3145728 | tf_op jit(solution)/shard_map/all_to_all | solution.py:77
  296.0 6.5 %copy-start.8 = (pred[512]{0:T(512)(128)(4,1)S(1)}, pred[512]{0:T(512)(128)(4,1)}, u32[]{:S(2)}) copy-start(pred[512]{0:T(512)(128)(4,1)} %get-tuple-element.16) | copy-start | bytes 1540
  307.1 8.5 %copy-start.9 = (f32[48]{0:T(128)S(1)}, f32[48]{0:T(128)}, u32[]{:S(2)}) copy-start(f32[48]{0:T(128)} %param.10) | copy-start | bytes 580
  307.1 10.1 %copy-start.1 = (f32[32,128]{1,0:T(8,128)S(1)}, f32[32,128]{1,0:T(8,128)}, u32[]{:S(2)}) copy-start(f32[32,128]{1,0:T(8,128)} %param.7) | copy-start | bytes 49156

commit v2 on v1

v2 whole, which is shorter than its diff:
```python
import jax
import jax.numpy as jnp
from jax import lax
from jax.sharding import PartitionSpec as P


def _split3(x):
    hi = lax.reduce_precision(x, exponent_bits=8, mantissa_bits=7)
    r1 = x - hi
    mid = lax.reduce_precision(r1, exponent_bits=8, mantissa_bits=7)
    lo = r1 - mid
    return hi.astype(jnp.bfloat16), mid.astype(jnp.bfloat16), lo.astype(jnp.bfloat16)


def local(ensemble, inflation, weights, region_ids, extinction, obs_cols):
    n_space = lax.axis_size("space")
    n_member = lax.axis_size("member")
    local_members = ensemble.shape[0]
    tracers = ensemble.shape[1]
    columns = ensemble.shape[2]
    members = local_members * n_member
    reg_count = weights.shape[0]
    all_regions = inflation.shape[1]
    groups_per_dev = n_space // n_member
    send_cols = columns // n_space
    own_cols = columns // n_member
    row_len = local_members * tracers
    extra_len = 128
    me_space = lax.axis_index("space")
    me_member = lax.axis_index("member")

    fetched = []
    for q in range(groups_per_dev):
        perm = []
        for m in range(n_member):
            for s in range(n_space):
                src = (s + groups_per_dev * m + q) % n_space
                perm.append((m * n_space + src, m * n_space + s))
        fetched.append(lax.ppermute(weights, ("member", "space"), perm))
    w_all = jnp.stack(fetched)

    owner = region_ids // reg_count
    shift = (owner - me_space) % n_space
    owner_hot = (owner[:, None] == jnp.arange(n_space, dtype=jnp.int32)[None, :]).astype(jnp.int32)
    before = jnp.cumsum(owner_hot, axis=0) - owner_hot
    rank_in = jnp.sum(before * owner_hot, axis=1)
    position = shift * send_cols + rank_in
    ordering = (
        jnp.zeros((columns,), jnp.int32).at[position].set(jnp.arange(columns, dtype=jnp.int32))
    )
    labels_sorted = jnp.take(region_ids % reg_count, ordering).reshape(n_member, own_cols)
    my_labels = lax.dynamic_index_in_dim(labels_sorted, me_member, 0, keepdims=False)

    region_hot = (jnp.arange(all_regions, dtype=jnp.int32)[:, None] == region_ids[None, :]).astype(
        jnp.float32
    )
    factor = jnp.dot(inflation, region_hot, precision=lax.Precision.HIGHEST)
    f_hi, f_mid, f_lo = _split3(factor.T)
    pad = jnp.zeros((columns, extra_len - 3 * local_members), jnp.bfloat16)
    extra = jnp.concatenate([f_hi, f_mid, f_lo, pad], axis=1)
    rows_major = jnp.transpose(ensemble, (2, 0, 1)).reshape(columns, row_len)
    rows = jnp.concatenate([rows_major, extra], axis=1)
    width = row_len + extra_len
    payload = jnp.take(rows, ordering, axis=0).reshape(n_member, own_cols, width)
    received = lax.all_to_all(payload, "member", split_axis=0, concat_axis=0, tiled=True)
    gathered = jnp.transpose(received, (1, 0, 2))
    ens_part = gathered[:, :, :row_len].reshape(own_cols, members, tracers)
    ext = gathered[:, :, row_len:].astype(jnp.float32)
    lm = local_members
    fac = ((ext[:, :, 0:lm] + ext[:, :, lm:2 * lm]) + ext[:, :, 2 * lm:3 * lm]).reshape(
        own_cols, members
    )
    ens32 = ens_part.astype(jnp.float32)
    mean = jnp.sum(ens32, axis=1) / members
    anomaly = ((ens32 - mean[:, None, :]) * fac[:, :, None]).astype(jnp.bfloat16)
    anomaly = anomaly.reshape(groups_per_dev, send_cols, members, tracers)
    labels_g = my_labels.reshape(groups_per_dev, send_cols)
    accum = jnp.zeros((groups_per_dev, send_cols, members, tracers), jnp.float32)
    for region in range(reg_count):
        partial_prod = jnp.einsum(
            "qjk,qcjt->qckt", w_all[:, region], anomaly, preferred_element_type=jnp.float32
        )
        accum = accum + jnp.where((labels_g == region)[:, :, None, None], partial_prod, 0.0)
    increment = lax.reduce_precision(accum, exponent_bits=8, mantissa_bits=7)
    increment = increment.reshape(own_cols, members, tracers)
    result = (mean[:, None, :] + increment).astype(jnp.bfloat16)
    result = jnp.transpose(result.reshape(own_cols, n_member, row_len), (1, 0, 2))
    returned = lax.all_to_all(result, "member", split_axis=0, concat_axis=0, tiled=True)
    restored = jnp.take(returned.reshape(columns, row_len), position, axis=0)
    analysis = jnp.transpose(restored.reshape(columns, local_members, tracers), (1, 2, 0))
    local_index = obs_cols - me_space * columns
    picked = jnp.take(analysis, local_index, axis=2).astype(jnp.float32)
    obs_analysis = jnp.einsum("t,kto->ko", extinction, picked, precision=lax.Precision.HIGHEST)
    return (analysis, obs_analysis)


def solution(mesh):
    in_specs = (
        P("member", None, "space"),
        P("member", None),
        P("space", None, None),
        P("space"),
        P(),
        P("space"),
    )
    out_specs = (P("member", None, "space"), P("member", "space"))
    return jax.shard_map(local, mesh=mesh, in_specs=in_specs, out_specs=out_specs, check_vma=False)
```

time: 320 us -> 261 us (0.82)
  blocking collectives: 126 us -> 0 us
  starting transfers between devices: 3.97 us -> 103 us
  local copies, waits for them, and re-layouts: 129 us -> 80.1 us
  waiting for transfers between devices: 21 us -> 49.5 us
  matrix products: 11.8 us -> 5.63 us
  other arithmetic: 23.7 us -> 19.8 us
    all_to_all x3 -> x0, blocking collectives: 126 us -> none  [the longest x1 52.3 us: local(): lax.all_to_all(lax.all_to_all(payload, 'member', split_axis=1, concat_axi...]
    all_to_all x1 -> x2, starting transfers between devices: 3.97 us -> 93.8 us  [the longest x1 86.3 us: local(): lax.all_to_all(result, 'member', split_axis=0, concat_axis=0, tiled=True)]
    ppermute x0 -> x4, waiting for transfers between devices: none -> 28.4 us  [local(): fetched.append(lax.ppermute(weights, ('member', 'space'), perm))]
    all_to_all x4 -> x0, local copies, waits for them, and re-layouts: 26.9 us -> none  [the longest x1 14.4 us: local(): lax.all_to_all(halfway, 'member', split_axis=3, concat_axis=1, tiled=True)]
    mul x3 -> x1, local copies, waits for them, and re-layouts: 13.7 us -> 0.13 us  [local(): (ens32 - mean[:, None, :]) * fac[:, :, None]]
    unnamed x25 -> x13, local copies, waits for them, and re-layouts: 20.4 us -> 7.67 us
    convert_element_type x1 -> x4, local copies, waits for them, and re-layouts: 7.51 us -> 17.8 us  [local(): ens32 = ens_part.astype(jnp.float32)]
    ppermute x0 -> x4, starting transfers between devices: none -> 8.98 us  [local(): fetched.append(lax.ppermute(weights, ('member', 'space'), perm))]
  transfers between devices with their start and end apart: 1 -> 6, of which waited for: 1 -> 4; matrix products, arithmetic and copies ran while one was open for 0% -> 3% of each run, Pallas kernels for 0% -> 0%
where the time goes in v2:
time: 261 us; the launch traced here: 259 us
  starting transfers between devices  103 us (39%)
  local copies, waits for them, and re-layouts  80.1 us (31%)
  waiting for transfers between devices  49.5 us (19%)
  other arithmetic  19.8 us (8%)
  matrix products  5.63 us (2%)
    all_to_all x1, starting transfers between devices, local(): lax.all_to_all(result, 'member', split_axis=0, concat_axis=0, tiled=True)  86.3 us
    ppermute x4, waiting for transfers between devices, local(): fetched.append(lax.ppermute(weights, ('member', 'space'), perm))  28.4 us
    all_to_all x1, waiting for transfers between devices, local(): lax.all_to_all(result, 'member', split_axis=0, concat_axis=0, tiled=True)  21.1 us
    convert_element_type x4, local copies, waits for them, and re-layouts, local(): ens32 = ens_part.astype(jnp.float32)  17.8 us
    add x2, local copies, waits for them, and re-layouts, local(): result = (mean[:, None, :] + increment).astype(jnp.bfloat16)  12.8 us
    gather x3, local copies, waits for them, and re-layouts, local(): restored = jnp.take(returned.reshape(columns, row_len), position, axis=0)  9.38 us
    ppermute x4, starting transfers between devices, local(): fetched.append(lax.ppermute(weights, ('member', 'space'), perm))  8.98 us
    reshape x1, local copies, waits for them, and re-layouts, local(): increment = increment.reshape(own_cols, members, tracers)  7.94 us
  transfers between devices with their start and end apart: 6, of which 4 were waited for; matrix products, arithmetic and copies ran while one was open for 3% of the time, Pallas kernels for 0%

profile of v2, /device:TPU:1, one launch (start us, length us, event | category | flops | bytes accessed | tf_op | source)
XLA Modules:
  0.0 258.8 jit_solution(11149922819634101963)
XLA Ops:
  2.9 2.4 scatter_custom_fusion
  12.5 2.3 gather_fusion
  16.3 7.5 %all-to-all-start = ((bf16[8,64,1664]{2,1,0:T(8,128)(2,1)}), bf16[8,64,1664]{2,1,0:T(8,128)(2,1)S(1)}, u32[]{:S(2)}, u32[]{:S(2)}) async-start(bf16[8,64,1664]{2,1,0:T(8,128)(2,1)} %broadcast_select_fusion), calls=%async_computation | async-start | bytes 3407872 | tf_op jit(solution)/shard_map/all_to_all | solution.py:65
  23.7 6.5 %collective-permute-start.3 = (bf16[4,256,256]{2,1,0:T(8,128)(2,1)}, bf16[4,256,256]{2,1,0:T(8,128)(2,1)S(1)}, u32[]{:S(2)}, u32[]{:S(2)}) collective-permute-start(bf16[4,256,256]{2,1,0:T(8,128)(2,1)} %param.8), channel_id=1, source_target_pairs={{3,0},{4,1},{5,2},{6,3},{7,4},{8,5},{9,6},{10,7},{11,8},{12,9},{13... | collective-permute-start | bytes 1572872 | tf_op jit(solution)/shard_map/ppermute | solution.py:39
  32.7 3.5 %gather_fusion.1 = s32[512]{0:T(512)S(1)} fusion(s32[512]{0:T(512)S(1)} %get-tuple-element.19, s32[1024]{0:T(1024)S(1)} %pad_clamp_fusion.2), kind=kCustom, calls=%fused_computation.1 | custom fusion | bytes 6144 | tf_op jit(solution)/shard_map/jit(_take)/gather | solution.py:51
  36.7 17.2 %collective-permute-done.3 = bf16[4,256,256]{2,1,0:T(8,128)(2,1)S(1)} collective-permute-done((bf16[4,256,256]{2,1,0:T(8,128)(2,1)}, bf16[4,256,256]{2,1,0:T(8,128)(2,1)S(1)}, u32[]{:S(2)}, u32[]{:S(2)}) %collective-permute-start.3) | collective-permute-done | bytes 524320 | tf_op jit(solution)/shard_map/ppermute | solution.py:39
  55.3 9.8 %collective-permute-done.2 = bf16[4,256,256]{2,1,0:T(8,128)(2,1)} collective-permute-done((bf16[4,256,256]{2,1,0:T(8,128)(2,1)}, bf16[4,256,256]{2,1,0:T(8,128)(2,1)}, u32[]{:S(2)}, u32[]{:S(2)}) %collective-permute-start.2) | collective-permute-done | bytes 524320 | tf_op jit(solution)/shard_map/ppermute | solution.py:39
  65.1 2.6 %pad_maximum_fusion = bf16[4,4,256,256]{3,2,0,1:T(8,128)(2,1)} fusion(bf16[1,4,256,256]{3,2,0,1:T(8,128)(2,1)S(1)} %bitcast.82, bf16[1,4,256,256]{3,2,0,1:T(8,128)(2,1)} %bitcast.9, bf16[1,4,256,256]{3,2,0,1:T(8,128)(2,1)S(1)} %bitcast.84, bf16[1,4,256,256]{3,2,0,1:T(8,128)(2,1)S(1)} %bitcast.83), kind=kLoop, calls=%fused_computation.9 | loop fusion | flops 3145728 | bytes 4194304 | tf_op jit(solution)/shard_map/stack | solution.py:40
  71.1 5.4 %reshape.118 = f32[64,256,48]{2,1,0:T(8,128)} reshape(f32[64,8,1536]{2,1,0:T(8,128)S(1)} %copy.51) | data formatting | bytes 6291456 | tf_op jit(solution)/shard_map/convert_element_type | solution.py:73
  76.5 5.4 %reshape.119 = f32[4,16,256,48]{3,2,1,0:T(8,128)} reshape(f32[64,8,1536]{2,1,0:T(8,128)S(1)} %copy.51) | data formatting | bytes 6291456 | tf_op jit(solution)/shard_map/convert_element_type | solution.py:73
  82.9 4.5 %reduce_sum.19 = f32[64,48]{1,0:T(8,128)S(1)} reduce(f32[64,256,48]{2,1,0:T(8,128)} %reshape.118, f32[]{:T(128)} %constant.119.clone.1), dimensions={1}, to_apply=%region_4.5 | reduce | flops 783360 | bytes 3158020 | tf_op jit(solution)/shard_map/reduce_sum | solution.py:74
  87.4 5.1 %copy.53 = f32[4,16,256,48]{2,3,1,0:T(8,128)S(1)} copy(f32[4,16,256,48]{3,2,1,0:T(8,128)} %reshape.119) | data formatting | bytes 6291456 | tf_op jit(solution)/shard_map/convert_element_type | solution.py:73
  97.8 4.7 %copy.55 = f32[4,16,256,48]{3,2,1,0:T(8,128)} copy(f32[4,16,256,48]{2,3,1,0:T(8,128)S(1)} %reduce-precision_bitcast_fusion) | data formatting | bytes 6291456 | tf_op jit(solution)/shard_map/reduce_precision | solution.py:84
  102.5 7.9 %reshape.116 = f32[64,8,1536]{2,1,0:T(8,128)S(1)} reshape(f32[4,16,256,48]{3,2,1,0:T(8,128)} %copy.55) | data formatting | bytes 6291456 | tf_op jit(solution)/shard_map/reshape | solution.py:85
  110.5 3.8 %add.84 = f32[64,256,48]{2,1,0:T(8,128)} broadcast(f32[64,48]{1,0:T(8,128)S(1)} %broadcast_multiply_fusion), dimensions={0,2} | broadcast | bytes 3158016 | tf_op jit(solution)/shard_map/add | solution.py:86
  114.2 9.0 %add.85 = f32[64,8,1536]{2,1,0:T(8,128)} reshape(f32[64,256,48]{2,1,0:T(8,128)} %add.84) | data formatting | bytes 6291456 | tf_op jit(solution)/shard_map/add | solution.py:86
  123.3 2.3 fusion
  127.2 86.3 %all-to-all-start.1 = ((bf16[8,64,1536]{2,1,0:T(8,128)(2,1)}), bf16[8,64,1536]{2,1,0:T(8,128)(2,1)S(1)}, u32[]{:S(2)}, u32[]{:S(2)}) async-start(bf16[8,64,1536]{2,1,0:T(8,128)(2,1)} %copy.56), calls=%async_computation.1 | async-start | bytes 3145728 | tf_op jit(solution)/shard_map/all_to_all | solution.py:88
  213.6 21.1 %all-to-all-done.1 = bf16[8,64,1536]{2,1,0:T(8,128)(2,1)S(1)} async-done(((bf16[8,64,1536]{2,1,0:T(8,128)(2,1)}), bf16[8,64,1536]{2,1,0:T(8,128)(2,1)S(1)}, u32[]{:S(2)}, u32[]{:S(2)}) %all-to-all-start.1) | async-done | bytes 1572896 | tf_op jit(solution)/shard_map/all_to_all | solution.py:88
  234.7 2.1 gather_fusion.2
  237.6 6.5 %copy.58 = bf16[512,32,48]{2,1,0:T(8,128)(2,1)} copy(bf16[512,32,48]{0,2,1:T(8,128)(2,1)S(1)} %bitcast.80) | data formatting | bytes 3145728 | tf_op jit(solution)/shard_map/jit(_take)/gather | solution.py:89
  244.1 4.5 %select_bitcast_fusion = bf16[32,48,512]{1,0,2:T(8,128)(2,1)} fusion(bf16[512,32,48]{2,1,0:T(8,128)(2,1)} %copy.58, pred[512]{0:T(512)(128)(4,1)S(1)} %get-tuple-element.14), kind=kLoop, calls=%fused_computation.5 | loop fusion | flops 786432 | bytes 3146240 | tf_op jit(solution)/shard_map/transpose | solution.py:90
  248.6 5.3 %copy.59 = bf16[32,48,512]{2,1,0:T(8,128)(2,1)} copy(bf16[32,48,512]{1,0,2:T(8,128)(2,1)} %select_bitcast_fusion) | data formatting | bytes 3145728
  254.0 3.0 %gather_fusion.3 = bf16[128,32,48]{2,1,0:T(8,128)(2,1)S(1)} fusion(bf16[32,48,512]{1,0,2:T(8,128)(2,1)} %select_bitcast_fusion, s32[1024]{0:T(1024)S(1)} %pad_clamp_fusion), kind=kCustom, calls=%fused_computation.3 | custom fusion | bytes 786944 | tf_op jit(solution)/shard_map/jit(_take)/gather | solution.py:92
  (65 shorter events, 28.8 us)
Async XLA Ops:
  0.6 4.8 %copy-start = (f32[32,128]{1,0:T(8,128)S(1)}, f32[32,128]{1,0:T(8,128)}, u32[]{:S(2)}) copy-start(f32[32,128]{1,0:T(8,128)} %param.7) | copy-start | bytes 49156
  16.3 51.4 %all-to-all-start = ((bf16[8,64,1664]{2,1,0:T(8,128)(2,1)}), bf16[8,64,1664]{2,1,0:T(8,128)(2,1)S(1)}, u32[]{:S(2)}, u32[]{:S(2)}) async-start(bf16[8,64,1664]{2,1,0:T(8,128)(2,1)} %broadcast_select_fusion), calls=%async_computation | async-start | bytes 3407872 | tf_op jit(solution)/shard_map/all_to_all | solution.py:65
  23.7 30.1 %collective-permute-start.3 = (bf16[4,256,256]{2,1,0:T(8,128)(2,1)}, bf16[4,256,256]{2,1,0:T(8,128)(2,1)S(1)}, u32[]{:S(2)}, u32[]{:S(2)}) collective-permute-start(bf16[4,256,256]{2,1,0:T(8,128)(2,1)} %param.8), channel_id=1, source_target_pairs={{3,0},{4,1},{5,2},{6,3},{7,4},{8,5},{9,6},{10,7},{11,8},{12,9},{13... | collective-permute-start | bytes 1572872 | tf_op jit(solution)/shard_map/ppermute | solution.py:39
  30.3 23.6 %collective-permute-start = (bf16[4,256,256]{2,1,0:T(8,128)(2,1)}, bf16[4,256,256]{2,1,0:T(8,128)(2,1)S(1)}, u32[]{:S(2)}, u32[]{:S(2)}) collective-permute-start(bf16[4,256,256]{2,1,0:T(8,128)(2,1)} %param.8), channel_id=1, source_target_pairs={{0,0},{1,1},{2,2},{3,3},{4,4},{5,5},{6,6},{7,7},{8,8},{9,9},{10,10... | collective-permute-start | bytes 1572872 | tf_op jit(solution)/shard_map/ppermute | solution.py:39
  32.0 23.3 %collective-permute-start.1 = (bf16[4,256,256]{2,1,0:T(8,128)(2,1)}, bf16[4,256,256]{2,1,0:T(8,128)(2,1)S(1)}, u32[]{:S(2)}, u32[]{:S(2)}) collective-permute-start(bf16[4,256,256]{2,1,0:T(8,128)(2,1)} %param.8), channel_id=1, source_target_pairs={{1,0},{2,1},{3,2},{4,3},{5,4},{6,5},{7,6},{8,7},{9,8},{10,9},{11,1... | collective-permute-start | bytes 1572872 | tf_op jit(solution)/shard_map/ppermute | solution.py:39
  32.0 33.1 %collective-permute-start.2 = (bf16[4,256,256]{2,1,0:T(8,128)(2,1)}, bf16[4,256,256]{2,1,0:T(8,128)(2,1)}, u32[]{:S(2)}, u32[]{:S(2)}) collective-permute-start(bf16[4,256,256]{2,1,0:T(8,128)(2,1)} %param.8), channel_id=1, source_target_pairs={{2,0},{3,1},{4,2},{5,3},{6,4},{7,5},{8,6},{9,7},{10,8},{11,9},{12,... | collective-permute-start | bytes 1572872 | tf_op jit(solution)/shard_map/ppermute | solution.py:39
  67.7 1.2 copy-start.3
  93.1 1.6 copy-start.2
  127.2 86.3 %copy-start.5 = (s32[128]{0:T(128)S(1)}, s32[128]{0:T(128)}, u32[]{:S(2)}) copy-start(s32[128]{0:T(128)} %param.11) | copy-start | bytes 1540
  127.2 107.5 %all-to-all-start.1 = ((bf16[8,64,1536]{2,1,0:T(8,128)(2,1)}), bf16[8,64,1536]{2,1,0:T(8,128)(2,1)S(1)}, u32[]{:S(2)}, u32[]{:S(2)}) async-start(bf16[8,64,1536]{2,1,0:T(8,128)(2,1)} %copy.56), calls=%async_computation.1 | async-start | bytes 3145728 | tf_op jit(solution)/shard_map/all_to_all | solution.py:88
  248.6 10.1 %copy-start.1 = (f32[32,128]{1,0:T(8,128)S(1)}, f32[32,128]{1,0:T(8,128)}, u32[]{:S(2)}) copy-start(f32[32,128]{1,0:T(8,128)} %param.7) | copy-start | bytes 49156
  254.0 3.2 %copy-start.4 = (f32[48]{0:T(128)S(1)}, f32[48]{0:T(128)}, u32[]{:S(2)}) copy-start(f32[48]{0:T(128)} %param.10) | copy-start | bytes 580

commit v3 on v2

v3 whole, which is shorter than its diff:
```python
import jax
import jax.numpy as jnp
from jax import lax
from jax.sharding import PartitionSpec as P


def local(ensemble, inflation, weights, region_ids, extinction, obs_cols):
    n_space = lax.axis_size("space")
    n_member = lax.axis_size("member")
    local_members, tracers, columns = ensemble.shape
    members = local_members * n_member
    reg_count = weights.shape[0]
    all_regions = inflation.shape[1]
    groups_per_dev = n_space // n_member
    send_cols = columns // n_space
    own_cols = columns // n_member
    n_chip = n_space // 2
    chips_per_dev = groups_per_dev // 2
    n_slot = groups_per_dev * reg_count
    me_space = lax.axis_index("space")
    me_member = lax.axis_index("member")
    chip = me_space // 2
    core = me_space % 2

    own = []
    for a in range(chips_per_dev):
        perm = []
        for m in range(n_member):
            for s in range(n_space):
                src = 2 * ((s // 2 + chips_per_dev * m + a) % n_chip) + s % 2
                perm.append((m * n_space + src, m * n_space + s))
        own.append(lax.ppermute(weights, ("member", "space"), perm))
    own = jnp.stack(own)
    sib_perm = [(m * n_space + s, m * n_space + (s ^ 1)) for m in range(n_member) for s in range(n_space)]
    sib = lax.ppermute(own, ("member", "space"), sib_perm)
    w_all = jnp.concatenate([own, sib], axis=0).reshape(n_slot, members, members)

    group = region_ids // reg_count
    offset = (group // 2 - chip) % n_chip
    dest = offset // chips_per_dev
    slot = (group % 2 != core).astype(jnp.int32) * chips_per_dev + offset % chips_per_dev
    group_hot = (group[:, None] == jnp.arange(n_space, dtype=jnp.int32)[None, :]).astype(jnp.int32)
    before = jnp.cumsum(group_hot, axis=0) - group_hot
    rank_in = jnp.sum(before * group_hot, axis=1)
    position = dest * own_cols + slot * send_cols + rank_in
    label = slot * reg_count + region_ids % reg_count
    pos_iota = jnp.arange(columns, dtype=jnp.int32)
    perm_hot = position[:, None] == pos_iota[None, :]
    perm_mat = perm_hot.astype(jnp.bfloat16).reshape(columns, n_member, own_cols)
    label_sorted = jnp.sum(jnp.where(perm_hot, label[:, None], 0), axis=0).reshape(n_member, own_cols)
    my_labels = lax.dynamic_index_in_dim(label_sorted, me_member, 0, keepdims=False)

    region_hot = (jnp.arange(all_regions, dtype=jnp.int32)[:, None] == region_ids[None, :]).astype(
        jnp.float32
    )
    factor = jnp.dot(inflation, region_hot, precision=lax.Precision.HIGHEST)
    fac_perm = jnp.einsum(
        "jc,cdi->dji", factor, perm_mat.astype(jnp.float32), precision=lax.Precision.HIGHEST
    )
    payload = jnp.einsum("jtc,cdi->djti", ensemble, perm_mat, preferred_element_type=jnp.bfloat16)

    received = lax.all_to_all(payload, "member", split_axis=0, concat_axis=0, tiled=True)
    fac_got = lax.all_to_all(fac_perm, "member", split_axis=0, concat_axis=0, tiled=True)
    ens32 = received.reshape(members, tracers, own_cols).astype(jnp.float32)
    fac = fac_got.reshape(members, own_cols)
    mean = jnp.sum(ens32, axis=0) / members
    anomaly = ((ens32 - mean[None]) * fac[:, None, :]).astype(jnp.bfloat16)
    mask = my_labels[None, :] == jnp.arange(n_slot, dtype=jnp.int32)[:, None]
    masked = jnp.where(mask[:, None, None, :], anomaly[None], jnp.zeros((), jnp.bfloat16))
    inc = jnp.einsum("rjk,rjtc->ktc", w_all, masked, preferred_element_type=jnp.float32)
    inc = lax.reduce_precision(inc, exponent_bits=8, mantissa_bits=7)
    result = (mean[None] + inc).astype(jnp.bfloat16)
    result = result.reshape(n_member, local_members, tracers, own_cols)
    returned = lax.all_to_all(result, "member", split_axis=0, concat_axis=0, tiled=True)
    analysis = jnp.einsum("dkti,cdi->ktc", returned, perm_mat, preferred_element_type=jnp.bfloat16)

    local_index = obs_cols - me_space * columns
    obs_pos = jnp.take(position, local_index)
    obs_mat = (pos_iota[:, None] == obs_pos[None, :]).astype(jnp.bfloat16)
    obs_mat = obs_mat.reshape(n_member, own_cols, obs_cols.shape[0])
    picked = jnp.einsum("dkti,dio->kto", returned, obs_mat, preferred_element_type=jnp.float32)
    obs_analysis = jnp.einsum("t,kto->ko", extinction, picked, precision=lax.Precision.HIGHEST)
    return (analysis, obs_analysis)


def solution(mesh):
    in_specs = (
        P("member", None, "space"),
        P("member", None),
        P("space", None, None),
        P("space"),
        P(),
        P("space"),
    )
    out_specs = (P("member", None, "space"), P("member", "space"))
    return jax.shard_map(local, mesh=mesh, in_specs=in_specs, out_specs=out_specs, check_vma=False)
```

time: 261 us -> 179 us (0.69)
  local copies, waits for them, and re-layouts: 80.1 us -> 36 us
  starting transfers between devices: 103 us -> 71.3 us
  matrix products: 5.63 us -> 18.6 us
  waiting for transfers between devices: 49.5 us -> 37.7 us
  other arithmetic: 19.8 us -> 11.8 us
    all_to_all x1, starting transfers between devices: 86.3 us -> 42.9 us  [local(): lax.all_to_all(result, 'member', split_axis=0, concat_axis=0, tiled=True)]
    gather x7 -> x1, local copies, waits for them, and re-layouts: 18.2 us -> 1.27 us  [local(): obs_pos = jnp.take(position, local_index)]
    unnamed x13 -> x18, local copies, waits for them, and re-layouts: 7.67 us -> 23.8 us
    ppermute x4 -> x3, waiting for transfers between devices: 28.4 us -> 14.9 us  [the longest x2 14.9 us: local(): own.append(lax.ppermute(weights, ('member', 'space'), perm))]
    dot_general x4 -> x5, matrix products: 3.14 us -> 16.5 us  [the longest x1 7.15 us: local(): jnp.einsum('rjk,rjtc->ktc', w_all, masked, preferred_element_type=jnp.flo...]
    add x3 -> x0, local copies, waits for them, and re-layouts: 13 us -> none  [the longest x2 12.8 us: local(): result = (mean[:, None, :] + increment).astype(jnp.bfloat16)]
    reshape x2 -> x1, local copies, waits for them, and re-layouts: 9.65 us -> 0.08 us  [local(): jnp.sum(jnp.where(perm_hot, label[:, None], 0), axis=0)]
    convert_element_type x7 -> x2, local copies, waits for them, and re-layouts: 19.4 us -> 10 us  [the longest x1 6.02 us: local(): ens32 = received.reshape(members, tracers, own_cols).astype(jnp.float32)]
  transfers between devices with their start and end apart: 6 -> 6, of which waited for: 4 -> 2; matrix products, arithmetic and copies ran while one was open for 3% -> 17% of each run, Pallas kernels for 0% -> 0%
where the time goes in v3:
time: 179 us; the launch traced here: 176 us
  starting transfers between devices  71.3 us (40%)
  waiting for transfers between devices  37.7 us (21%)
  local copies, waits for them, and re-layouts  36 us (20%)
  matrix products  18.6 us (10%)
  other arithmetic  11.8 us (7%)
    all_to_all x1, starting transfers between devices, local(): lax.all_to_all(result, 'member', split_axis=0, concat_axis=0, tiled=True)  42.9 us
    unnamed x18, local copies, waits for them, and re-layouts  23.8 us
    all_to_all x1, waiting for transfers between devices, local(): lax.all_to_all(result, 'member', split_axis=0, concat_axis=0, tiled=True)  22.8 us
    ppermute x2, waiting for transfers between devices, local(): own.append(lax.ppermute(weights, ('member', 'space'), perm))  14.9 us
    ppermute x2, starting transfers between devices, local(): own.append(lax.ppermute(weights, ('member', 'space'), perm))  11 us
    all_to_all x1, starting transfers between devices, local(): lax.all_to_all(fac_perm, 'member', split_axis=0, concat_axis=0, tiled=True)  7.48 us
    dot_general x1, matrix products, local(): jnp.einsum('rjk,rjtc->ktc', w_all, masked, preferred_element_type=jnp.flo...  7.15 us
    all_to_all x1, starting transfers between devices, local(): lax.all_to_all(payload, 'member', split_axis=0, concat_axis=0, tiled=True)  6.62 us
  transfers between devices with their start and end apart: 6, of which 2 were waited for; matrix products, arithmetic and copies ran while one was open for 17% of the time, Pallas kernels for 0%

profile of v3, /device:TPU:1, one launch (start us, length us, event | category | flops | bytes accessed | tf_op | source)
XLA Modules:
  0.0 176.3 jit_solution(27787132124434593)
XLA Ops:
  2.2 1.2 reduce-window.6
  3.6 0.9 convolution_bitcast_fusion.3
  7.0 7.5 %all-to-all-start.1 = ((f32[8,1,2048]{2,1,0:T(1,128)}), f32[8,1,2048]{2,1,0:T(1,128)S(1)}, u32[]{:S(2)}, u32[]{:S(2)}) async-start(f32[8,1,2048]{2,1,0:T(1,128)} %reshape.131), calls=%async_computation.1 | async-start | bytes 131072 | tf_op jit(solution)/shard_map/all_to_all | solution.py:63
  14.5 3.4 %convolution_bitcast_fusion = bf16[8,32,48,64]{3,2,1,0:T(8,128)(2,1)} fusion(bf16[32,48,512]{2,1,0:T(8,128)(2,1)S(1)} %copy-done, s32[8,64]{1,0:T(8,128)S(1)} %multiply_add_fusion, s32[512]{0:T(512)S(1)} %get-tuple-element.2), kind=kOutput, calls=%fused_computation.11 | convolution fusion | flops 805568512 | bytes 3149824 | tf_op jit(solution)/shard_map/jtc,cdi->djti/dot_general | solution.py:60
  17.9 6.9 %reshape.129 = bf16[8,2,49152]{2,1,0:T(2,128)(2,1)} reshape(bf16[8,32,48,64]{3,2,1,0:T(8,128)(2,1)} %convolution_bitcast_fusion) | data formatting | bytes 3145728
  24.8 6.6 %all-to-all-start = ((bf16[8,2,49152]{2,1,0:T(2,128)(2,1)}), bf16[8,2,49152]{2,1,0:T(2,128)(2,1)S(1)}, u32[]{:S(2)}, u32[]{:S(2)}) async-start(bf16[8,2,49152]{2,1,0:T(2,128)(2,1)} %reshape.129), calls=%async_computation | async-start | bytes 3145728 | tf_op jit(solution)/shard_map/all_to_all | solution.py:62
  31.4 5.3 %collective-permute-start = (bf16[4,256,256]{2,1,0:T(8,128)(2,1)}, bf16[4,256,256]{2,1,0:T(8,128)(2,1)}, u32[]{:S(2)}, u32[]{:S(2)}) collective-permute-start(bf16[4,256,256]{2,1,0:T(8,128)(2,1)} %param.8), channel_id=1, source_target_pairs={{0,0},{1,1},{2,2},{3,3},{4,4},{5,5},{6,6},{7,7},{8,8},{9,9},{10,10... | collective-permute-start | bytes 1572872 | tf_op jit(solution)/shard_map/ppermute | solution.py:32
  36.8 5.7 %collective-permute-start.1 = (bf16[4,256,256]{2,1,0:T(8,128)(2,1)}, bf16[4,256,256]{2,1,0:T(8,128)(2,1)}, u32[]{:S(2)}, u32[]{:S(2)}) collective-permute-start(bf16[4,256,256]{2,1,0:T(8,128)(2,1)} %param.8), channel_id=1, source_target_pairs={{2,0},{3,1},{4,2},{5,3},{6,4},{7,5},{8,6},{9,7},{10,8},{11,9},{12,... | collective-permute-start | bytes 1572872 | tf_op jit(solution)/shard_map/ppermute | solution.py:32
  42.8 14.9 %collective-permute-done.1 = bf16[4,256,256]{2,1,0:T(8,128)(2,1)} collective-permute-done((bf16[4,256,256]{2,1,0:T(8,128)(2,1)}, bf16[4,256,256]{2,1,0:T(8,128)(2,1)}, u32[]{:S(2)}, u32[]{:S(2)}) %collective-permute-start.1) | collective-permute-done | bytes 524320 | tf_op jit(solution)/shard_map/ppermute | solution.py:32
  57.7 2.3 %pad_maximum_fusion.1 = bf16[2,4,256,256]{3,2,1,0:T(8,128)(2,1)} fusion(bf16[1,4,256,256]{3,2,1,0:T(8,128)(2,1)} %bitcast.13, bf16[1,4,256,256]{3,2,1,0:T(8,128)(2,1)} %bitcast.12), kind=kLoop, calls=%fused_computation.21 | loop fusion | flops 524288 | bytes 2097152 | tf_op jit(solution)/shard_map/stack | solution.py:33
  60.0 3.2 %collective-permute-start.2 = (bf16[2,4,256,256]{3,2,1,0:T(8,128)(2,1)}, bf16[2,4,256,256]{3,2,1,0:T(8,128)(2,1)}, u32[]{:S(2)}, u32[]{:S(2)}) collective-permute-start(bf16[2,4,256,256]{3,2,1,0:T(8,128)(2,1)} %pad_maximum_fusion.1), channel_id=1, source_target_pairs={{0,1},{1,0},{2,3},{3,2},{4,5},{5,4},{6,7},{7,6},{8,9},{9,8},{10,11... | collective-permute-start | bytes 3145736 | tf_op jit(solution)/shard_map/ppermute | solution.py:35
  64.7 4.5 %reshape.130 = bf16[8,32,48,64]{3,2,1,0:T(8,128)(2,1)} reshape(bf16[8,2,49152]{2,1,0:T(2,128)(2,1)S(1)} %all-to-all-done) | data formatting | bytes 3145728
  69.2 6.0 %copy.23 = f32[256,48,64]{0,2,1:T(8,128)} copy(bf16[256,48,64]{2,1,0:T(8,128)(2,1)} %bitcast.75) | data formatting | bytes 4718592 | tf_op jit(solution)/shard_map/convert_element_type | solution.py:64
  75.3 2.7 %convert_reduce_fusion = f32[48,64]{1,0:T(8,128)S(1)} fusion(bf16[8,32,48,64]{3,2,1,0:T(8,128)(2,1)} %reshape.130), kind=kLoop, calls=%fused_computation.13 | loop fusion | flops 1569792 | bytes 1585152 | tf_op jit(solution)/shard_map/reduce_sum | solution.py:66
  78.6 1.7 pad_maximum_fusion
  80.3 7.2 %fusion.6 = bf16[256,48,64]{0,2,1:T(8,128)(2,1)S(1)} fusion(bf16[16,256,256,1]{2,1,0,3:T(8,128)(2,1)S(1)} %bitcast.77, pred[16,64]{1,0:T(8,128)(4,1)S(1)} %iota_compare_fusion.5, bf16[256,48,64]{0,2,1:T(8,128)(2,1)S(1)} %multiply_convert_fusion, f32[48,64]{1,0:T(8,128)S(1)} %broadcast_multiply_fusion), kind=kOutput, calls=%fused_computation.8 | convolution fusion | flops 6457393152 | bytes 5256192 | tf_op jit(solution)/shard_map/rjk,rjtc->ktc/dot_general | solution.py:70
  87.5 4.0 %copy.25 = bf16[256,48,64]{2,1,0:T(8,128)(2,1)} copy(bf16[256,48,64]{0,2,1:T(8,128)(2,1)S(1)} %fusion.6) | data formatting | bytes 3145728 | tf_op jit(solution)/shard_map/convert_element_type | solution.py:72
  91.5 6.9 %reshape.133 = bf16[8,2,49152]{2,1,0:T(2,128)(2,1)} reshape(bf16[8,32,48,64]{3,2,1,0:T(8,128)(2,1)} %bitcast.76) | data formatting | bytes 3145728
  98.5 42.9 %all-to-all-start.2 = ((bf16[8,2,49152]{2,1,0:T(2,128)(2,1)}), bf16[8,2,49152]{2,1,0:T(2,128)(2,1)S(1)}, u32[]{:S(2)}, u32[]{:S(2)}) async-start(bf16[8,2,49152]{2,1,0:T(2,128)(2,1)} %reshape.133), calls=%async_computation.2 | async-start | bytes 3145728 | tf_op jit(solution)/shard_map/all_to_all | solution.py:74
  141.4 1.3 gather_fusion
  142.7 22.8 %all-to-all-done.2 = bf16[8,2,49152]{2,1,0:T(2,128)(2,1)S(1)} async-done(((bf16[8,2,49152]{2,1,0:T(2,128)(2,1)}), bf16[8,2,49152]{2,1,0:T(2,128)(2,1)S(1)}, u32[]{:S(2)}, u32[]{:S(2)}) %all-to-all-start.2) | async-done | bytes 1572896 | tf_op jit(solution)/shard_map/all_to_all | solution.py:74
  165.5 4.5 %reshape.134 = bf16[8,32,48,64]{3,2,1,0:T(8,128)(2,1)} reshape(bf16[8,2,49152]{2,1,0:T(2,128)(2,1)S(1)} %all-to-all-done.2) | data formatting | bytes 3145728
  170.0 4.3 %convolution_bitcast_fusion.1 = bf16[32,48,512]{2,1,0:T(8,128)(2,1)} fusion(bf16[8,32,48,64]{3,2,1,0:T(8,128)(2,1)} %reshape.134, s32[8,64]{1,0:T(8,128)S(1)} %multiply_add_fusion, s32[512]{0:T(512)S(1)} %get-tuple-element.2), kind=kOutput, calls=%fused_computation.14 | convolution fusion | flops 805568512 | bytes 3149824 | tf_op jit(solution)/shard_map/dkti,cdi->ktc/dot_general | solution.py:75
  175.1 1.1 fusion.41
  (42 shorter events, 7.5 us)
Async XLA Ops:
  0.6 13.9 %copy-start = (bf16[32,48,512]{2,1,0:T(8,128)(2,1)S(1)}, bf16[32,48,512]{2,1,0:T(8,128)(2,1)}, u32[]{:S(2)}) copy-start(bf16[32,48,512]{2,1,0:T(8,128)(2,1)} %param.6) | copy-start | bytes 4718596
  7.0 17.8 %all-to-all-start.1 = ((f32[8,1,2048]{2,1,0:T(1,128)}), f32[8,1,2048]{2,1,0:T(1,128)S(1)}, u32[]{:S(2)}, u32[]{:S(2)}) async-start(f32[8,1,2048]{2,1,0:T(1,128)} %reshape.131), calls=%async_computation.1 | async-start | bytes 131072 | tf_op jit(solution)/shard_map/all_to_all | solution.py:63
  17.9 24.6 %copy-start.3 = (s32[512]{0:T(512)S(1)}, s32[512]{0:T(512)}, u32[]{:S(2)}) copy-start(s32[512]{0:T(512)} %param.9) | copy-start | bytes 6148
  24.8 39.9 %all-to-all-start = ((bf16[8,2,49152]{2,1,0:T(2,128)(2,1)}), bf16[8,2,49152]{2,1,0:T(2,128)(2,1)S(1)}, u32[]{:S(2)}, u32[]{:S(2)}) async-start(bf16[8,2,49152]{2,1,0:T(2,128)(2,1)} %reshape.129), calls=%async_computation | async-start | bytes 3145728 | tf_op jit(solution)/shard_map/all_to_all | solution.py:62
  31.4 11.4 %collective-permute-start = (bf16[4,256,256]{2,1,0:T(8,128)(2,1)}, bf16[4,256,256]{2,1,0:T(8,128)(2,1)}, u32[]{:S(2)}, u32[]{:S(2)}) collective-permute-start(bf16[4,256,256]{2,1,0:T(8,128)(2,1)} %param.8), channel_id=1, source_target_pairs={{0,0},{1,1},{2,2},{3,3},{4,4},{5,5},{6,6},{7,7},{8,8},{9,9},{10,10... | collective-permute-start | bytes 1572872 | tf_op jit(solution)/shard_map/ppermute | solution.py:32
  36.8 20.9 %collective-permute-start.1 = (bf16[4,256,256]{2,1,0:T(8,128)(2,1)}, bf16[4,256,256]{2,1,0:T(8,128)(2,1)}, u32[]{:S(2)}, u32[]{:S(2)}) collective-permute-start(bf16[4,256,256]{2,1,0:T(8,128)(2,1)} %param.8), channel_id=1, source_target_pairs={{2,0},{3,1},{4,2},{5,3},{6,4},{7,5},{8,6},{9,7},{10,8},{11,9},{12,... | collective-permute-start | bytes 1572872 | tf_op jit(solution)/shard_map/ppermute | solution.py:32
  60.0 18.6 %collective-permute-start.2 = (bf16[2,4,256,256]{3,2,1,0:T(8,128)(2,1)}, bf16[2,4,256,256]{3,2,1,0:T(8,128)(2,1)}, u32[]{:S(2)}, u32[]{:S(2)}) collective-permute-start(bf16[2,4,256,256]{3,2,1,0:T(8,128)(2,1)} %pad_maximum_fusion.1), channel_id=1, source_target_pairs={{0,1},{1,0},{2,3},{3,2},{4,5},{5,4},{6,7},{7,6},{8,9},{9,8},{10,11... | collective-permute-start | bytes 3145736 | tf_op jit(solution)/shard_map/ppermute | solution.py:35
  75.2 2.8 %copy-start.1 = (f32[256,48,64]{0,2,1:T(8,128)S(1)}, f32[256,48,64]{0,2,1:T(8,128)}, u32[]{:S(2)}) copy-start(f32[256,48,64]{0,2,1:T(8,128)} %copy.23) | copy-start | bytes 9437188
  91.5 49.9 %copy-start.4 = (s32[128]{0:T(128)S(1)}, s32[128]{0:T(128)}, u32[]{:S(2)}) copy-start(s32[128]{0:T(128)} %param.11) | copy-start | bytes 1540
  98.5 67.0 %all-to-all-start.2 = ((bf16[8,2,49152]{2,1,0:T(2,128)(2,1)}), bf16[8,2,49152]{2,1,0:T(2,128)(2,1)S(1)}, u32[]{:S(2)}, u32[]{:S(2)}) async-start(bf16[8,2,49152]{2,1,0:T(2,128)(2,1)} %reshape.133), calls=%async_computation.2 | async-start | bytes 3145728 | tf_op jit(solution)/shard_map/all_to_all | solution.py:74
  170.0 4.3 %copy-start.2 = (bf16[8,32,48,64]{3,2,1,0:T(8,128)(2,1)S(1)}, bf16[8,32,48,64]{3,2,1,0:T(8,128)(2,1)}, u32[]{:S(2)}) copy-start(bf16[8,32,48,64]{3,2,1,0:T(8,128)(2,1)} %reshape.134) | copy-start | bytes 4718596
  174.3 0.8 copy-start.5

commit v4 on v3

--- a/solution.py
+++ b/solution.py
@@ -2,6 +2,14 @@
 import jax.numpy as jnp
 from jax import lax
 from jax.sharding import PartitionSpec as P
+
+
+def _split3(x):
+    hi = lax.reduce_precision(x, exponent_bits=8, mantissa_bits=7)
+    r1 = x - hi
+    mid = lax.reduce_precision(r1, exponent_bits=8, mantissa_bits=7)
+    lo = r1 - mid
+    return hi.astype(jnp.bfloat16), mid.astype(jnp.bfloat16), lo.astype(jnp.bfloat16)
 
 
 def local(ensemble, inflation, weights, region_ids, extinction, obs_cols):
@@ -22,12 +30,21 @@
     chip = me_space // 2
     core = me_space % 2
 
+    ring = n_chip // 2
+    pairs = [(0, ring // 2)] + [(b, ring - b) for b in range(1, ring // 2)]
+    pairs = pairs + [(a + ring, b + ring) for a, b in pairs]
+    owner_of = [0] * n_chip
+    slot_of = [0] * n_chip
+    for m, pair in enumerate(pairs):
+        for a, off in enumerate(pair):
+            owner_of[off] = m
+            slot_of[off] = a
     own = []
     for a in range(chips_per_dev):
         perm = []
         for m in range(n_member):
             for s in range(n_space):
-                src = 2 * ((s // 2 + chips_per_dev * m + a) % n_chip) + s % 2
+                src = 2 * ((s // 2 + pairs[m][a]) % n_chip) + s % 2
                 perm.append((m * n_space + src, m * n_space + s))
         own.append(lax.ppermute(weights, ("member", "space"), perm))
     own = jnp.stack(own)
@@ -37,8 +54,8 @@
 
     group = region_ids // reg_count
     offset = (group // 2 - chip) % n_chip
-    dest = offset // chips_per_dev
-    slot = (group % 2 != core).astype(jnp.int32) * chips_per_dev + offset % chips_per_dev
+    dest = jnp.array(owner_of, jnp.int32)[offset]
+    slot = (group % 2 != core).astype(jnp.int32) * chips_per_dev + jnp.array(slot_of, jnp.int32)[offset]
     group_hot = (group[:, None] == jnp.arange(n_space, dtype=jnp.int32)[None, :]).astype(jnp.int32)
     before = jnp.cumsum(group_hot, axis=0) - group_hot
     rank_in = jnp.sum(before * group_hot, axis=1)
@@ -57,12 +74,17 @@
     fac_perm = jnp.einsum(
         "jc,cdi->dji", factor, perm_mat.astype(jnp.float32), precision=lax.Precision.HIGHEST
     )
-    payload = jnp.einsum("jtc,cdi->djti", ensemble, perm_mat, preferred_element_type=jnp.bfloat16)
+    main = jnp.einsum("jtc,cdi->djti", ensemble, perm_mat, preferred_element_type=jnp.bfloat16)
+    pieces = jnp.stack(_split3(fac_perm), axis=1)
+    extra_rows = 3 * local_members // tracers
+    pieces = pieces.reshape(n_member, extra_rows, tracers, own_cols)
+    payload = jnp.concatenate([main, pieces], axis=1)
 
     received = lax.all_to_all(payload, "member", split_axis=0, concat_axis=0, tiled=True)
-    fac_got = lax.all_to_all(fac_perm, "member", split_axis=0, concat_axis=0, tiled=True)
-    ens32 = received.reshape(members, tracers, own_cols).astype(jnp.float32)
-    fac = fac_got.reshape(members, own_cols)
+    ens32 = received[:, :local_members].reshape(members, tracers, own_cols).astype(jnp.float32)
+    got = received[:, local_members:].reshape(n_member, 3, local_members, own_cols)
+    got = got.astype(jnp.float32)
+    fac = ((got[:, 0] + got[:, 1]) + got[:, 2]).reshape(members, own_cols)
     mean = jnp.sum(ens32, axis=0) / members
     anomaly = ((ens32 - mean[None]) * fac[:, None, :]).astype(jnp.bfloat16)
     mask = my_labels[None, :] == jnp.arange(n_slot, dtype=jnp.int32)[:, None]

time: 179 us -> 162 us (0.905)
  the two profiles are of different devices: /device:TPU:1 before, /device:TPU:152 now
where the time goes in v4:
time: 162 us; the launch traced here: 161 us
  starting transfers between devices  45.2 us (28%)
  waiting for transfers between devices  45.2 us (28%)
  local copies, waits for them, and re-layouts  35.1 us (22%)
  matrix products  17.4 us (11%)
  other arithmetic  17.3 us (11%)
    all_to_all x1, starting transfers between devices, local(): lax.all_to_all(result, 'member', split_axis=0, concat_axis=0, tiled=True)  32.6 us
    unnamed x14, local copies, waits for them, and re-layouts  22.8 us
    ppermute x2, waiting for transfers between devices, local(): own.append(lax.ppermute(weights, ('member', 'space'), perm))  22.7 us
    all_to_all x1, waiting for transfers between devices, local(): lax.all_to_all(result, 'member', split_axis=0, concat_axis=0, tiled=True)  22.5 us
    all_to_all x1, starting transfers between devices, local(): lax.all_to_all(payload, 'member', split_axis=0, concat_axis=0, tiled=True)  7.27 us
    dot_general x1, matrix products, local(): jnp.einsum('rjk,rjtc->ktc', w_all, masked, preferred_element_type=jnp.flo...  7.15 us
    convert_element_type x1, local copies, waits for them, and re-layouts, local(): received[:, :local_members].reshape(members, tracers, own_cols)  6.61 us
    ppermute x2, starting transfers between devices, local(): own.append(lax.ppermute(weights, ('member', 'space'), perm))  5.32 us
  transfers between devices with their start and end apart: 5, of which 2 were waited for; matrix products, arithmetic and copies ran while one was open for 15% of the time, Pallas kernels for 0%

profile of v4, /device:TPU:152, one launch (start us, length us, event | category | flops | bytes accessed | tf_op | source)
XLA Modules:
  0.0 161.1 jit_solution(3993690456468250862)
XLA Ops:
  1.5 1.2 reduce-window.6
  3.1 0.9 convolution_bitcast_fusion.3
  5.0 2.2 %convolution_bitcast_fusion = bf16[8,32,48,64]{3,2,1,0:T(8,128)(2,1)S(1)} fusion(bf16[32,48,512]{2,1,0:T(8,128)(2,1)S(1)} %copy-done, s32[8,64]{1,0:T(8,128)S(1)} %multiply_add_fusion, s32[512]{0:T(512)S(1)} %fusion.40), kind=kOutput, calls=%fused_computation.13 | convolution fusion | flops 805568512 | bytes 3149824 | tf_op jit(solution)/shard_map/jtc,cdi->djti/dot_general | solution.py:77
  7.3 2.3 %pad_maximum_fusion = bf16[8,34,48,64]{3,2,1,0:T(8,128)(2,1)} fusion(bf16[8,2,48,64]{3,2,1,0:T(8,128)(2,1)S(1)} %bitcast.88, bf16[8,32,48,64]{3,2,1,0:T(8,128)(2,1)S(1)} %convolution_bitcast_fusion), kind=kLoop, calls=%fused_computation.6 | loop fusion | flops 835584 | bytes 3342336 | tf_op jit(solution)/shard_map/concatenate | solution.py:81
  9.6 6.8 %reshape.200 = bf16[8,2,52224]{2,1,0:T(2,128)(2,1)} reshape(bf16[8,34,48,64]{3,2,1,0:T(8,128)(2,1)} %pad_maximum_fusion) | data formatting | bytes 3342336
  16.4 7.3 %all-to-all-start = ((bf16[8,2,52224]{2,1,0:T(2,128)(2,1)}), bf16[8,2,52224]{2,1,0:T(2,128)(2,1)S(1)}, u32[]{:S(2)}, u32[]{:S(2)}) async-start(bf16[8,2,52224]{2,1,0:T(2,128)(2,1)} %reshape.200), calls=%async_computation | async-start | bytes 3342336 | tf_op jit(solution)/shard_map/all_to_all | solution.py:83
  23.6 1.2 collective-permute-start.1
  24.8 4.1 %collective-permute-start = (bf16[4,256,256]{2,1,0:T(8,128)(2,1)}, bf16[4,256,256]{2,1,0:T(8,128)(2,1)}, u32[]{:S(2)}, u32[]{:S(2)}) collective-permute-start(bf16[4,256,256]{2,1,0:T(8,128)(2,1)} %param.10), channel_id=1, source_target_pairs={{0,0},{1,1},{2,2},{3,3},{4,4},{5,5},{6,6},{7,7},{8,8},{9,9},{10,10... | collective-permute-start | bytes 1572872 | tf_op jit(solution)/shard_map/ppermute | solution.py:49
  29.3 22.7 %collective-permute-done.1 = bf16[4,256,256]{2,1,0:T(8,128)(2,1)} collective-permute-done((bf16[4,256,256]{2,1,0:T(8,128)(2,1)}, bf16[4,256,256]{2,1,0:T(8,128)(2,1)}, u32[]{:S(2)}, u32[]{:S(2)}) %collective-permute-start.1) | collective-permute-done | bytes 524320 | tf_op jit(solution)/shard_map/ppermute | solution.py:49
  52.0 2.3 %pad_maximum_fusion.2 = bf16[2,4,256,256]{3,2,1,0:T(8,128)(2,1)} fusion(bf16[1,4,256,256]{3,2,1,0:T(8,128)(2,1)} %bitcast.19, bf16[1,4,256,256]{3,2,1,0:T(8,128)(2,1)} %bitcast.18), kind=kLoop, calls=%fused_computation.23 | loop fusion | flops 524288 | bytes 2097152 | tf_op jit(solution)/shard_map/stack | solution.py:50
  54.3 4.5 %reshape.201 = bf16[8,34,48,64]{3,2,1,0:T(8,128)(2,1)} reshape(bf16[8,2,52224]{2,1,0:T(2,128)(2,1)S(1)} %all-to-all-done) | data formatting | bytes 3342336
  58.8 5.2 %slice_convert_fusion = f32[8,32,48,64]{3,2,1,0:T(8,128)} fusion(bf16[8,34,48,64]{3,2,1,0:T(8,128)(2,1)} %reshape.201), kind=kLoop, calls=%fused_computation.7 | loop fusion | flops 786432 | bytes 4718592 | tf_op jit(solution)/shard_map/convert_element_type | solution.py:84
  64.1 6.6 %copy.29 = f32[256,48,64]{0,2,1:T(8,128)} copy(f32[256,48,64]{2,1,0:T(8,128)} %bitcast.85) | data formatting | bytes 6291456 | tf_op jit(solution)/shard_map/convert_element_type | solution.py:84
  70.7 2.7 %fusion.12 = f32[48,64]{1,0:T(8,128)S(1)} fusion(bf16[8,34,48,64]{3,2,1,0:T(8,128)(2,1)} %reshape.201), kind=kLoop, calls=%fused_computation.20 | loop fusion | flops 1569792 | bytes 1585152 | tf_op jit(solution)/shard_map/reduce_sum | solution.py:88
  74.0 1.7 %pad_maximum_fusion.1 = bf16[4,4,256,256]{3,2,1,0:T(8,128)(2,1)S(1)} fusion(bf16[2,4,256,256]{3,2,1,0:T(8,128)(2,1)} %collective-permute-done.2, bf16[1,4,256,256]{3,2,1,0:T(8,128)(2,1)} %bitcast.19, bf16[1,4,256,256]{3,2,1,0:T(8,128)(2,1)} %bitcast.18), kind=kLoop, calls=%fused_computation.12 | loop fusion | flops 2097152 | bytes 4194304 | tf_op jit(solution)/shard_map/concatenate | solution.py:53
  75.8 7.2 %fusion.6 = bf16[256,48,64]{0,2,1:T(8,128)(2,1)S(1)} fusion(bf16[16,256,256,1]{2,1,0,3:T(8,128)(2,1)S(1)} %bitcast.87, pred[16,64]{1,0:T(8,128)(4,1)S(1)} %iota_compare_fusion.5, bf16[256,48,64]{0,2,1:T(8,128)(2,1)S(1)} %multiply_convert_fusion, f32[48,64]{1,0:T(8,128)S(1)} %broadcast_multiply_fusion), kind=kOutput, calls=%fused_computation.10 | convolution fusion | flops 6457393152 | bytes 5256192 | tf_op jit(solution)/shard_map/rjk,rjtc->ktc/dot_general | solution.py:92
  82.9 4.0 %copy.31 = bf16[256,48,64]{2,1,0:T(8,128)(2,1)} copy(bf16[256,48,64]{0,2,1:T(8,128)(2,1)S(1)} %fusion.6) | data formatting | bytes 3145728 | tf_op jit(solution)/shard_map/convert_element_type | solution.py:94
  86.9 6.9 %reshape.202 = bf16[8,2,49152]{2,1,0:T(2,128)(2,1)} reshape(bf16[8,32,48,64]{3,2,1,0:T(8,128)(2,1)} %bitcast.86) | data formatting | bytes 3145728
  93.9 32.6 %all-to-all-start.1 = ((bf16[8,2,49152]{2,1,0:T(2,128)(2,1)}), bf16[8,2,49152]{2,1,0:T(2,128)(2,1)S(1)}, u32[]{:S(2)}, u32[]{:S(2)}) async-start(bf16[8,2,49152]{2,1,0:T(2,128)(2,1)} %reshape.202), calls=%async_computation.1 | async-start | bytes 3145728 | tf_op jit(solution)/shard_map/all_to_all | solution.py:96
  126.5 1.3 gather_fusion
  127.8 22.5 %all-to-all-done.1 = bf16[8,2,49152]{2,1,0:T(2,128)(2,1)S(1)} async-done(((bf16[8,2,49152]{2,1,0:T(2,128)(2,1)}), bf16[8,2,49152]{2,1,0:T(2,128)(2,1)S(1)}, u32[]{:S(2)}, u32[]{:S(2)}) %all-to-all-start.1) | async-done | bytes 1572896 | tf_op jit(solution)/shard_map/all_to_all | solution.py:96
  150.3 4.5 %reshape.203 = bf16[8,32,48,64]{3,2,1,0:T(8,128)(2,1)} reshape(bf16[8,2,49152]{2,1,0:T(2,128)(2,1)S(1)} %all-to-all-done.1) | data formatting | bytes 3145728
  154.8 4.3 %convolution_bitcast_fusion.1 = bf16[32,48,512]{2,1,0:T(8,128)(2,1)} fusion(bf16[8,32,48,64]{3,2,1,0:T(8,128)(2,1)} %reshape.203, s32[8,64]{1,0:T(8,128)S(1)} %multiply_add_fusion, s32[512]{0:T(512)S(1)} %fusion.40), kind=kOutput, calls=%fused_computation.15 | convolution fusion | flops 805568512 | bytes 3149824 | tf_op jit(solution)/shard_map/dkti,cdi->ktc/dot_general | solution.py:97
  160.0 1.1 fusion.43
  (40 shorter events, 4.1 us)
Async XLA Ops:
  0.6 4.4 %copy-start = (bf16[32,48,512]{2,1,0:T(8,128)(2,1)S(1)}, bf16[32,48,512]{2,1,0:T(8,128)(2,1)}, u32[]{:S(2)}) copy-start(bf16[32,48,512]{2,1,0:T(8,128)(2,1)} %param.8) | copy-start | bytes 4718596
  16.4 37.9 %all-to-all-start = ((bf16[8,2,52224]{2,1,0:T(2,128)(2,1)}), bf16[8,2,52224]{2,1,0:T(2,128)(2,1)S(1)}, u32[]{:S(2)}, u32[]{:S(2)}) async-start(bf16[8,2,52224]{2,1,0:T(2,128)(2,1)} %reshape.200), calls=%async_computation | async-start | bytes 3342336 | tf_op jit(solution)/shard_map/all_to_all | solution.py:83
  23.6 28.4 %collective-permute-start.1 = (bf16[4,256,256]{2,1,0:T(8,128)(2,1)}, bf16[4,256,256]{2,1,0:T(8,128)(2,1)}, u32[]{:S(2)}, u32[]{:S(2)}) collective-permute-start(bf16[4,256,256]{2,1,0:T(8,128)(2,1)} %param.10), channel_id=1, source_target_pairs={{8,0},{9,1},{10,2},{11,3},{12,4},{13,5},{14,6},{15,7},{16,8},{17,9... | collective-permute-start | bytes 1572872 | tf_op jit(solution)/shard_map/ppermute | solution.py:49
  24.8 27.2 %collective-permute-start = (bf16[4,256,256]{2,1,0:T(8,128)(2,1)}, bf16[4,256,256]{2,1,0:T(8,128)(2,1)}, u32[]{:S(2)}, u32[]{:S(2)}) collective-permute-start(bf16[4,256,256]{2,1,0:T(8,128)(2,1)} %param.10), channel_id=1, source_target_pairs={{0,0},{1,1},{2,2},{3,3},{4,4},{5,5},{6,6},{7,7},{8,8},{9,9},{10,10... | collective-permute-start | bytes 1572872 | tf_op jit(solution)/shard_map/ppermute | solution.py:49
  54.2 19.8 %collective-permute-start.2 = (bf16[2,4,256,256]{3,2,1,0:T(8,128)(2,1)}, bf16[2,4,256,256]{3,2,1,0:T(8,128)(2,1)}, u32[]{:S(2)}, u32[]{:S(2)}) collective-permute-start(bf16[2,4,256,256]{3,2,1,0:T(8,128)(2,1)} %pad_maximum_fusion.2), channel_id=1, source_target_pairs={{0,1},{1,0},{2,3},{3,2},{4,5},{5,4},{6,7},{7,6},{8,9},{9,8},{10,11... | collective-permute-start | bytes 3145736 | tf_op jit(solution)/shard_map/ppermute | solution.py:52
  58.8 5.2 %slice-start = ((bf16[8,34,48,64]{3,2,1,0:T(8,128)(2,1)}), bf16[8,2,48,64]{3,2,1,0:T(8,128)(2,1)S(1)}, s32[]{:S(2)}) async-start(bf16[8,34,48,64]{3,2,1,0:T(8,128)(2,1)} %reshape.201), calls=%async_computation.2 | async-start | bytes 393216 | tf_op jit(solution)/shard_map/slice | solution.py:85
  70.7 2.8 %copy-start.2 = (f32[256,48,64]{0,2,1:T(8,128)S(1)}, f32[256,48,64]{0,2,1:T(8,128)}, u32[]{:S(2)}) copy-start(f32[256,48,64]{0,2,1:T(8,128)} %copy.29) | copy-start | bytes 9437188
  86.9 39.6 %copy-start.3 = (s32[128]{0:T(128)S(1)}, s32[128]{0:T(128)}, u32[]{:S(2)}) copy-start(s32[128]{0:T(128)} %param.13) | copy-start | bytes 1540
  93.9 56.5 %all-to-all-start.1 = ((bf16[8,2,49152]{2,1,0:T(2,128)(2,1)}), bf16[8,2,49152]{2,1,0:T(2,128)(2,1)S(1)}, u32[]{:S(2)}, u32[]{:S(2)}) async-start(bf16[8,2,49152]{2,1,0:T(2,128)(2,1)} %reshape.202), calls=%async_computation.1 | async-start | bytes 3145728 | tf_op jit(solution)/shard_map/all_to_all | solution.py:96
  154.8 4.3 %copy-start.1 = (bf16[8,32,48,64]{3,2,1,0:T(8,128)(2,1)S(1)}, bf16[8,32,48,64]{3,2,1,0:T(8,128)(2,1)}, u32[]{:S(2)}) copy-start(bf16[8,32,48,64]{3,2,1,0:T(8,128)(2,1)} %reshape.203) | copy-start | bytes 4718596
  159.1 0.8 copy-start.4

commit v5 on v4

--- a/solution.py
+++ b/solution.py
@@ -81,17 +81,22 @@
     payload = jnp.concatenate([main, pieces], axis=1)
 
     received = lax.all_to_all(payload, "member", split_axis=0, concat_axis=0, tiled=True)
-    ens32 = received[:, :local_members].reshape(members, tracers, own_cols).astype(jnp.float32)
+    ens = received[:, :local_members].reshape(members, tracers, own_cols)
     got = received[:, local_members:].reshape(n_member, 3, local_members, own_cols)
     got = got.astype(jnp.float32)
     fac = ((got[:, 0] + got[:, 1]) + got[:, 2]).reshape(members, own_cols)
-    mean = jnp.sum(ens32, axis=0) / members
-    anomaly = ((ens32 - mean[None]) * fac[:, None, :]).astype(jnp.bfloat16)
+    j_iota = jnp.arange(members, dtype=jnp.int32)
+    eye = (j_iota[:, None] == j_iota[None, :]).astype(jnp.bfloat16)
+    ens_t = jnp.einsum("jtc,jk->tck", ens, eye, preferred_element_type=jnp.bfloat16)
+    ens32 = ens_t.astype(jnp.float32)
+    mean = jnp.sum(ens32, axis=2) / members
+    anomaly = ((ens32 - mean[:, :, None]) * fac.T[None]).astype(jnp.bfloat16)
     mask = my_labels[None, :] == jnp.arange(n_slot, dtype=jnp.int32)[:, None]
-    masked = jnp.where(mask[:, None, None, :], anomaly[None], jnp.zeros((), jnp.bfloat16))
-    inc = jnp.einsum("rjk,rjtc->ktc", w_all, masked, preferred_element_type=jnp.float32)
+    masked = jnp.where(mask[:, None, :, None], anomaly[None], jnp.zeros((), jnp.bfloat16))
+    inc = jnp.einsum("rtcj,rjk->tck", masked, w_all, preferred_element_type=jnp.float32)
     inc = lax.reduce_precision(inc, exponent_bits=8, mantissa_bits=7)
-    result = (mean[None] + inc).astype(jnp.bfloat16)
+    result_t = (mean[:, :, None] + inc).astype(jnp.bfloat16)
+    result = jnp.einsum("kl,tcl->ktc", eye, result_t, preferred_element_type=jnp.bfloat16)
     result = result.reshape(n_member, local_members, tracers, own_cols)
     returned = lax.all_to_all(result, "member", split_axis=0, concat_axis=0, tiled=True)
     analysis = jnp.einsum("dkti,cdi->ktc", returned, perm_mat, preferred_element_type=jnp.bfloat16)

time: 162 us -> 165 us (1.019)
  the two profiles are of different devices: /device:TPU:152 before, /device:TPU:1 now
where the time goes in v5:
time: 165 us; the launch traced here: 162 us
  starting transfers between devices  56.4 us (34%)
  waiting for transfers between devices  36.1 us (22%)
  local copies, waits for them, and re-layouts  33.8 us (20%)
  matrix products  24.1 us (15%)
  other arithmetic  10.7 us (6%)
    all_to_all x1, starting transfers between devices, local(): lax.all_to_all(result, 'member', split_axis=0, concat_axis=0, tiled=True)  26.6 us
    all_to_all x1, waiting for transfers between devices, local(): lax.all_to_all(result, 'member', split_axis=0, concat_axis=0, tiled=True)  22.8 us
    unnamed x12, local copies, waits for them, and re-layouts  22.7 us
    ppermute x2, waiting for transfers between devices, local(): own.append(lax.ppermute(weights, ('member', 'space'), perm))  13.3 us
    ppermute x2, starting transfers between devices, local(): own.append(lax.ppermute(weights, ('member', 'space'), perm))  12.4 us
    dot_general x1, matrix products, local(): jnp.einsum('kl,tcl->ktc', eye, result_t, preferred_element_type=jnp.bfloa...  10.6 us
    ppermute x1, starting transfers between devices, local(): sib = lax.ppermute(own, ('member', 'space'), sib_perm)  9.96 us
    all_to_all x1, starting transfers between devices, local(): lax.all_to_all(payload, 'member', split_axis=0, concat_axis=0, tiled=True)  7.48 us
  transfers between devices with their start and end apart: 5, of which 2 were waited for; matrix products, arithmetic and copies ran while one was open for 10% of the time, Pallas kernels for 0%

profile of v5, /device:TPU:1, one launch (start us, length us, event | category | flops | bytes accessed | tf_op | source)
XLA Modules:
  0.0 161.9 jit_solution(5246751605740490768)
XLA Ops:
  1.5 1.2 reduce-window.6
  3.1 0.9 convolution_bitcast_fusion.3
  4.1 2.2 %convolution_bitcast_fusion = bf16[8,32,48,64]{3,2,1,0:T(8,128)(2,1)S(1)} fusion(bf16[32,48,512]{2,1,0:T(8,128)(2,1)S(1)} %copy-done, s32[8,64]{1,0:T(8,128)S(1)} %multiply_add_fusion, s32[512]{0:T(512)S(1)} %fusion.49), kind=kOutput, calls=%fused_computation.17 | convolution fusion | flops 805568512 | bytes 3149824 | tf_op jit(solution)/shard_map/jtc,cdi->djti/dot_general | solution.py:77
  7.3 2.3 %pad_maximum_fusion = bf16[8,34,48,64]{3,2,1,0:T(8,128)(2,1)} fusion(bf16[8,2,48,64]{3,2,1,0:T(8,128)(2,1)S(1)} %bitcast.97, bf16[8,32,48,64]{3,2,1,0:T(8,128)(2,1)S(1)} %convolution_bitcast_fusion), kind=kLoop, calls=%fused_computation.8 | loop fusion | flops 835584 | bytes 3342336 | tf_op jit(solution)/shard_map/concatenate | solution.py:81
  9.6 6.8 %reshape.186 = bf16[8,2,52224]{2,1,0:T(2,128)(2,1)} reshape(bf16[8,34,48,64]{3,2,1,0:T(8,128)(2,1)} %pad_maximum_fusion) | data formatting | bytes 3342336
  16.4 7.5 %all-to-all-start = ((bf16[8,2,52224]{2,1,0:T(2,128)(2,1)}), bf16[8,2,52224]{2,1,0:T(2,128)(2,1)S(1)}, u32[]{:S(2)}, u32[]{:S(2)}) async-start(bf16[8,2,52224]{2,1,0:T(2,128)(2,1)} %reshape.186), calls=%async_computation | async-start | bytes 3342336 | tf_op jit(solution)/shard_map/all_to_all | solution.py:83
  23.8 5.4 %collective-permute-start = (bf16[4,256,256]{2,1,0:T(8,128)(2,1)}, bf16[4,256,256]{2,1,0:T(8,128)(2,1)}, u32[]{:S(2)}, u32[]{:S(2)}) collective-permute-start(bf16[4,256,256]{2,1,0:T(8,128)(2,1)} %param.10), channel_id=1, source_target_pairs={{0,0},{1,1},{2,2},{3,3},{4,4},{5,5},{6,6},{7,7},{8,8},{9,9},{10,10... | collective-permute-start | bytes 1572872 | tf_op jit(solution)/shard_map/ppermute | solution.py:49
  29.2 7.0 %collective-permute-start.1 = (bf16[4,256,256]{2,1,0:T(8,128)(2,1)}, bf16[4,256,256]{2,1,0:T(8,128)(2,1)}, u32[]{:S(2)}, u32[]{:S(2)}) collective-permute-start(bf16[4,256,256]{2,1,0:T(8,128)(2,1)} %param.10), channel_id=1, source_target_pairs={{8,0},{9,1},{10,2},{11,3},{12,4},{13,5},{14,6},{15,7},{16,8},{17,9... | collective-permute-start | bytes 1572872 | tf_op jit(solution)/shard_map/ppermute | solution.py:49
  36.5 13.3 %collective-permute-done.1 = bf16[4,256,256]{2,1,0:T(8,128)(2,1)} collective-permute-done((bf16[4,256,256]{2,1,0:T(8,128)(2,1)}, bf16[4,256,256]{2,1,0:T(8,128)(2,1)}, u32[]{:S(2)}, u32[]{:S(2)}) %collective-permute-start.1) | collective-permute-done | bytes 524320 | tf_op jit(solution)/shard_map/ppermute | solution.py:49
  49.8 2.3 %pad_maximum_fusion.2 = bf16[2,4,256,256]{3,2,1,0:T(8,128)(2,1)} fusion(bf16[1,4,256,256]{3,2,1,0:T(8,128)(2,1)} %bitcast.20, bf16[1,4,256,256]{3,2,1,0:T(8,128)(2,1)} %bitcast.19), kind=kLoop, calls=%fused_computation.27 | loop fusion | flops 524288 | bytes 2097152 | tf_op jit(solution)/shard_map/stack | solution.py:50
  52.1 10.0 %collective-permute-start.2 = (bf16[2,4,256,256]{3,2,1,0:T(8,128)(2,1)}, bf16[2,4,256,256]{3,2,1,0:T(8,128)(2,1)}, u32[]{:S(2)}, u32[]{:S(2)}) collective-permute-start(bf16[2,4,256,256]{3,2,1,0:T(8,128)(2,1)} %pad_maximum_fusion.2), channel_id=1, source_target_pairs={{0,1},{1,0},{2,3},{3,2},{4,5},{5,4},{6,7},{7,6},{8,9},{9,8},{10,11... | collective-permute-start | bytes 3145736 | tf_op jit(solution)/shard_map/ppermute | solution.py:52
  62.1 4.5 %reshape.187 = bf16[8,34,48,64]{3,2,1,0:T(8,128)(2,1)} reshape(bf16[8,2,52224]{2,1,0:T(2,128)(2,1)S(1)} %all-to-all-done) | data formatting | bytes 3342336
  66.5 4.1 %slice.65 = bf16[8,32,48,64]{3,2,1,0:T(8,128)(2,1)} slice(bf16[8,34,48,64]{3,2,1,0:T(8,128)(2,1)} %reshape.187), slice={[0:8], [0:32], [0:48], [0:64]} | slice | bytes 3145728 | tf_op jit(solution)/shard_map/slice | solution.py:84
  70.8 3.2 %convert_reduce_fusion = (f32[48,64]{1,0:T(8,128)S(1)}, bf16[48,64,256]{2,1,0:T(8,128)(2,1)S(1)}) fusion(bf16[256,48,64]{2,1,0:T(8,128)(2,1)} %bitcast.94), kind=kOutput, calls=%fused_computation.7 | convolution fusion | flops 404288512 | bytes 3158016 | tf_op jit(solution)/shard_map/jtc,jk->tck/dot_general | solution.py:90
  74.6 3.1 %pad_maximum_fusion.1 = bf16[4,4,256,256]{3,2,1,0:T(8,128)(2,1)} fusion(bf16[2,4,256,256]{3,2,1,0:T(8,128)(2,1)} %collective-permute-done.2, bf16[1,4,256,256]{3,2,1,0:T(8,128)(2,1)} %bitcast.20, bf16[1,4,256,256]{3,2,1,0:T(8,128)(2,1)} %bitcast.19), kind=kLoop, calls=%fused_computation.16 | loop fusion | flops 2097152 | bytes 4194304 | tf_op jit(solution)/shard_map/concatenate | solution.py:53
  77.6 10.6 %fusion.15 = bf16[256,48,64]{0,2,1:T(8,128)(2,1)} fusion(bf16[16,256,256,1]{2,1,3,0:T(8,128)(2,1)} %bitcast.96, pred[16,64]{1,0:T(8,128)(4,1)S(1)} %iota_compare_fusion.6, bf16[48,64,256]{2,1,0:T(8,128)(2,1)S(1)} %fusion.6, f32[48,64]{1,0:T(8,128)S(1)} %broadcast_multiply_fusion), kind=kOutput, calls=%fused_computation.20 | convolution fusion | flops 6860111872 | bytes 5256192 | tf_op jit(solution)/shard_map/kl,tcl->ktc/dot_general | solution.py:99
  88.2 5.3 %copy.31 = bf16[256,48,64]{2,1,0:T(8,128)(2,1)} copy(bf16[256,48,64]{0,2,1:T(8,128)(2,1)} %fusion.15) | data formatting | bytes 3145728 | tf_op jit(solution)/shard_map/kl,tcl->ktc/dot_general | solution.py:99
  93.5 6.9 %reshape.188 = bf16[8,2,49152]{2,1,0:T(2,128)(2,1)} reshape(bf16[8,32,48,64]{3,2,1,0:T(8,128)(2,1)} %bitcast.95) | data formatting | bytes 3145728
  100.5 26.6 %all-to-all-start.1 = ((bf16[8,2,49152]{2,1,0:T(2,128)(2,1)}), bf16[8,2,49152]{2,1,0:T(2,128)(2,1)S(1)}, u32[]{:S(2)}, u32[]{:S(2)}) async-start(bf16[8,2,49152]{2,1,0:T(2,128)(2,1)} %reshape.188), calls=%async_computation.1 | async-start | bytes 3145728 | tf_op jit(solution)/shard_map/all_to_all | solution.py:101
  127.1 1.3 gather_fusion
  128.4 22.8 %all-to-all-done.1 = bf16[8,2,49152]{2,1,0:T(2,128)(2,1)S(1)} async-done(((bf16[8,2,49152]{2,1,0:T(2,128)(2,1)}), bf16[8,2,49152]{2,1,0:T(2,128)(2,1)S(1)}, u32[]{:S(2)}, u32[]{:S(2)}) %all-to-all-start.1) | async-done | bytes 1572896 | tf_op jit(solution)/shard_map/all_to_all | solution.py:101
  151.1 4.5 %reshape.189 = bf16[8,32,48,64]{3,2,1,0:T(8,128)(2,1)} reshape(bf16[8,2,49152]{2,1,0:T(2,128)(2,1)S(1)} %all-to-all-done.1) | data formatting | bytes 3145728
  155.6 4.3 %convolution_bitcast_fusion.1 = bf16[32,48,512]{2,1,0:T(8,128)(2,1)} fusion(bf16[8,32,48,64]{3,2,1,0:T(8,128)(2,1)} %reshape.189, s32[8,64]{1,0:T(8,128)S(1)} %multiply_add_fusion, s32[512]{0:T(512)S(1)} %fusion.49), kind=kOutput, calls=%fused_computation.19 | convolution fusion | flops 805568512 | bytes 3149824 | tf_op jit(solution)/shard_map/dkti,cdi->ktc/dot_general | solution.py:102
  160.8 1.1 fusion.52
  (37 shorter events, 4.0 us)
Async XLA Ops:
  0.6 3.4 %copy-start = (bf16[32,48,512]{2,1,0:T(8,128)(2,1)S(1)}, bf16[32,48,512]{2,1,0:T(8,128)(2,1)}, u32[]{:S(2)}) copy-start(bf16[32,48,512]{2,1,0:T(8,128)(2,1)} %param.8) | copy-start | bytes 4718596
  16.4 45.7 %all-to-all-start = ((bf16[8,2,52224]{2,1,0:T(2,128)(2,1)}), bf16[8,2,52224]{2,1,0:T(2,128)(2,1)S(1)}, u32[]{:S(2)}, u32[]{:S(2)}) async-start(bf16[8,2,52224]{2,1,0:T(2,128)(2,1)} %reshape.186), calls=%async_computation | async-start | bytes 3342336 | tf_op jit(solution)/shard_map/all_to_all | solution.py:83
  23.8 12.7 %collective-permute-start = (bf16[4,256,256]{2,1,0:T(8,128)(2,1)}, bf16[4,256,256]{2,1,0:T(8,128)(2,1)}, u32[]{:S(2)}, u32[]{:S(2)}) collective-permute-start(bf16[4,256,256]{2,1,0:T(8,128)(2,1)} %param.10), channel_id=1, source_target_pairs={{0,0},{1,1},{2,2},{3,3},{4,4},{5,5},{6,6},{7,7},{8,8},{9,9},{10,10... | collective-permute-start | bytes 1572872 | tf_op jit(solution)/shard_map/ppermute | solution.py:49
  29.2 20.6 %collective-permute-start.1 = (bf16[4,256,256]{2,1,0:T(8,128)(2,1)}, bf16[4,256,256]{2,1,0:T(8,128)(2,1)}, u32[]{:S(2)}, u32[]{:S(2)}) collective-permute-start(bf16[4,256,256]{2,1,0:T(8,128)(2,1)} %param.10), channel_id=1, source_target_pairs={{8,0},{9,1},{10,2},{11,3},{12,4},{13,5},{14,6},{15,7},{16,8},{17,9... | collective-permute-start | bytes 1572872 | tf_op jit(solution)/shard_map/ppermute | solution.py:49
  52.1 22.4 %collective-permute-start.2 = (bf16[2,4,256,256]{3,2,1,0:T(8,128)(2,1)}, bf16[2,4,256,256]{3,2,1,0:T(8,128)(2,1)}, u32[]{:S(2)}, u32[]{:S(2)}) collective-permute-start(bf16[2,4,256,256]{3,2,1,0:T(8,128)(2,1)} %pad_maximum_fusion.2), channel_id=1, source_target_pairs={{0,1},{1,0},{2,3},{3,2},{4,5},{5,4},{6,7},{7,6},{8,9},{9,8},{10,11... | collective-permute-start | bytes 3145736 | tf_op jit(solution)/shard_map/ppermute | solution.py:52
  66.5 4.2 %slice-start = ((bf16[8,34,48,64]{3,2,1,0:T(8,128)(2,1)}), bf16[8,2,48,64]{3,2,1,0:T(8,128)(2,1)S(1)}, s32[]{:S(2)}) async-start(bf16[8,34,48,64]{3,2,1,0:T(8,128)(2,1)} %reshape.187), calls=%async_computation.2 | async-start | bytes 393216 | tf_op jit(solution)/shard_map/slice | solution.py:85
  93.5 33.5 %copy-start.2 = (s32[128]{0:T(128)S(1)}, s32[128]{0:T(128)}, u32[]{:S(2)}) copy-start(s32[128]{0:T(128)} %param.13) | copy-start | bytes 1540
  100.5 50.7 %all-to-all-start.1 = ((bf16[8,2,49152]{2,1,0:T(2,128)(2,1)}), bf16[8,2,49152]{2,1,0:T(2,128)(2,1)S(1)}, u32[]{:S(2)}, u32[]{:S(2)}) async-start(bf16[8,2,49152]{2,1,0:T(2,128)(2,1)} %reshape.188), calls=%async_computation.1 | async-start | bytes 3145728 | tf_op jit(solution)/shard_map/all_to_all | solution.py:101
  155.6 4.3 %copy-start.1 = (bf16[8,32,48,64]{3,2,1,0:T(8,128)(2,1)S(1)}, bf16[8,32,48,64]{3,2,1,0:T(8,128)(2,1)}, u32[]{:S(2)}) copy-start(bf16[8,32,48,64]{3,2,1,0:T(8,128)(2,1)} %reshape.189) | copy-start | bytes 4718596
  159.9 0.8 copy-start.3

commit v6 on v4

--- a/solution.py
+++ b/solution.py
@@ -74,26 +74,33 @@
     fac_perm = jnp.einsum(
         "jc,cdi->dji", factor, perm_mat.astype(jnp.float32), precision=lax.Precision.HIGHEST
     )
+    flat = tracers * own_cols
     main = jnp.einsum("jtc,cdi->djti", ensemble, perm_mat, preferred_element_type=jnp.bfloat16)
-    pieces = jnp.stack(_split3(fac_perm), axis=1)
-    extra_rows = 3 * local_members // tracers
-    pieces = pieces.reshape(n_member, extra_rows, tracers, own_cols)
-    payload = jnp.concatenate([main, pieces], axis=1)
+    main = main.reshape(n_member, local_members, flat)
+    hi, mid, lo = _split3(fac_perm)
+    spare = 128 - (3 * own_cols) % 128
+    pad = jnp.zeros((n_member, local_members, spare), jnp.bfloat16)
+    payload = jnp.concatenate([main, hi, mid, lo, pad], axis=2)
 
     received = lax.all_to_all(payload, "member", split_axis=0, concat_axis=0, tiled=True)
-    ens32 = received[:, :local_members].reshape(members, tracers, own_cols).astype(jnp.float32)
-    got = received[:, local_members:].reshape(n_member, 3, local_members, own_cols)
-    got = got.astype(jnp.float32)
-    fac = ((got[:, 0] + got[:, 1]) + got[:, 2]).reshape(members, own_cols)
+    received = received.reshape(members, payload.shape[2])
+    ens32 = received[:, :flat].astype(jnp.float32)
+    got = received[:, flat:].astype(jnp.float32)
+    fac = (got[:, 0:own_cols] + got[:, own_cols:2 * own_cols]) + got[:, 2 * own_cols:3 * own_cols]
+    lane_col = jnp.arange(flat, dtype=jnp.int32) % own_cols
+    spread = (jnp.arange(own_cols, dtype=jnp.int32)[:, None] == lane_col[None, :]).astype(jnp.float32)
+    fac_wide = jnp.dot(fac, spread, precision=lax.Precision.HIGHEST)
     mean = jnp.sum(ens32, axis=0) / members
-    anomaly = ((ens32 - mean[None]) * fac[:, None, :]).astype(jnp.bfloat16)
+    anomaly = ((ens32 - mean[None]) * fac_wide).astype(jnp.bfloat16)
     mask = my_labels[None, :] == jnp.arange(n_slot, dtype=jnp.int32)[:, None]
-    masked = jnp.where(mask[:, None, None, :], anomaly[None], jnp.zeros((), jnp.bfloat16))
-    inc = jnp.einsum("rjk,rjtc->ktc", w_all, masked, preferred_element_type=jnp.float32)
+    mask = jnp.tile(mask, (1, tracers))
+    masked = jnp.where(mask[:, None, :], anomaly[None], jnp.zeros((), jnp.bfloat16))
+    inc = jnp.einsum("rjk,rjx->kx", w_all, masked, preferred_element_type=jnp.float32)
     inc = lax.reduce_precision(inc, exponent_bits=8, mantissa_bits=7)
     result = (mean[None] + inc).astype(jnp.bfloat16)
-    result = result.reshape(n_member, local_members, tracers, own_cols)
+    result = result.reshape(n_member, local_members, flat)
     returned = lax.all_to_all(result, "member", split_axis=0, concat_axis=0, tiled=True)
+    returned = returned.reshape(n_member, local_members, tracers, own_cols)
     analysis = jnp.einsum("dkti,cdi->ktc", returned, perm_mat, preferred_element_type=jnp.bfloat16)
 
     local_index = obs_cols - me_space * columns

time: 162 us -> 134 us (0.83)
  the two profiles are of different devices: /device:TPU:152 before, /device:TPU:136 now
where the time goes in v6:
time: 134 us; the launch traced here: 133 us
  waiting for transfers between devices  51.2 us (38%)
  starting transfers between devices  39.4 us (29%)
  matrix products  20.1 us (15%)
  local copies, waits for them, and re-layouts  14.7 us (11%)
  other arithmetic  6.71 us (5%)
    all_to_all x1, starting transfers between devices, local(): lax.all_to_all(result, 'member', split_axis=0, concat_axis=0, tiled=True)  28.1 us
    ppermute x2, waiting for transfers between devices, local(): own.append(lax.ppermute(weights, ('member', 'space'), perm))  27.2 us
    all_to_all x1, waiting for transfers between devices, local(): lax.all_to_all(result, 'member', split_axis=0, concat_axis=0, tiled=True)  22.9 us
    dot_general x1, matrix products, local(): jnp.einsum('rjk,rjx->kx', w_all, masked, preferred_element_type=jnp.float32)  7.81 us
    all_to_all x1, starting transfers between devices, local(): lax.all_to_all(payload, 'member', split_axis=0, concat_axis=0, tiled=True)  6.03 us
    ppermute x2, starting transfers between devices, local(): own.append(lax.ppermute(weights, ('member', 'space'), perm))  5.35 us
    reshape x1, local copies, waits for them, and re-layouts, local(): returned = returned.reshape(n_member, local_members, tracers, own_cols)  4.86 us
    dot_general x1, matrix products, local(): jnp.einsum('dkti,cdi->ktc', returned, perm_mat, preferred_element_type=jn...  4.31 us
  transfers between devices with their start and end apart: 5, of which 3 were waited for; matrix products, arithmetic and copies ran while one was open for 4% of the time, Pallas kernels for 0%

profile of v6, /device:TPU:136, one launch (start us, length us, event | category | flops | bytes accessed | tf_op | source)
XLA Modules:
  0.0 133.0 jit_solution(15207002193039906321)
XLA Ops:
  0.7 0.8 fusion.48
  1.5 1.2 reduce-window.6
  2.7 0.2 slice_reduce_fusion
  3.1 3.4 %convolution_bitcast_fusion = bf16[8,32,48,64]{3,2,1,0:T(8,128)(2,1)} fusion(bf16[32,48,512]{2,1,0:T(8,128)(2,1)S(1)} %copy-done, s32[8,64]{1,0:T(8,128)S(1)} %multiply_add_fusion, s32[512]{0:T(512)S(1)} %fusion.50), kind=kOutput, calls=%fused_computation.15 | convolution fusion | flops 805568512 | bytes 3149824 | tf_op jit(solution)/shard_map/jtc,cdi->djti/dot_general | solution.py:78
  6.5 4.0 %reshape.126 = bf16[8,32,3072]{2,1,0:T(8,128)(2,1)S(1)} reshape(bf16[8,32,48,64]{3,2,1,0:T(8,128)(2,1)} %convolution_bitcast_fusion) | data formatting | bytes 3145728 | tf_op jit(solution)/shard_map/reshape | solution.py:79
  10.8 0.9 fusion.33
  11.7 2.0 %concatenate.7 = bf16[8,32,3328]{2,1,0:T(8,128)(2,1)} concatenate(bf16[8,32,3072]{2,1,0:T(8,128)(2,1)S(1)} %reshape.126, bf16[8,32,64]{2,1,0:T(8,128)(2,1)S(1)} %get-tuple-element.6, bf16[8,32,64]{2,1,0:T(8,128)(2,1)S(1)} %get-tuple-element.5, bf16[8,32,64]{2,1,0:T(8,128)(2,1)S(1)} %get-tuple-element.4, bf16[8,32,64]{2,1,0:T(8,128)(2,1)S(1)} %broadcast_in_dim.64), dimensions={2} | concatenate | bytes 3407872 | tf_op jit(solution)/shard_map/concatenate | solution.py:83
  13.6 6.0 %all-to-all-start = ((bf16[8,32,3328]{2,1,0:T(8,128)(2,1)}), bf16[8,32,3328]{2,1,0:T(8,128)(2,1)S(1)}, u32[]{:S(2)}, u32[]{:S(2)}) async-start(bf16[8,32,3328]{2,1,0:T(8,128)(2,1)} %concatenate.7), calls=%async_computation | async-start | bytes 3407872 | tf_op jit(solution)/shard_map/all_to_all | solution.py:85
  19.7 5.3 %collective-permute-start = (bf16[4,256,256]{2,1,0:T(8,128)(2,1)}, bf16[4,256,256]{2,1,0:T(8,128)(2,1)}, u32[]{:S(2)}, u32[]{:S(2)}) collective-permute-start(bf16[4,256,256]{2,1,0:T(8,128)(2,1)} %param.10), channel_id=1, source_target_pairs={{0,0},{1,1},{2,2},{3,3},{4,4},{5,5},{6,6},{7,7},{8,8},{9,9},{10,10... | collective-permute-start | bytes 1572872 | tf_op jit(solution)/shard_map/ppermute | solution.py:49
  25.6 27.2 %collective-permute-done.1 = bf16[4,256,256]{2,1,0:T(8,128)(2,1)} collective-permute-done((bf16[4,256,256]{2,1,0:T(8,128)(2,1)}, bf16[4,256,256]{2,1,0:T(8,128)(2,1)}, u32[]{:S(2)}, u32[]{:S(2)}) %collective-permute-start.1) | collective-permute-done | bytes 524320 | tf_op jit(solution)/shard_map/ppermute | solution.py:49
  52.8 2.3 %pad_maximum_fusion.1 = bf16[2,4,256,256]{3,2,1,0:T(8,128)(2,1)} fusion(bf16[1,4,256,256]{3,2,1,0:T(8,128)(2,1)} %bitcast.10, bf16[1,4,256,256]{3,2,1,0:T(8,128)(2,1)} %bitcast.9), kind=kLoop, calls=%fused_computation.25 | loop fusion | flops 524288 | bytes 2097152 | tf_op jit(solution)/shard_map/stack | solution.py:50
  55.1 0.3 convert_reduce_fusion
  55.4 1.6 %fusion.17 = bf16[256,3072]{1,0:T(8,128)(2,1)S(1)} fusion(f32[3072]{0:T(1024)S(1)} %broadcast_multiply_fusion, bf16[256,3328]{1,0:T(8,128)(2,1)S(1)} %bitcast.78, s32[3072]{0:T(1024)S(1)} %add_select_fusion, f32[256,256]{1,0:T(8,128)S(1)} %slice_convert_fusion), kind=kOutput, calls=%fused_computation.13 | convolution fusion | flops 607354880 | bytes 3563520 | tf_op jit(solution)/shard_map/dot_general | solution.py:92
  57.0 1.1 collective-permute-done.2
  58.1 1.7 %pad_maximum_fusion = bf16[4,4,256,256]{3,2,1,0:T(8,128)(2,1)S(1)} fusion(bf16[2,4,256,256]{3,2,1,0:T(8,128)(2,1)} %collective-permute-done.2, bf16[1,4,256,256]{3,2,1,0:T(8,128)(2,1)} %bitcast.10, bf16[1,4,256,256]{3,2,1,0:T(8,128)(2,1)} %bitcast.9), kind=kLoop, calls=%fused_computation.14 | loop fusion | flops 2097152 | bytes 4194304 | tf_op jit(solution)/shard_map/concatenate | solution.py:53
  59.8 7.8 %fusion.14 = bf16[256,3072]{1,0:T(8,128)(2,1)} fusion(bf16[16,256,256]{2,1,0:T(8,128)(2,1)S(1)} %bitcast.79, pred[16,3072]{1,0:T(8,128)(4,1)S(1)} %tile.9, bf16[256,3072]{1,0:T(8,128)(2,1)S(1)} %fusion.17, f32[3072]{0:T(1024)S(1)} %broadcast_multiply_fusion), kind=kOutput, calls=%fused_computation.12 | convolution fusion | flops 6457393152 | bytes 5304320 | tf_op jit(solution)/shard_map/rjk,rjx->kx/dot_general | solution.py:98
  67.6 28.1 %all-to-all-start.1 = ((bf16[8,32,3072]{2,1,0:T(8,128)(2,1)}), bf16[8,32,3072]{2,1,0:T(8,128)(2,1)S(1)}, u32[]{:S(2)}, u32[]{:S(2)}) async-start(bf16[8,32,3072]{2,1,0:T(8,128)(2,1)} %bitcast.80), calls=%async_computation.1 | async-start | bytes 3145728 | tf_op jit(solution)/shard_map/all_to_all | solution.py:102
  95.7 1.3 gather_fusion
  97.0 22.9 %all-to-all-done.1 = bf16[8,32,3072]{2,1,0:T(8,128)(2,1)S(1)} async-done(((bf16[8,32,3072]{2,1,0:T(8,128)(2,1)}), bf16[8,32,3072]{2,1,0:T(8,128)(2,1)S(1)}, u32[]{:S(2)}, u32[]{:S(2)}) %all-to-all-start.1) | async-done | bytes 1572896 | tf_op jit(solution)/shard_map/all_to_all | solution.py:102
  119.9 2.0 %copy.17 = bf16[8,32,3072]{2,0,1:T(8,128)(2,1)} copy(bf16[8,32,3072]{2,1,0:T(8,128)(2,1)S(1)} %all-to-all-done.1) | data formatting | bytes 3145728 | tf_op jit(solution)/shard_map/all_to_all | solution.py:102
  121.9 4.9 %reshape.131 = bf16[8,32,48,64]{3,2,0,1:T(8,128)(2,1)} reshape(bf16[8,32,3072]{2,0,1:T(8,128)(2,1)} %copy.17) | data formatting | bytes 3145728 | tf_op jit(solution)/shard_map/reshape | solution.py:103
  126.7 4.3 %convolution_bitcast_fusion.1 = bf16[32,48,512]{2,1,0:T(8,128)(2,1)} fusion(bf16[8,32,48,64]{3,2,0,1:T(8,128)(2,1)} %reshape.131, s32[8,64]{1,0:T(8,128)S(1)} %multiply_add_fusion, s32[512]{0:T(512)S(1)} %fusion.50), kind=kOutput, calls=%fused_computation.21 | convolution fusion | flops 805568512 | bytes 3149824 | tf_op jit(solution)/shard_map/dkti,cdi->ktc/dot_general | solution.py:104
  131.0 0.8 convolution_bitcast_fusion.2
  131.9 1.1 fusion.53
  (36 shorter events, 1.0 us)
Async XLA Ops:
  0.6 2.5 %copy-start = (bf16[32,48,512]{2,1,0:T(8,128)(2,1)S(1)}, bf16[32,48,512]{2,1,0:T(8,128)(2,1)}, u32[]{:S(2)}) copy-start(bf16[32,48,512]{2,1,0:T(8,128)(2,1)} %param.8) | copy-start | bytes 4718596
  6.5 4.0 %copy-start.2 = (f32[32,128]{1,0:T(8,128)S(1)}, f32[32,128]{1,0:T(8,128)}, u32[]{:S(2)}) copy-start(f32[32,128]{1,0:T(8,128)} %param.9) | copy-start | bytes 49156
  6.5 4.1 %copy-start.3 = (s32[512]{0:T(512)S(1)}, s32[512]{0:T(512)}, u32[]{:S(2)}) copy-start(s32[512]{0:T(512)} %param.11) | copy-start | bytes 6148
  13.6 41.4 %all-to-all-start = ((bf16[8,32,3328]{2,1,0:T(8,128)(2,1)}), bf16[8,32,3328]{2,1,0:T(8,128)(2,1)S(1)}, u32[]{:S(2)}, u32[]{:S(2)}) async-start(bf16[8,32,3328]{2,1,0:T(8,128)(2,1)} %concatenate.7), calls=%async_computation | async-start | bytes 3407872 | tf_op jit(solution)/shard_map/all_to_all | solution.py:85
  19.7 33.1 %collective-permute-start.1 = (bf16[4,256,256]{2,1,0:T(8,128)(2,1)}, bf16[4,256,256]{2,1,0:T(8,128)(2,1)}, u32[]{:S(2)}, u32[]{:S(2)}) collective-permute-start(bf16[4,256,256]{2,1,0:T(8,128)(2,1)} %param.10), channel_id=1, source_target_pairs={{8,0},{9,1},{10,2},{11,3},{12,4},{13,5},{14,6},{15,7},{16,8},{17,9... | collective-permute-start | bytes 1572872 | tf_op jit(solution)/shard_map/ppermute | solution.py:49
  19.7 33.1 %collective-permute-start = (bf16[4,256,256]{2,1,0:T(8,128)(2,1)}, bf16[4,256,256]{2,1,0:T(8,128)(2,1)}, u32[]{:S(2)}, u32[]{:S(2)}) collective-permute-start(bf16[4,256,256]{2,1,0:T(8,128)(2,1)} %param.10), channel_id=1, source_target_pairs={{0,0},{1,1},{2,2},{3,3},{4,4},{5,5},{6,6},{7,7},{8,8},{9,9},{10,10... | collective-permute-start | bytes 1572872 | tf_op jit(solution)/shard_map/ppermute | solution.py:49
  55.1 3.0 %collective-permute-start.2 = (bf16[2,4,256,256]{3,2,1,0:T(8,128)(2,1)}, bf16[2,4,256,256]{3,2,1,0:T(8,128)(2,1)}, u32[]{:S(2)}, u32[]{:S(2)}) collective-permute-start(bf16[2,4,256,256]{3,2,1,0:T(8,128)(2,1)} %pad_maximum_fusion.1), channel_id=1, source_target_pairs={{0,1},{1,0},{2,3},{3,2},{4,5},{5,4},{6,7},{7,6},{8,9},{9,8},{10,11... | collective-permute-start | bytes 3145736 | tf_op jit(solution)/shard_map/ppermute | solution.py:52
  67.6 28.1 %copy-start.4 = (s32[128]{0:T(128)S(1)}, s32[128]{0:T(128)}, u32[]{:S(2)}) copy-start(s32[128]{0:T(128)} %param.13) | copy-start | bytes 1540
  67.6 52.3 %all-to-all-start.1 = ((bf16[8,32,3072]{2,1,0:T(8,128)(2,1)}), bf16[8,32,3072]{2,1,0:T(8,128)(2,1)S(1)}, u32[]{:S(2)}, u32[]{:S(2)}) async-start(bf16[8,32,3072]{2,1,0:T(8,128)(2,1)} %bitcast.80), calls=%async_computation.1 | async-start | bytes 3145728 | tf_op jit(solution)/shard_map/all_to_all | solution.py:102
  126.7 4.3 %copy-start.1 = (bf16[8,32,48,64]{3,2,0,1:T(8,128)(2,1)S(1)}, bf16[8,32,48,64]{3,2,0,1:T(8,128)(2,1)}, u32[]{:S(2)}) copy-start(bf16[8,32,48,64]{3,2,0,1:T(8,128)(2,1)} %reshape.131) | copy-start | bytes 4718596
  131.0 0.8 copy-start.5

commit v7 on v6

--- a/solution.py
+++ b/solution.py
@@ -33,19 +33,23 @@
     ring = n_chip // 2
     pairs = [(0, ring // 2)] + [(b, ring - b) for b in range(1, ring // 2)]
     pairs = pairs + [(a + ring, b + ring) for a, b in pairs]
-    owner_of = [0] * n_chip
-    slot_of = [0] * n_chip
-    for m, pair in enumerate(pairs):
-        for a, off in enumerate(pair):
-            owner_of[off] = m
-            slot_of[off] = a
+    pairs_of = [pairs, [pairs[m ^ 2] for m in range(n_member)]]
+    owner_of = [[0] * n_chip for _ in range(2)]
+    slot_of = [[0] * n_chip for _ in range(2)]
+    for par in range(2):
+        for m, pair in enumerate(pairs_of[par]):
+            for a, off in enumerate(pair):
+                owner_of[par][off] = m
+                slot_of[par][off] = a
     own = []
     for a in range(chips_per_dev):
         perm = []
         for m in range(n_member):
             for s in range(n_space):
-                src = 2 * ((s // 2 + pairs[m][a]) % n_chip) + s % 2
+                p = s // 2
+                src = 2 * ((p + pairs_of[p % 2][m][a]) % n_chip) + s % 2
                 perm.append((m * n_space + src, m * n_space + s))
+        assert len({src for src, _ in perm}) == len(perm)
         own.append(lax.ppermute(weights, ("member", "space"), perm))
     own = jnp.stack(own)
     sib_perm = [(m * n_space + s, m * n_space + (s ^ 1)) for m in range(n_member) for s in range(n_space)]
@@ -54,8 +58,9 @@
 
     group = region_ids // reg_count
     offset = (group // 2 - chip) % n_chip
-    dest = jnp.array(owner_of, jnp.int32)[offset]
-    slot = (group % 2 != core).astype(jnp.int32) * chips_per_dev + jnp.array(slot_of, jnp.int32)[offset]
+    par = chip % 2
+    dest = jnp.array(owner_of, jnp.int32)[par, offset]
+    slot = (group % 2 != core).astype(jnp.int32) * chips_per_dev + jnp.array(slot_of, jnp.int32)[par, offset]
     group_hot = (group[:, None] == jnp.arange(n_space, dtype=jnp.int32)[None, :]).astype(jnp.int32)
     before = jnp.cumsum(group_hot, axis=0) - group_hot
     rank_in = jnp.sum(before * group_hot, axis=1)

time: 134 us -> 133 us (level)
  the two profiles are of different devices: /device:TPU:136 before, /device:TPU:1 now
where the time goes in v7:
time: 133 us; the launch traced here: 131 us
  waiting for transfers between devices  44.7 us (34%)
  starting transfers between devices  34.8 us (26%)
  local copies, waits for them, and re-layouts  24.3 us (18%)
  matrix products  20.1 us (15%)
  other arithmetic  6.68 us (5%)
    all_to_all x1, waiting for transfers between devices, local(): lax.all_to_all(result, 'member', split_axis=0, concat_axis=0, tiled=True)  22.1 us
    ppermute x2, waiting for transfers between devices, local(): own.append(lax.ppermute(weights, ('member', 'space'), perm))  21.9 us
    ppermute x2, starting transfers between devices, local(): own.append(lax.ppermute(weights, ('member', 'space'), perm))  12.4 us
    all_to_all x1, starting transfers between devices, local(): lax.all_to_all(result, 'member', split_axis=0, concat_axis=0, tiled=True)  8.26 us
    dot_general x1, matrix products, local(): jnp.einsum('rjk,rjx->kx', w_all, masked, preferred_element_type=jnp.float32)  7.81 us
    all_to_all x1, starting transfers between devices, local(): lax.all_to_all(payload, 'member', split_axis=0, concat_axis=0, tiled=True)  7.48 us
    ppermute x1, starting transfers between devices, local(): sib = lax.ppermute(own, ('member', 'space'), sib_perm)  6.69 us
    gather x1, local copies, waits for them, and re-layouts, local(): dest = jnp.array(owner_of, jnp.int32)[par, offset]  4.88 us
  transfers between devices with their start and end apart: 5, of which 3 were waited for; matrix products, arithmetic and copies ran while one was open for 5% of the time, Pallas kernels for 0%

profile of v7, /device:TPU:1, one launch (start us, length us, event | category | flops | bytes accessed | tf_op | source)
XLA Modules:
  0.0 131.5 jit_solution(13507507635736058446)
XLA Ops:
  0.7 0.8 fusion.51
  1.5 1.2 reduce-window.6
  3.1 4.9 %gather_fusion = s32[512]{0:T(512)S(1)} fusion(s32[2,16]{1,0:T(2,128)} %constant.145.clone, s32[512]{0:T(512)S(1)} %get-tuple-element.2), kind=kCustom, calls=%fused_computation | custom fusion | bytes 8192 | tf_op jit(solution)/shard_map/gather | solution.py:62
  8.0 4.7 %gather_fusion.1 = s32[512]{0:T(512)S(1)} fusion(s32[2,16]{1,0:T(2,128)S(1)} %copy-done.1, s32[512]{0:T(512)S(1)} %get-tuple-element.2), kind=kCustom, calls=%fused_computation.1 | custom fusion | bytes 8192 | tf_op jit(solution)/shard_map/gather | solution.py:63
  12.8 3.4 %convolution_bitcast_fusion = bf16[8,32,48,64]{3,2,1,0:T(8,128)(2,1)} fusion(bf16[32,48,512]{2,1,0:T(8,128)(2,1)S(1)} %copy-done, s32[8,64]{1,0:T(8,128)S(1)} %multiply_add_fusion, s32[512]{0:T(512)S(1)} %get-tuple-element.7), kind=kOutput, calls=%fused_computation.17 | convolution fusion | flops 805568512 | bytes 3149824 | tf_op jit(solution)/shard_map/jtc,cdi->djti/dot_general | solution.py:83
  16.1 4.0 %reshape.126 = bf16[8,32,3072]{2,1,0:T(8,128)(2,1)S(1)} reshape(bf16[8,32,48,64]{3,2,1,0:T(8,128)(2,1)} %convolution_bitcast_fusion) | data formatting | bytes 3145728 | tf_op jit(solution)/shard_map/reshape | solution.py:84
  20.4 0.9 fusion.33
  21.3 2.0 %concatenate.12 = bf16[8,32,3328]{2,1,0:T(8,128)(2,1)} concatenate(bf16[8,32,3072]{2,1,0:T(8,128)(2,1)S(1)} %reshape.126, bf16[8,32,64]{2,1,0:T(8,128)(2,1)S(1)} %get-tuple-element.6, bf16[8,32,64]{2,1,0:T(8,128)(2,1)S(1)} %get-tuple-element.5, bf16[8,32,64]{2,1,0:T(8,128)(2,1)S(1)} %get-tuple-element.4, bf16[8,32,64]{2,1,0:T(8,128)(2,1)S(1)} %broadcast_in_dim.45), dimensions={2} | concatenate | bytes 3407872 | tf_op jit(solution)/shard_map/concatenate | solution.py:88
  23.3 7.5 %all-to-all-start = ((bf16[8,32,3328]{2,1,0:T(8,128)(2,1)}), bf16[8,32,3328]{2,1,0:T(8,128)(2,1)S(1)}, u32[]{:S(2)}, u32[]{:S(2)}) async-start(bf16[8,32,3328]{2,1,0:T(8,128)(2,1)} %concatenate.12), calls=%async_computation | async-start | bytes 3407872 | tf_op jit(solution)/shard_map/all_to_all | solution.py:90
  30.8 7.0 %collective-permute-start.1 = (bf16[4,256,256]{2,1,0:T(8,128)(2,1)}, bf16[4,256,256]{2,1,0:T(8,128)(2,1)}, u32[]{:S(2)}, u32[]{:S(2)}) collective-permute-start(bf16[4,256,256]{2,1,0:T(8,128)(2,1)} %param.10), channel_id=1, source_target_pairs={{8,0},{9,1},{14,2},{15,3},{12,4},{13,5},{18,6},{19,7},{16,8},{17,9... | collective-permute-start | bytes 1572872 | tf_op jit(solution)/shard_map/ppermute | solution.py:53
  37.8 5.3 %collective-permute-start = (bf16[4,256,256]{2,1,0:T(8,128)(2,1)}, bf16[4,256,256]{2,1,0:T(8,128)(2,1)}, u32[]{:S(2)}, u32[]{:S(2)}) collective-permute-start(bf16[4,256,256]{2,1,0:T(8,128)(2,1)} %param.10), channel_id=1, source_target_pairs={{0,0},{1,1},{6,2},{7,3},{4,4},{5,5},{10,6},{11,7},{8,8},{9,9},{14,... | collective-permute-start | bytes 1572872 | tf_op jit(solution)/shard_map/ppermute | solution.py:53
  43.7 21.9 %collective-permute-done.1 = bf16[4,256,256]{2,1,0:T(8,128)(2,1)} collective-permute-done((bf16[4,256,256]{2,1,0:T(8,128)(2,1)}, bf16[4,256,256]{2,1,0:T(8,128)(2,1)}, u32[]{:S(2)}, u32[]{:S(2)}) %collective-permute-start.1) | collective-permute-done | bytes 524320 | tf_op jit(solution)/shard_map/ppermute | solution.py:53
  65.5 2.3 %pad_maximum_fusion.1 = bf16[2,4,256,256]{3,2,1,0:T(8,128)(2,1)} fusion(bf16[1,4,256,256]{3,2,1,0:T(8,128)(2,1)} %bitcast.10, bf16[1,4,256,256]{3,2,1,0:T(8,128)(2,1)} %bitcast.9), kind=kLoop, calls=%fused_computation.27 | loop fusion | flops 524288 | bytes 2097152 | tf_op jit(solution)/shard_map/stack | solution.py:54
  67.8 6.7 %collective-permute-start.2 = (bf16[2,4,256,256]{3,2,1,0:T(8,128)(2,1)}, bf16[2,4,256,256]{3,2,1,0:T(8,128)(2,1)}, u32[]{:S(2)}, u32[]{:S(2)}) collective-permute-start(bf16[2,4,256,256]{3,2,1,0:T(8,128)(2,1)} %pad_maximum_fusion.1), channel_id=1, source_target_pairs={{0,1},{1,0},{2,3},{3,2},{4,5},{5,4},{6,7},{7,6},{8,9},{9,8},{10,11... | collective-permute-start | bytes 3145736 | tf_op jit(solution)/shard_map/ppermute | solution.py:56
  74.8 1.6 %fusion.17 = bf16[256,3072]{1,0:T(8,128)(2,1)S(1)} fusion(f32[3072]{0:T(1024)S(1)} %broadcast_multiply_fusion, bf16[256,3328]{1,0:T(8,128)(2,1)S(1)} %bitcast.78, s32[3072]{0:T(1024)S(1)} %add_select_fusion, f32[256,256]{1,0:T(8,128)S(1)} %slice_convert_fusion), kind=kOutput, calls=%fused_computation.15 | convolution fusion | flops 607354880 | bytes 3563520 | tf_op jit(solution)/shard_map/dot_general | solution.py:97
  77.1 1.7 %pad_maximum_fusion = bf16[4,4,256,256]{3,2,1,0:T(8,128)(2,1)S(1)} fusion(bf16[2,4,256,256]{3,2,1,0:T(8,128)(2,1)} %collective-permute-done.2, bf16[1,4,256,256]{3,2,1,0:T(8,128)(2,1)} %bitcast.10, bf16[1,4,256,256]{3,2,1,0:T(8,128)(2,1)} %bitcast.9), kind=kLoop, calls=%fused_computation.16 | loop fusion | flops 2097152 | bytes 4194304 | tf_op jit(solution)/shard_map/concatenate | solution.py:57
  78.9 7.8 %fusion.14 = bf16[256,3072]{1,0:T(8,128)(2,1)} fusion(bf16[16,256,256]{2,1,0:T(8,128)(2,1)S(1)} %bitcast.79, pred[16,3072]{1,0:T(8,128)(4,1)S(1)} %tile.9, bf16[256,3072]{1,0:T(8,128)(2,1)S(1)} %fusion.17, f32[3072]{0:T(1024)S(1)} %broadcast_multiply_fusion), kind=kOutput, calls=%fused_computation.14 | convolution fusion | flops 6457393152 | bytes 5304320 | tf_op jit(solution)/shard_map/rjk,rjx->kx/dot_general | solution.py:103
  86.7 8.3 %all-to-all-start.1 = ((bf16[8,32,3072]{2,1,0:T(8,128)(2,1)}), bf16[8,32,3072]{2,1,0:T(8,128)(2,1)S(1)}, u32[]{:S(2)}, u32[]{:S(2)}) async-start(bf16[8,32,3072]{2,1,0:T(8,128)(2,1)} %bitcast.80), calls=%async_computation.1 | async-start | bytes 3145728 | tf_op jit(solution)/shard_map/all_to_all | solution.py:107
  95.0 1.3 gather_fusion.2
  96.2 22.1 %all-to-all-done.1 = bf16[8,32,3072]{2,1,0:T(8,128)(2,1)S(1)} async-done(((bf16[8,32,3072]{2,1,0:T(8,128)(2,1)}), bf16[8,32,3072]{2,1,0:T(8,128)(2,1)S(1)}, u32[]{:S(2)}, u32[]{:S(2)}) %all-to-all-start.1) | async-done | bytes 1572896 | tf_op jit(solution)/shard_map/all_to_all | solution.py:107
  118.3 2.0 %copy.17 = bf16[8,32,3072]{2,0,1:T(8,128)(2,1)} copy(bf16[8,32,3072]{2,1,0:T(8,128)(2,1)S(1)} %all-to-all-done.1) | data formatting | bytes 3145728 | tf_op jit(solution)/shard_map/all_to_all | solution.py:107
  120.3 4.9 %reshape.131 = bf16[8,32,48,64]{3,2,0,1:T(8,128)(2,1)} reshape(bf16[8,32,3072]{2,0,1:T(8,128)(2,1)} %copy.17) | data formatting | bytes 3145728 | tf_op jit(solution)/shard_map/reshape | solution.py:108
  125.2 4.3 %convolution_bitcast_fusion.1 = bf16[32,48,512]{2,1,0:T(8,128)(2,1)} fusion(bf16[8,32,48,64]{3,2,0,1:T(8,128)(2,1)} %reshape.131, s32[8,64]{1,0:T(8,128)S(1)} %multiply_add_fusion, s32[512]{0:T(512)S(1)} %get-tuple-element.7), kind=kOutput, calls=%fused_computation.23 | convolution fusion | flops 805568512 | bytes 3149824 | tf_op jit(solution)/shard_map/dkti,cdi->ktc/dot_general | solution.py:109
  130.3 1.1 fusion.54
  (40 shorter events, 3.0 us)
Async XLA Ops:
  0.6 12.2 %copy-start = (bf16[32,48,512]{2,1,0:T(8,128)(2,1)S(1)}, bf16[32,48,512]{2,1,0:T(8,128)(2,1)}, u32[]{:S(2)}) copy-start(bf16[32,48,512]{2,1,0:T(8,128)(2,1)} %param.8) | copy-start | bytes 4718596
  0.6 7.3 %copy-start.1 = (s32[2,16]{1,0:T(2,128)S(1)}, s32[2,16]{1,0:T(2,128)}, u32[]{:S(2)}) copy-start(s32[2,16]{1,0:T(2,128)} %constant.146.clone) | copy-start | bytes 388
  3.1 9.7 %copy-start.3 = (s32[512]{0:T(512)S(1)}, s32[512]{0:T(512)}, u32[]{:S(2)}) copy-start(s32[512]{0:T(512)} %param.11) | copy-start | bytes 6148
  16.1 4.0 %copy-start.4 = (f32[32,128]{1,0:T(8,128)S(1)}, f32[32,128]{1,0:T(8,128)}, u32[]{:S(2)}) copy-start(f32[32,128]{1,0:T(8,128)} %param.9) | copy-start | bytes 49156
  23.3 51.2 %all-to-all-start = ((bf16[8,32,3328]{2,1,0:T(8,128)(2,1)}), bf16[8,32,3328]{2,1,0:T(8,128)(2,1)S(1)}, u32[]{:S(2)}, u32[]{:S(2)}) async-start(bf16[8,32,3328]{2,1,0:T(8,128)(2,1)} %concatenate.12), calls=%async_computation | async-start | bytes 3407872 | tf_op jit(solution)/shard_map/all_to_all | solution.py:90
  30.8 34.8 %collective-permute-start.1 = (bf16[4,256,256]{2,1,0:T(8,128)(2,1)}, bf16[4,256,256]{2,1,0:T(8,128)(2,1)}, u32[]{:S(2)}, u32[]{:S(2)}) collective-permute-start(bf16[4,256,256]{2,1,0:T(8,128)(2,1)} %param.10), channel_id=1, source_target_pairs={{8,0},{9,1},{14,2},{15,3},{12,4},{13,5},{18,6},{19,7},{16,8},{17,9... | collective-permute-start | bytes 1572872 | tf_op jit(solution)/shard_map/ppermute | solution.py:53
  37.8 27.8 %collective-permute-start = (bf16[4,256,256]{2,1,0:T(8,128)(2,1)}, bf16[4,256,256]{2,1,0:T(8,128)(2,1)}, u32[]{:S(2)}, u32[]{:S(2)}) collective-permute-start(bf16[4,256,256]{2,1,0:T(8,128)(2,1)} %param.10), channel_id=1, source_target_pairs={{0,0},{1,1},{6,2},{7,3},{4,4},{5,5},{10,6},{11,7},{8,8},{9,9},{14,... | collective-permute-start | bytes 1572872 | tf_op jit(solution)/shard_map/ppermute | solution.py:53
  67.8 9.3 %collective-permute-start.2 = (bf16[2,4,256,256]{3,2,1,0:T(8,128)(2,1)}, bf16[2,4,256,256]{3,2,1,0:T(8,128)(2,1)}, u32[]{:S(2)}, u32[]{:S(2)}) collective-permute-start(bf16[2,4,256,256]{3,2,1,0:T(8,128)(2,1)} %pad_maximum_fusion.1), channel_id=1, source_target_pairs={{0,1},{1,0},{2,3},{3,2},{4,5},{5,4},{6,7},{7,6},{8,9},{9,8},{10,11... | collective-permute-start | bytes 3145736 | tf_op jit(solution)/shard_map/ppermute | solution.py:56
  86.7 8.3 %copy-start.5 = (s32[128]{0:T(128)S(1)}, s32[128]{0:T(128)}, u32[]{:S(2)}) copy-start(s32[128]{0:T(128)} %param.13) | copy-start | bytes 1540
  86.7 31.7 %all-to-all-start.1 = ((bf16[8,32,3072]{2,1,0:T(8,128)(2,1)}), bf16[8,32,3072]{2,1,0:T(8,128)(2,1)S(1)}, u32[]{:S(2)}, u32[]{:S(2)}) async-start(bf16[8,32,3072]{2,1,0:T(8,128)(2,1)} %bitcast.80), calls=%async_computation.1 | async-start | bytes 3145728 | tf_op jit(solution)/shard_map/all_to_all | solution.py:107
  125.2 4.3 %copy-start.2 = (bf16[8,32,48,64]{3,2,0,1:T(8,128)(2,1)S(1)}, bf16[8,32,48,64]{3,2,0,1:T(8,128)(2,1)}, u32[]{:S(2)}) copy-start(bf16[8,32,48,64]{3,2,0,1:T(8,128)(2,1)} %reshape.131) | copy-start | bytes 4718596
  129.5 0.8 copy-start.6

commit v8 on v7

--- a/solution.py
+++ b/solution.py
@@ -1,4 +1,5 @@
 import jax
+import numpy as np
 import jax.numpy as jnp
 from jax import lax
 from jax.sharding import PartitionSpec as P
@@ -59,8 +60,19 @@
     group = region_ids // reg_count
     offset = (group // 2 - chip) % n_chip
     par = chip % 2
-    dest = jnp.array(owner_of, jnp.int32)[par, offset]
-    slot = (group % 2 != core).astype(jnp.int32) * chips_per_dev + jnp.array(slot_of, jnp.int32)[par, offset]
+    half_ring = ring // 2
+
+    def owner_slot(o, p, xp):
+        r = o % ring
+        base = xp.where(r == half_ring, 0, xp.where(r < half_ring, r, ring - r))
+        return xp.bitwise_xor(base + half_ring * (o // ring), 2 * p), (r >= half_ring).astype(xp.int32)
+
+    for p_ in range(2):
+        o_ = np.arange(n_chip)
+        m_, a_ = owner_slot(o_, p_, np)
+        assert list(m_) == owner_of[p_] and list(a_) == slot_of[p_]
+    dest, slot_a = owner_slot(offset, par, jnp)
+    slot = (group % 2 != core).astype(jnp.int32) * chips_per_dev + slot_a
     group_hot = (group[:, None] == jnp.arange(n_space, dtype=jnp.int32)[None, :]).astype(jnp.int32)
     before = jnp.cumsum(group_hot, axis=0) - group_hot
     rank_in = jnp.sum(before * group_hot, axis=1)

time: 133 us -> 125 us (0.940)
  local copies, waits for them, and re-layouts: 24.3 us -> 14.7 us
  other arithmetic: 6.68 us -> 8.08 us
    gather x2 -> x0, local copies, waits for them, and re-layouts: 9.63 us -> none  [the longest x1 4.88 us: local(): dest = jnp.array(owner_of, jnp.int32)[par, offset]]
where the time goes in v8:
time: 125 us; the launch traced here: 123 us
  waiting for transfers between devices  44.8 us (36%)
  starting transfers between devices  34.8 us (28%)
  matrix products  20.1 us (16%)
  local copies, waits for them, and re-layouts  14.7 us (12%)
  other arithmetic  8.08 us (6%)
    all_to_all x1, waiting for transfers between devices, local(): lax.all_to_all(result, 'member', split_axis=0, concat_axis=0, tiled=True)  22.1 us
    ppermute x2, waiting for transfers between devices, local(): own.append(lax.ppermute(weights, ('member', 'space'), perm))  22 us
    ppermute x2, starting transfers between devices, local(): own.append(lax.ppermute(weights, ('member', 'space'), perm))  12.4 us
    all_to_all x1, starting transfers between devices, local(): lax.all_to_all(result, 'member', split_axis=0, concat_axis=0, tiled=True)  8.4 us
    dot_general x1, matrix products, local(): jnp.einsum('rjk,rjx->kx', w_all, masked, preferred_element_type=jnp.float32)  7.82 us
    all_to_all x1, starting transfers between devices, local(): lax.all_to_all(payload, 'member', split_axis=0, concat_axis=0, tiled=True)  7.48 us
    ppermute x1, starting transfers between devices, local(): sib = lax.ppermute(own, ('member', 'space'), sib_perm)  6.6 us
    reshape x1, local copies, waits for them, and re-layouts, local(): returned = returned.reshape(n_member, local_members, tracers, own_cols)  4.86 us
  transfers between devices with their start and end apart: 5, of which 3 were waited for; matrix products, arithmetic and copies ran while one was open for 5% of the time, Pallas kernels for 0%

profile of v8, /device:TPU:1, one launch (start us, length us, event | category | flops | bytes accessed | tf_op | source)
XLA Modules:
  0.0 123.3 jit_solution(10495518857534026271)
XLA Ops:
  0.7 0.8 fusion.68
  2.2 1.2 reduce-window.6
  4.5 3.4 %convolution_bitcast_fusion = bf16[8,32,48,64]{3,2,1,0:T(8,128)(2,1)} fusion(bf16[32,48,512]{2,1,0:T(8,128)(2,1)S(1)} %copy-done, s32[8,64]{1,0:T(8,128)S(1)} %multiply_add_fusion, s32[512]{0:T(512)S(1)} %get-tuple-element.2), kind=kOutput, calls=%fused_computation.15 | convolution fusion | flops 805568512 | bytes 3149824 | tf_op jit(solution)/shard_map/jtc,cdi->djti/dot_general | solution.py:95
  7.8 4.0 %reshape.126 = bf16[8,32,3072]{2,1,0:T(8,128)(2,1)S(1)} reshape(bf16[8,32,48,64]{3,2,1,0:T(8,128)(2,1)} %convolution_bitcast_fusion) | data formatting | bytes 3145728 | tf_op jit(solution)/shard_map/reshape | solution.py:96
  12.1 0.9 fusion.33
  13.0 2.0 %concatenate.7 = bf16[8,32,3328]{2,1,0:T(8,128)(2,1)} concatenate(bf16[8,32,3072]{2,1,0:T(8,128)(2,1)S(1)} %reshape.126, bf16[8,32,64]{2,1,0:T(8,128)(2,1)S(1)} %get-tuple-element.6, bf16[8,32,64]{2,1,0:T(8,128)(2,1)S(1)} %get-tuple-element.5, bf16[8,32,64]{2,1,0:T(8,128)(2,1)S(1)} %get-tuple-element.4, bf16[8,32,64]{2,1,0:T(8,128)(2,1)S(1)} %broadcast_in_dim.44), dimensions={2} | concatenate | bytes 3407872 | tf_op jit(solution)/shard_map/concatenate | solution.py:100
  15.0 7.5 %all-to-all-start = ((bf16[8,32,3328]{2,1,0:T(8,128)(2,1)}), bf16[8,32,3328]{2,1,0:T(8,128)(2,1)S(1)}, u32[]{:S(2)}, u32[]{:S(2)}) async-start(bf16[8,32,3328]{2,1,0:T(8,128)(2,1)} %concatenate.7), calls=%async_computation | async-start | bytes 3407872 | tf_op jit(solution)/shard_map/all_to_all | solution.py:102
  22.5 7.0 %collective-permute-start.1 = (bf16[4,256,256]{2,1,0:T(8,128)(2,1)}, bf16[4,256,256]{2,1,0:T(8,128)(2,1)}, u32[]{:S(2)}, u32[]{:S(2)}) collective-permute-start(bf16[4,256,256]{2,1,0:T(8,128)(2,1)} %param.8), channel_id=1, source_target_pairs={{8,0},{9,1},{14,2},{15,3},{12,4},{13,5},{18,6},{19,7},{16,8},{17,9... | collective-permute-start | bytes 1572872 | tf_op jit(solution)/shard_map/ppermute | solution.py:54
  29.5 5.3 %collective-permute-start = (bf16[4,256,256]{2,1,0:T(8,128)(2,1)}, bf16[4,256,256]{2,1,0:T(8,128)(2,1)}, u32[]{:S(2)}, u32[]{:S(2)}) collective-permute-start(bf16[4,256,256]{2,1,0:T(8,128)(2,1)} %param.8), channel_id=1, source_target_pairs={{0,0},{1,1},{6,2},{7,3},{4,4},{5,5},{10,6},{11,7},{8,8},{9,9},{14,... | collective-permute-start | bytes 1572872 | tf_op jit(solution)/shard_map/ppermute | solution.py:54
  35.4 22.0 %collective-permute-done.1 = bf16[4,256,256]{2,1,0:T(8,128)(2,1)} collective-permute-done((bf16[4,256,256]{2,1,0:T(8,128)(2,1)}, bf16[4,256,256]{2,1,0:T(8,128)(2,1)}, u32[]{:S(2)}, u32[]{:S(2)}) %collective-permute-start.1) | collective-permute-done | bytes 524320 | tf_op jit(solution)/shard_map/ppermute | solution.py:54
  57.4 2.3 %pad_maximum_fusion.1 = bf16[2,4,256,256]{3,2,1,0:T(8,128)(2,1)} fusion(bf16[1,4,256,256]{3,2,1,0:T(8,128)(2,1)} %bitcast.10, bf16[1,4,256,256]{3,2,1,0:T(8,128)(2,1)} %bitcast.9), kind=kLoop, calls=%fused_computation.25 | loop fusion | flops 524288 | bytes 2097152 | tf_op jit(solution)/shard_map/stack | solution.py:55
  59.6 6.6 %collective-permute-start.2 = (bf16[2,4,256,256]{3,2,1,0:T(8,128)(2,1)}, bf16[2,4,256,256]{3,2,1,0:T(8,128)(2,1)}, u32[]{:S(2)}, u32[]{:S(2)}) collective-permute-start(bf16[2,4,256,256]{3,2,1,0:T(8,128)(2,1)} %pad_maximum_fusion.1), channel_id=1, source_target_pairs={{0,1},{1,0},{2,3},{3,2},{4,5},{5,4},{6,7},{7,6},{8,9},{9,8},{10,11... | collective-permute-start | bytes 3145736 | tf_op jit(solution)/shard_map/ppermute | solution.py:57
  66.5 1.6 %fusion.17 = bf16[256,3072]{1,0:T(8,128)(2,1)S(1)} fusion(f32[3072]{0:T(1024)S(1)} %broadcast_multiply_fusion, bf16[256,3328]{1,0:T(8,128)(2,1)S(1)} %bitcast.79, s32[3072]{0:T(1024)S(1)} %add_select_fusion, f32[256,256]{1,0:T(8,128)S(1)} %slice_convert_fusion), kind=kOutput, calls=%fused_computation.13 | convolution fusion | flops 607354880 | bytes 3563520 | tf_op jit(solution)/shard_map/dot_general | solution.py:109
  68.1 0.7 collective-permute-done.2
  68.9 1.7 %pad_maximum_fusion = bf16[4,4,256,256]{3,2,1,0:T(8,128)(2,1)S(1)} fusion(bf16[2,4,256,256]{3,2,1,0:T(8,128)(2,1)} %collective-permute-done.2, bf16[1,4,256,256]{3,2,1,0:T(8,128)(2,1)} %bitcast.10, bf16[1,4,256,256]{3,2,1,0:T(8,128)(2,1)} %bitcast.9), kind=kLoop, calls=%fused_computation.14 | loop fusion | flops 2097152 | bytes 4194304 | tf_op jit(solution)/shard_map/concatenate | solution.py:58
  70.6 7.8 %fusion.14 = bf16[256,3072]{1,0:T(8,128)(2,1)} fusion(bf16[16,256,256]{2,1,0:T(8,128)(2,1)S(1)} %bitcast.80, pred[16,3072]{1,0:T(8,128)(4,1)S(1)} %tile.9, bf16[256,3072]{1,0:T(8,128)(2,1)S(1)} %fusion.17, f32[3072]{0:T(1024)S(1)} %broadcast_multiply_fusion), kind=kOutput, calls=%fused_computation.12 | convolution fusion | flops 6457393152 | bytes 5304320 | tf_op jit(solution)/shard_map/rjk,rjx->kx/dot_general | solution.py:115
  78.4 8.4 %all-to-all-start.1 = ((bf16[8,32,3072]{2,1,0:T(8,128)(2,1)}), bf16[8,32,3072]{2,1,0:T(8,128)(2,1)S(1)}, u32[]{:S(2)}, u32[]{:S(2)}) async-start(bf16[8,32,3072]{2,1,0:T(8,128)(2,1)} %bitcast.81), calls=%async_computation.1 | async-start | bytes 3145728 | tf_op jit(solution)/shard_map/all_to_all | solution.py:119
  86.8 1.3 %gather_fusion = s32[128]{0:T(128)S(1)} fusion(s32[512]{0:T(512)S(1)} %get-tuple-element.2, s32[1024]{0:T(1024)S(1)} %pad_clamp_fusion), kind=kCustom, calls=%fused_computation | custom fusion | bytes 1536 | tf_op jit(solution)/shard_map/jit(_take)/gather | solution.py:124
  88.1 22.1 %all-to-all-done.1 = bf16[8,32,3072]{2,1,0:T(8,128)(2,1)S(1)} async-done(((bf16[8,32,3072]{2,1,0:T(8,128)(2,1)}), bf16[8,32,3072]{2,1,0:T(8,128)(2,1)S(1)}, u32[]{:S(2)}, u32[]{:S(2)}) %all-to-all-start.1) | async-done | bytes 1572896 | tf_op jit(solution)/shard_map/all_to_all | solution.py:119
  110.2 2.0 %copy.15 = bf16[8,32,3072]{2,0,1:T(8,128)(2,1)} copy(bf16[8,32,3072]{2,1,0:T(8,128)(2,1)S(1)} %all-to-all-done.1) | data formatting | bytes 3145728 | tf_op jit(solution)/shard_map/all_to_all | solution.py:119
  112.2 4.9 %reshape.131 = bf16[8,32,48,64]{3,2,0,1:T(8,128)(2,1)} reshape(bf16[8,32,3072]{2,0,1:T(8,128)(2,1)} %copy.15) | data formatting | bytes 3145728 | tf_op jit(solution)/shard_map/reshape | solution.py:120
  117.1 4.3 %convolution_bitcast_fusion.1 = bf16[32,48,512]{2,1,0:T(8,128)(2,1)} fusion(bf16[8,32,48,64]{3,2,0,1:T(8,128)(2,1)} %reshape.131, s32[8,64]{1,0:T(8,128)S(1)} %multiply_add_fusion, s32[512]{0:T(512)S(1)} %get-tuple-element.2), kind=kOutput, calls=%fused_computation.21 | convolution fusion | flops 805568512 | bytes 3149824 | tf_op jit(solution)/shard_map/dkti,cdi->ktc/dot_general | solution.py:121
  121.4 0.8 convolution_bitcast_fusion.2
  122.2 1.1 fusion.59
  (38 shorter events, 2.9 us)
Async XLA Ops:
  0.6 3.8 %copy-start = (bf16[32,48,512]{2,1,0:T(8,128)(2,1)S(1)}, bf16[32,48,512]{2,1,0:T(8,128)(2,1)}, u32[]{:S(2)}) copy-start(bf16[32,48,512]{2,1,0:T(8,128)(2,1)} %param.6) | copy-start | bytes 4718596
  7.8 4.0 %copy-start.2 = (s32[512]{0:T(512)S(1)}, s32[512]{0:T(512)}, u32[]{:S(2)}) copy-start(s32[512]{0:T(512)} %param.9) | copy-start | bytes 6148
  7.8 4.1 %copy-start.3 = (f32[32,128]{1,0:T(8,128)S(1)}, f32[32,128]{1,0:T(8,128)}, u32[]{:S(2)}) copy-start(f32[32,128]{1,0:T(8,128)} %param.7) | copy-start | bytes 49156
  15.0 51.3 %all-to-all-start = ((bf16[8,32,3328]{2,1,0:T(8,128)(2,1)}), bf16[8,32,3328]{2,1,0:T(8,128)(2,1)S(1)}, u32[]{:S(2)}, u32[]{:S(2)}) async-start(bf16[8,32,3328]{2,1,0:T(8,128)(2,1)} %concatenate.7), calls=%async_computation | async-start | bytes 3407872 | tf_op jit(solution)/shard_map/all_to_all | solution.py:102
  22.5 34.9 %collective-permute-start.1 = (bf16[4,256,256]{2,1,0:T(8,128)(2,1)}, bf16[4,256,256]{2,1,0:T(8,128)(2,1)}, u32[]{:S(2)}, u32[]{:S(2)}) collective-permute-start(bf16[4,256,256]{2,1,0:T(8,128)(2,1)} %param.8), channel_id=1, source_target_pairs={{8,0},{9,1},{14,2},{15,3},{12,4},{13,5},{18,6},{19,7},{16,8},{17,9... | collective-permute-start | bytes 1572872 | tf_op jit(solution)/shard_map/ppermute | solution.py:54
  29.5 27.9 %collective-permute-start = (bf16[4,256,256]{2,1,0:T(8,128)(2,1)}, bf16[4,256,256]{2,1,0:T(8,128)(2,1)}, u32[]{:S(2)}, u32[]{:S(2)}) collective-permute-start(bf16[4,256,256]{2,1,0:T(8,128)(2,1)} %param.8), channel_id=1, source_target_pairs={{0,0},{1,1},{6,2},{7,3},{4,4},{5,5},{10,6},{11,7},{8,8},{9,9},{14,... | collective-permute-start | bytes 1572872 | tf_op jit(solution)/shard_map/ppermute | solution.py:54
  59.6 9.2 %collective-permute-start.2 = (bf16[2,4,256,256]{3,2,1,0:T(8,128)(2,1)}, bf16[2,4,256,256]{3,2,1,0:T(8,128)(2,1)}, u32[]{:S(2)}, u32[]{:S(2)}) collective-permute-start(bf16[2,4,256,256]{3,2,1,0:T(8,128)(2,1)} %pad_maximum_fusion.1), channel_id=1, source_target_pairs={{0,1},{1,0},{2,3},{3,2},{4,5},{5,4},{6,7},{7,6},{8,9},{9,8},{10,11... | collective-permute-start | bytes 3145736 | tf_op jit(solution)/shard_map/ppermute | solution.py:57
  78.4 8.4 %copy-start.4 = (s32[128]{0:T(128)S(1)}, s32[128]{0:T(128)}, u32[]{:S(2)}) copy-start(s32[128]{0:T(128)} %param.11) | copy-start | bytes 1540
  78.4 31.8 %all-to-all-start.1 = ((bf16[8,32,3072]{2,1,0:T(8,128)(2,1)}), bf16[8,32,3072]{2,1,0:T(8,128)(2,1)S(1)}, u32[]{:S(2)}, u32[]{:S(2)}) async-start(bf16[8,32,3072]{2,1,0:T(8,128)(2,1)} %bitcast.81), calls=%async_computation.1 | async-start | bytes 3145728 | tf_op jit(solution)/shard_map/all_to_all | solution.py:119
  117.1 4.3 %copy-start.1 = (bf16[8,32,48,64]{3,2,0,1:T(8,128)(2,1)S(1)}, bf16[8,32,48,64]{3,2,0,1:T(8,128)(2,1)}, u32[]{:S(2)}) copy-start(bf16[8,32,48,64]{3,2,0,1:T(8,128)(2,1)} %reshape.131) | copy-start | bytes 4718596
  121.4 0.8 copy-start.5

commit v9 on v8

--- a/solution.py
+++ b/solution.py
@@ -52,10 +52,9 @@
                 perm.append((m * n_space + src, m * n_space + s))
         assert len({src for src, _ in perm}) == len(perm)
         own.append(lax.ppermute(weights, ("member", "space"), perm))
-    own = jnp.stack(own)
     sib_perm = [(m * n_space + s, m * n_space + (s ^ 1)) for m in range(n_member) for s in range(n_space)]
-    sib = lax.ppermute(own, ("member", "space"), sib_perm)
-    w_all = jnp.concatenate([own, sib], axis=0).reshape(n_slot, members, members)
+    sib = [lax.ppermute(w, ("member", "space"), sib_perm) for w in own]
+    w_blocks = own + sib
 
     group = region_ids // reg_count
     offset = (group // 2 - chip) % n_chip
@@ -112,7 +111,13 @@
     mask = my_labels[None, :] == jnp.arange(n_slot, dtype=jnp.int32)[:, None]
     mask = jnp.tile(mask, (1, tracers))
     masked = jnp.where(mask[:, None, :], anomaly[None], jnp.zeros((), jnp.bfloat16))
-    inc = jnp.einsum("rjk,rjx->kx", w_all, masked, preferred_element_type=jnp.float32)
+    inc = None
+    for b, w in enumerate(w_blocks):
+        part = jnp.einsum(
+            "rjk,rjx->kx", w, masked[b * reg_count:(b + 1) * reg_count],
+            preferred_element_type=jnp.float32,
+        )
+        inc = part if inc is None else inc + part
     inc = lax.reduce_precision(inc, exponent_bits=8, mantissa_bits=7)
     result = (mean[None] + inc).astype(jnp.bfloat16)
     result = result.reshape(n_member, local_members, flat)

time: 125 us -> 134 us (1.072)
  matrix products: 20.1 us -> 28.8 us
  local copies, waits for them, and re-layouts: 14.7 us -> 16.7 us
    dot_general x1 -> x4, matrix products: 7.82 us -> 15.8 us  [local(): jnp.einsum('rjk,rjx->kx', w, masked[b * reg_count:(b + 1) * reg_count], p...]
    select_n x0 -> x1, other arithmetic: none -> 3.53 us  [local(): jnp.where(mask[:, None, :], anomaly[None], jnp.zeros((), jnp.bfloat16))]
    another operation x3 -> x2, other arithmetic: 3.47 us -> 1.2 us  [the longest x1 2.27 us: local(): own = jnp.stack(own)]
    unnamed x12 -> x11, local copies, waits for them, and re-layouts: 0.03 us -> 2.07 us
    concatenate x1 -> x0, other arithmetic: 1.72 us -> none  [local(): jnp.concatenate([own, sib], axis=0).reshape(n_slot, members, members)]
    ppermute x1 -> x2, starting transfers between devices: 6.6 us -> 6.39 us  [local(): sib = [lax.ppermute(w, ('member', 'space'), sib_perm) for w in own]]
  transfers between devices with their start and end apart: 5 -> 6, of which waited for: 3 -> 2; matrix products, arithmetic and copies ran while one was open for 5% -> 15% of each run, Pallas kernels for 0% -> 0%
where the time goes in v9:
time: 134 us; the launch traced here: 133 us
  waiting for transfers between devices  44.8 us (33%)
  starting transfers between devices  34 us (25%)
  matrix products  28.8 us (21%)
  local copies, waits for them, and re-layouts  16.7 us (12%)
  other arithmetic  7.62 us (6%)
    all_to_all x1, waiting for transfers between devices, local(): lax.all_to_all(result, 'member', split_axis=0, concat_axis=0, tiled=True)  22.8 us
    ppermute x2, waiting for transfers between devices, local(): own.append(lax.ppermute(weights, ('member', 'space'), perm))  22 us
    dot_general x4, matrix products, local(): jnp.einsum('rjk,rjx->kx', w, masked[b * reg_count:(b + 1) * reg_count], p...  15.8 us
    ppermute x2, starting transfers between devices, local(): own.append(lax.ppermute(weights, ('member', 'space'), perm))  12.4 us
    all_to_all x1, starting transfers between devices, local(): lax.all_to_all(result, 'member', split_axis=0, concat_axis=0, tiled=True)  7.75 us
    all_to_all x1, starting transfers between devices, local(): lax.all_to_all(payload, 'member', split_axis=0, concat_axis=0, tiled=True)  7.48 us
    ppermute x2, starting transfers between devices, local(): sib = [lax.ppermute(w, ('member', 'space'), sib_perm) for w in own]  6.39 us
    reshape x1, local copies, waits for them, and re-layouts, local(): returned = returned.reshape(n_member, local_members, tracers, own_cols)  4.86 us
  transfers between devices with their start and end apart: 6, of which 2 were waited for; matrix products, arithmetic and copies ran while one was open for 15% of the time, Pallas kernels for 0%

profile of v9, /device:TPU:1, one launch (start us, length us, event | category | flops | bytes accessed | tf_op | source)
XLA Modules:
  0.0 132.9 jit_solution(7575042836201888034)
XLA Ops:
  2.2 1.2 reduce-window.6
  3.6 0.9 convolution_bitcast_fusion.3
  6.3 3.4 %convolution_bitcast_fusion = bf16[8,32,48,64]{3,2,1,0:T(8,128)(2,1)} fusion(bf16[32,48,512]{2,1,0:T(8,128)(2,1)S(1)} %copy-done, s32[8,64]{1,0:T(8,128)S(1)} %multiply_add_fusion, s32[512]{0:T(512)S(1)} %get-tuple-element.2), kind=kOutput, calls=%fused_computation.24 | convolution fusion | flops 805568512 | bytes 3149824 | tf_op jit(solution)/shard_map/jtc,cdi->djti/dot_general | solution.py:94
  9.7 4.0 %reshape.123 = bf16[8,32,3072]{2,1,0:T(8,128)(2,1)S(1)} reshape(bf16[8,32,48,64]{3,2,1,0:T(8,128)(2,1)} %convolution_bitcast_fusion) | data formatting | bytes 3145728 | tf_op jit(solution)/shard_map/reshape | solution.py:95
  13.7 2.0 %concatenate.3 = bf16[8,32,3328]{2,1,0:T(8,128)(2,1)} concatenate(bf16[8,32,3072]{2,1,0:T(8,128)(2,1)S(1)} %reshape.123, bf16[8,32,64]{2,1,0:T(8,128)(2,1)S(1)} %get-tuple-element.6, bf16[8,32,64]{2,1,0:T(8,128)(2,1)S(1)} %get-tuple-element.5, bf16[8,32,64]{2,1,0:T(8,128)(2,1)S(1)} %get-tuple-element.4, bf16[8,32,64]{2,1,0:T(8,128)(2,1)S(1)} %broadcast_in_dim.44), dimensions={2} | concatenate | bytes 3407872 | tf_op jit(solution)/shard_map/concatenate | solution.py:99
  15.7 7.5 %all-to-all-start = ((bf16[8,32,3328]{2,1,0:T(8,128)(2,1)}), bf16[8,32,3328]{2,1,0:T(8,128)(2,1)S(1)}, u32[]{:S(2)}, u32[]{:S(2)}) async-start(bf16[8,32,3328]{2,1,0:T(8,128)(2,1)} %concatenate.3), calls=%async_computation | async-start | bytes 3407872 | tf_op jit(solution)/shard_map/all_to_all | solution.py:101
  23.2 2.0 %copy.16 = bf16[4,256,256]{1,2,0:T(8,128)(2,1)} copy(bf16[4,256,256]{2,1,0:T(8,128)(2,1)} %param.8) | data formatting | bytes 1048576 | tf_op args[2]
  25.2 7.0 %collective-permute-start.1 = (bf16[4,256,256]{1,2,0:T(8,128)(2,1)}, bf16[4,256,256]{1,2,0:T(8,128)(2,1)}, u32[]{:S(2)}, u32[]{:S(2)}) collective-permute-start(bf16[4,256,256]{1,2,0:T(8,128)(2,1)} %copy.16), channel_id=1, source_target_pairs={{8,0},{9,1},{14,2},{15,3},{12,4},{13,5},{18,6},{19,7},{16,8},{17,9... | collective-permute-start | bytes 1572872 | tf_op jit(solution)/shard_map/ppermute | solution.py:54
  32.2 5.3 %collective-permute-start = (bf16[4,256,256]{1,2,0:T(8,128)(2,1)}, bf16[4,256,256]{1,2,0:T(8,128)(2,1)}, u32[]{:S(2)}, u32[]{:S(2)}) collective-permute-start(bf16[4,256,256]{1,2,0:T(8,128)(2,1)} %copy.16), channel_id=1, source_target_pairs={{0,0},{1,1},{6,2},{7,3},{4,4},{5,5},{10,6},{11,7},{8,8},{9,9},{14,... | collective-permute-start | bytes 1572872 | tf_op jit(solution)/shard_map/ppermute | solution.py:54
  38.2 22.0 %collective-permute-done.1 = bf16[4,256,256]{1,2,0:T(8,128)(2,1)} collective-permute-done((bf16[4,256,256]{1,2,0:T(8,128)(2,1)}, bf16[4,256,256]{1,2,0:T(8,128)(2,1)}, u32[]{:S(2)}, u32[]{:S(2)}) %collective-permute-start.1) | collective-permute-done | bytes 524320 | tf_op jit(solution)/shard_map/ppermute | solution.py:54
  60.2 6.4 %collective-permute-start.3 = (bf16[4,256,256]{1,2,0:T(8,128)(2,1)}, bf16[4,256,256]{1,2,0:T(8,128)(2,1)}, u32[]{:S(2)}, u32[]{:S(2)}) collective-permute-start(bf16[4,256,256]{1,2,0:T(8,128)(2,1)} %collective-permute-done.1), channel_id=1, source_target_pairs={{0,1},{1,0},{2,3},{3,2},{4,5},{5,4},{6,7},{7,6},{8,9},{9,8},{10,11... | collective-permute-start | bytes 1572872 | tf_op jit(solution)/shard_map/ppermute | solution.py:56
  66.9 1.6 %fusion.38 = bf16[256,3072]{1,0:T(8,128)(2,1)S(1)} fusion(f32[3072]{0:T(1024)S(1)} %broadcast_multiply_fusion, bf16[256,3328]{1,0:T(8,128)(2,1)S(1)} %bitcast.92, s32[3072]{0:T(1024)S(1)} %add_select_fusion, f32[256,256]{1,0:T(8,128)S(1)} %slice_convert_fusion), kind=kOutput, calls=%fused_computation.23 | convolution fusion | flops 607354880 | bytes 3563520 | tf_op jit(solution)/shard_map/dot_general | solution.py:108
  68.4 3.5 %broadcast_select_fusion = bf16[16,256,3072]{2,1,0:T(8,128)(2,1)S(1)} fusion(pred[16,3072]{1,0:T(8,128)(4,1)S(1)} %tile.9, bf16[256,3072]{1,0:T(8,128)(2,1)S(1)} %fusion.38), kind=kLoop, calls=%fused_computation.1 | loop fusion | flops 12582912 | bytes 26787840 | tf_op jit(solution)/shard_map/jit(_where)/select_n | solution.py:113
  72.0 2.9 %fusion.11 = f32[3072,256]{0,1:T(8,128)S(1)} fusion(bf16[4,256,256]{1,2,0:T(8,128)(2,1)} %collective-permute-done.1, bf16[16,256,3072]{2,1,0:T(8,128)(2,1)S(1)} %broadcast_select_fusion), kind=kOutput, calls=%fused_computation.12 | convolution fusion | flops 1610612736 | bytes 9961472 | tf_op jit(solution)/shard_map/rjk,rjx->kx/dot_general | solution.py:116
  74.9 3.0 %fusion.23 = f32[3072,256]{0,1:T(8,128)S(1)} fusion(f32[3072,256]{0,1:T(8,128)S(1)} %fusion.11, bf16[4,256,256]{1,2,0:T(8,128)(2,1)} %collective-permute-done, bf16[16,256,3072]{2,1,0:T(8,128)(2,1)S(1)} %broadcast_select_fusion), kind=kOutput, calls=%fused_computation.16 | convolution fusion | flops 1611399168 | bytes 13107200 | tf_op jit(solution)/shard_map/rjk,rjx->kx/dot_general | solution.py:116
  77.9 4.6 %fusion.17 = f32[3072,256]{0,1:T(8,128)} fusion(bf16[4,256,256]{1,2,0:T(8,128)(2,1)} %collective-permute-done.3, bf16[16,256,3072]{2,1,0:T(8,128)(2,1)S(1)} %broadcast_select_fusion), kind=kOutput, calls=%fused_computation.14 | convolution fusion | flops 1610612736 | bytes 9961472 | tf_op jit(solution)/shard_map/rjk,rjx->kx/dot_general | solution.py:116
  82.5 5.3 %fusion.35 = bf16[3072,256]{0,1:T(8,128)(2,1)} fusion(f32[3072,256]{0,1:T(8,128)} %fusion.17, f32[3072,256]{0,1:T(8,128)S(1)} %fusion.23, bf16[4,256,256]{1,2,0:T(8,128)(2,1)} %collective-permute-done.2, bf16[16,256,3072]{2,1,0:T(8,128)(2,1)S(1)} %broadcast_select_fusion, f32[3072]{0:T(1024)S(1)} %broadcast_multiply_fusion), kind=kOutput, calls=%fused_computation.22 | convolution fusion | flops 1614544896 | bytes 14692352 | tf_op jit(solution)/shard_map/rjk,rjx->kx/dot_general | solution.py:116
  87.8 7.8 %all-to-all-start.1 = ((bf16[8,32,3072]{2,1,0:T(8,128)(2,1)}), bf16[8,32,3072]{2,1,0:T(8,128)(2,1)S(1)}, u32[]{:S(2)}, u32[]{:S(2)}) async-start(bf16[8,32,3072]{2,1,0:T(8,128)(2,1)} %bitcast.93), calls=%async_computation.1 | async-start | bytes 3145728 | tf_op jit(solution)/shard_map/all_to_all | solution.py:124
  95.6 1.3 gather_fusion
  96.9 22.8 %all-to-all-done.1 = bf16[8,32,3072]{2,1,0:T(8,128)(2,1)S(1)} async-done(((bf16[8,32,3072]{2,1,0:T(8,128)(2,1)}), bf16[8,32,3072]{2,1,0:T(8,128)(2,1)S(1)}, u32[]{:S(2)}, u32[]{:S(2)}) %all-to-all-start.1) | async-done | bytes 1572896 | tf_op jit(solution)/shard_map/all_to_all | solution.py:124
  119.7 2.0 %copy.18 = bf16[8,32,3072]{2,0,1:T(8,128)(2,1)} copy(bf16[8,32,3072]{2,1,0:T(8,128)(2,1)S(1)} %all-to-all-done.1) | data formatting | bytes 3145728 | tf_op jit(solution)/shard_map/all_to_all | solution.py:124
  121.7 4.9 %reshape.127 = bf16[8,32,48,64]{3,2,0,1:T(8,128)(2,1)} reshape(bf16[8,32,3072]{2,0,1:T(8,128)(2,1)} %copy.18) | data formatting | bytes 3145728 | tf_op jit(solution)/shard_map/reshape | solution.py:125
  126.6 4.3 %convolution_bitcast_fusion.1 = bf16[32,48,512]{2,1,0:T(8,128)(2,1)} fusion(bf16[8,32,48,64]{3,2,0,1:T(8,128)(2,1)} %reshape.127, s32[8,64]{1,0:T(8,128)S(1)} %multiply_add_fusion, s32[512]{0:T(512)S(1)} %get-tuple-element.2), kind=kOutput, calls=%fused_computation.30 | convolution fusion | flops 805568512 | bytes 3149824 | tf_op jit(solution)/shard_map/dkti,cdi->ktc/dot_general | solution.py:126
  131.7 1.1 fusion.80
  (41 shorter events, 5.2 us)
Async XLA Ops:
  0.6 5.7 %copy-start = (bf16[32,48,512]{2,1,0:T(8,128)(2,1)S(1)}, bf16[32,48,512]{2,1,0:T(8,128)(2,1)}, u32[]{:S(2)}) copy-start(bf16[32,48,512]{2,1,0:T(8,128)(2,1)} %param.6) | copy-start | bytes 4718596
  13.7 23.9 %copy-start.2 = (s32[512]{0:T(512)S(1)}, s32[512]{0:T(512)}, u32[]{:S(2)}) copy-start(s32[512]{0:T(512)} %param.9) | copy-start | bytes 6148
  15.7 50.9 %all-to-all-start = ((bf16[8,32,3328]{2,1,0:T(8,128)(2,1)}), bf16[8,32,3328]{2,1,0:T(8,128)(2,1)S(1)}, u32[]{:S(2)}, u32[]{:S(2)}) async-start(bf16[8,32,3328]{2,1,0:T(8,128)(2,1)} %concatenate.3), calls=%async_computation | async-start | bytes 3407872 | tf_op jit(solution)/shard_map/all_to_all | solution.py:101
  25.2 34.9 %collective-permute-start.1 = (bf16[4,256,256]{1,2,0:T(8,128)(2,1)}, bf16[4,256,256]{1,2,0:T(8,128)(2,1)}, u32[]{:S(2)}, u32[]{:S(2)}) collective-permute-start(bf16[4,256,256]{1,2,0:T(8,128)(2,1)} %copy.16), channel_id=1, source_target_pairs={{8,0},{9,1},{14,2},{15,3},{12,4},{13,5},{18,6},{19,7},{16,8},{17,9... | collective-permute-start | bytes 1572872 | tf_op jit(solution)/shard_map/ppermute | solution.py:54
  32.2 34.3 %collective-permute-start = (bf16[4,256,256]{1,2,0:T(8,128)(2,1)}, bf16[4,256,256]{1,2,0:T(8,128)(2,1)}, u32[]{:S(2)}, u32[]{:S(2)}) collective-permute-start(bf16[4,256,256]{1,2,0:T(8,128)(2,1)} %copy.16), channel_id=1, source_target_pairs={{0,0},{1,1},{6,2},{7,3},{4,4},{5,5},{10,6},{11,7},{8,8},{9,9},{14,... | collective-permute-start | bytes 1572872 | tf_op jit(solution)/shard_map/ppermute | solution.py:54
  60.2 17.8 %collective-permute-start.3 = (bf16[4,256,256]{1,2,0:T(8,128)(2,1)}, bf16[4,256,256]{1,2,0:T(8,128)(2,1)}, u32[]{:S(2)}, u32[]{:S(2)}) collective-permute-start(bf16[4,256,256]{1,2,0:T(8,128)(2,1)} %collective-permute-done.1), channel_id=1, source_target_pairs={{0,1},{1,0},{2,3},{3,2},{4,5},{5,4},{6,7},{7,6},{8,9},{9,8},{10,11... | collective-permute-start | bytes 1572872 | tf_op jit(solution)/shard_map/ppermute | solution.py:56
  66.5 16.0 %collective-permute-start.2 = (bf16[4,256,256]{1,2,0:T(8,128)(2,1)}, bf16[4,256,256]{1,2,0:T(8,128)(2,1)}, u32[]{:S(2)}, u32[]{:S(2)}) collective-permute-start(bf16[4,256,256]{1,2,0:T(8,128)(2,1)} %collective-permute-done), channel_id=1, source_target_pairs={{0,1},{1,0},{2,3},{3,2},{4,5},{5,4},{6,7},{7,6},{8,9},{9,8},{10,11... | collective-permute-start | bytes 1572872 | tf_op jit(solution)/shard_map/ppermute | solution.py:56
  87.8 7.8 %copy-start.3 = (s32[128]{0:T(128)S(1)}, s32[128]{0:T(128)}, u32[]{:S(2)}) copy-start(s32[128]{0:T(128)} %param.11) | copy-start | bytes 1540
  87.8 31.9 %all-to-all-start.1 = ((bf16[8,32,3072]{2,1,0:T(8,128)(2,1)}), bf16[8,32,3072]{2,1,0:T(8,128)(2,1)S(1)}, u32[]{:S(2)}, u32[]{:S(2)}) async-start(bf16[8,32,3072]{2,1,0:T(8,128)(2,1)} %bitcast.93), calls=%async_computation.1 | async-start | bytes 3145728 | tf_op jit(solution)/shard_map/all_to_all | solution.py:124
  126.6 4.3 %copy-start.1 = (bf16[8,32,48,64]{3,2,0,1:T(8,128)(2,1)S(1)}, bf16[8,32,48,64]{3,2,0,1:T(8,128)(2,1)}, u32[]{:S(2)}) copy-start(bf16[8,32,48,64]{3,2,0,1:T(8,128)(2,1)} %reshape.127) | copy-start | bytes 4718596
  130.9 0.8 copy-start.4

commit v10 on v8

--- a/solution.py
+++ b/solution.py
@@ -116,15 +116,24 @@
     inc = lax.reduce_precision(inc, exponent_bits=8, mantissa_bits=7)
     result = (mean[None] + inc).astype(jnp.bfloat16)
     result = result.reshape(n_member, local_members, flat)
-    returned = lax.all_to_all(result, "member", split_axis=0, concat_axis=0, tiled=True)
-    returned = returned.reshape(n_member, local_members, tracers, own_cols)
-    analysis = jnp.einsum("dkti,cdi->ktc", returned, perm_mat, preferred_element_type=jnp.bfloat16)
-
     local_index = obs_cols - me_space * columns
     obs_pos = jnp.take(position, local_index)
     obs_mat = (pos_iota[:, None] == obs_pos[None, :]).astype(jnp.bfloat16)
     obs_mat = obs_mat.reshape(n_member, own_cols, obs_cols.shape[0])
-    picked = jnp.einsum("dkti,dio->kto", returned, obs_mat, preferred_element_type=jnp.float32)
+    chunk = local_members // 2
+    pieces_a, pieces_o = [], []
+    for part in range(2):
+        sent = result[:, part * chunk:(part + 1) * chunk]
+        back = lax.all_to_all(sent, "member", split_axis=0, concat_axis=0, tiled=True)
+        back = back.reshape(n_member, chunk, tracers, own_cols)
+        pieces_a.append(
+            jnp.einsum("dkti,cdi->ktc", back, perm_mat, preferred_element_type=jnp.bfloat16)
+        )
+        pieces_o.append(
+            jnp.einsum("dkti,dio->kto", back, obs_mat, preferred_element_type=jnp.float32)
+        )
+    analysis = jnp.concatenate(pieces_a, axis=0)
+    picked = jnp.concatenate(pieces_o, axis=0)
     obs_analysis = jnp.einsum("t,kto->ko", extinction, picked, precision=lax.Precision.HIGHEST)
     return (analysis, obs_analysis)
 

time: 125 us -> 130 us (1.040)
  the two profiles are of different devices: /device:TPU:1 before, /device:TPU:8 now
where the time goes in v10:
time: 130 us
  waiting for transfers between devices  36.8 us (28%)
  starting transfers between devices  23.8 us (18%)
  blocking collectives  22.9 us (18%)
  matrix products  18.2 us (14%)
  local copies, waits for them, and re-layouts  17.7 us (14%)
  other arithmetic  9.37 us (7%)
    ppermute x2, waiting for transfers between devices, local(): own.append(lax.ppermute(weights, ('member', 'space'), perm))  28.2 us
    all_to_all x1, blocking collectives, local(): lax.all_to_all(sent, 'member', split_axis=0, concat_axis=0, tiled=True)  22.9 us
    ppermute x2, starting transfers between devices, local(): own.append(lax.ppermute(weights, ('member', 'space'), perm))  13.3 us
    all_to_all x1, waiting for transfers between devices, local(): lax.all_to_all(sent, 'member', split_axis=0, concat_axis=0, tiled=True)  7.48 us
    dot_general x1, matrix products, local(): jnp.einsum('rjk,rjx->kx', w_all, masked, preferred_element_type=jnp.float32)  7.12 us
    all_to_all x1, starting transfers between devices, local(): lax.all_to_all(payload, 'member', split_axis=0, concat_axis=0, tiled=True)  6.03 us
    reshape x2, local copies, waits for them, and re-layouts, local(): back = back.reshape(n_member, chunk, tracers, own_cols)  5.03 us
    all_to_all x1, starting transfers between devices, local(): lax.all_to_all(sent, 'member', split_axis=0, concat_axis=0, tiled=True)  4.42 us
  transfers between devices with their start and end apart: 5, of which 3 were waited for; matrix products, arithmetic and copies ran while one was open for 7% of the time, Pallas kernels for 0%

profile of v10, /device:TPU:8, one launch (start us, length us, event | category | flops | bytes accessed | tf_op | source)
XLA Modules:
  0.0 129.7 jit_solution(14047688473180131054)
XLA Ops:
  2.2 1.2 reduce-window.6
  4.5 3.4 %convolution_bitcast_fusion = bf16[8,32,48,64]{3,2,1,0:T(8,128)(2,1)} fusion(bf16[32,48,512]{2,1,0:T(8,128)(2,1)S(1)} %copy-done, s32[8,64]{1,0:T(8,128)S(1)} %multiply_add_fusion, s32[512]{0:T(512)S(1)} %get-tuple-element.2), kind=kOutput, calls=%fused_computation.15 | convolution fusion | flops 805568512 | bytes 3149824 | tf_op jit(solution)/shard_map/jtc,cdi->djti/dot_general | solution.py:95
  7.8 4.0 %reshape.131 = bf16[8,32,3072]{2,1,0:T(8,128)(2,1)S(1)} reshape(bf16[8,32,48,64]{3,2,1,0:T(8,128)(2,1)} %convolution_bitcast_fusion) | data formatting | bytes 3145728 | tf_op jit(solution)/shard_map/reshape | solution.py:96
  13.0 2.0 %concatenate.13 = bf16[8,32,3328]{2,1,0:T(8,128)(2,1)} concatenate(bf16[8,32,3072]{2,1,0:T(8,128)(2,1)S(1)} %reshape.131, bf16[8,32,64]{2,1,0:T(8,128)(2,1)S(1)} %get-tuple-element.8, bf16[8,32,64]{2,1,0:T(8,128)(2,1)S(1)} %get-tuple-element.7, bf16[8,32,64]{2,1,0:T(8,128)(2,1)S(1)} %get-tuple-element.6, bf16[8,32,64]{2,1,0:T(8,128)(2,1)S(1)} %broadcast_in_dim.44), dimensions={2} | concatenate | bytes 3407872 | tf_op jit(solution)/shard_map/concatenate | solution.py:100
  15.0 6.0 %all-to-all-start = ((bf16[8,32,3328]{2,1,0:T(8,128)(2,1)}), bf16[8,32,3328]{2,1,0:T(8,128)(2,1)S(1)}, u32[]{:S(2)}, u32[]{:S(2)}) async-start(bf16[8,32,3328]{2,1,0:T(8,128)(2,1)} %concatenate.13), calls=%async_computation | async-start | bytes 3407872 | tf_op jit(solution)/shard_map/all_to_all | solution.py:102
  21.0 8.0 %collective-permute-start.1 = (bf16[4,256,256]{2,1,0:T(8,128)(2,1)}, bf16[4,256,256]{2,1,0:T(8,128)(2,1)}, u32[]{:S(2)}, u32[]{:S(2)}) collective-permute-start(bf16[4,256,256]{2,1,0:T(8,128)(2,1)} %param.8), channel_id=1, source_target_pairs={{8,0},{9,1},{14,2},{15,3},{12,4},{13,5},{18,6},{19,7},{16,8},{17,9... | collective-permute-start | bytes 1572872 | tf_op jit(solution)/shard_map/ppermute | solution.py:54
  29.0 5.3 %collective-permute-start = (bf16[4,256,256]{2,1,0:T(8,128)(2,1)}, bf16[4,256,256]{2,1,0:T(8,128)(2,1)}, u32[]{:S(2)}, u32[]{:S(2)}) collective-permute-start(bf16[4,256,256]{2,1,0:T(8,128)(2,1)} %param.8), channel_id=1, source_target_pairs={{0,0},{1,1},{6,2},{7,3},{4,4},{5,5},{10,6},{11,7},{8,8},{9,9},{14,... | collective-permute-start | bytes 1572872 | tf_op jit(solution)/shard_map/ppermute | solution.py:54
  34.9 28.2 %collective-permute-done.1 = bf16[4,256,256]{2,1,0:T(8,128)(2,1)} collective-permute-done((bf16[4,256,256]{2,1,0:T(8,128)(2,1)}, bf16[4,256,256]{2,1,0:T(8,128)(2,1)}, u32[]{:S(2)}, u32[]{:S(2)}) %collective-permute-start.1) | collective-permute-done | bytes 524320 | tf_op jit(solution)/shard_map/ppermute | solution.py:54
  63.1 2.3 %pad_maximum_fusion.2 = bf16[2,4,256,256]{3,2,1,0:T(8,128)(2,1)} fusion(bf16[1,4,256,256]{3,2,1,0:T(8,128)(2,1)} %bitcast.10, bf16[1,4,256,256]{3,2,1,0:T(8,128)(2,1)} %bitcast.9), kind=kLoop, calls=%fused_computation.28 | loop fusion | flops 524288 | bytes 2097152 | tf_op jit(solution)/shard_map/stack | solution.py:55
  65.7 1.6 %fusion.17 = bf16[256,3072]{1,0:T(8,128)(2,1)S(1)} fusion(f32[3072]{0:T(1024)S(1)} %broadcast_multiply_fusion, bf16[256,3328]{1,0:T(8,128)(2,1)S(1)} %bitcast.91, s32[3072]{0:T(1024)S(1)} %add_select_fusion, f32[256,256]{1,0:T(8,128)S(1)} %slice_convert_fusion), kind=kOutput, calls=%fused_computation.13 | convolution fusion | flops 607354880 | bytes 3563520 | tf_op jit(solution)/shard_map/dot_general | solution.py:109
  67.3 1.1 collective-permute-done.2
  68.4 1.7 %pad_maximum_fusion = bf16[4,4,256,256]{3,2,1,0:T(8,128)(2,1)S(1)} fusion(bf16[2,4,256,256]{3,2,1,0:T(8,128)(2,1)} %collective-permute-done.2, bf16[1,4,256,256]{3,2,1,0:T(8,128)(2,1)} %bitcast.10, bf16[1,4,256,256]{3,2,1,0:T(8,128)(2,1)} %bitcast.9), kind=kLoop, calls=%fused_computation.14 | loop fusion | flops 2097152 | bytes 4194304 | tf_op jit(solution)/shard_map/concatenate | solution.py:58
  70.1 7.1 %fusion.14 = bf16[256,3072]{1,0:T(8,128)(2,1)S(1)} fusion(bf16[16,256,256]{2,1,0:T(8,128)(2,1)S(1)} %bitcast.92, pred[16,3072]{1,0:T(8,128)(4,1)S(1)} %tile.9, bf16[256,3072]{1,0:T(8,128)(2,1)S(1)} %fusion.17, f32[3072]{0:T(1024)S(1)} %broadcast_multiply_fusion), kind=kOutput, calls=%fused_computation.12 | convolution fusion | flops 6457393152 | bytes 5304320 | tf_op jit(solution)/shard_map/rjk,rjx->kx/dot_general | solution.py:115
  78.2 22.9 %all_to_all.15 = bf16[8,16,3072]{2,1,0:T(8,128)(2,1)S(1)} all-to-all(bf16[8,16,3072]{2,1,0:T(8,128)(2,1)S(1)} %get-tuple-element.5), channel_id=1, replica_groups=mesh['member'=8,'space'=32] {'member'}, dimensions={0} | all-to-all | bytes 1572864 | tf_op jit(solution)/shard_map/all_to_all | solution.py:127
  101.2 4.4 %all-to-all-start.1 = ((bf16[8,16,3072]{2,1,0:T(8,128)(2,1)}), bf16[8,16,3072]{2,1,0:T(8,128)(2,1)}, u32[]{:S(2)}, u32[]{:S(2)}) async-start(bf16[8,16,3072]{2,1,0:T(8,128)(2,1)} %get-tuple-element.4), calls=%async_computation.1 | async-start | bytes 1572864 | tf_op jit(solution)/shard_map/all_to_all | solution.py:127
  105.6 1.3 gather_fusion
  106.9 1.3 %copy.18 = bf16[8,16,3072]{2,0,1:T(8,128)(2,1)} copy(bf16[8,16,3072]{2,1,0:T(8,128)(2,1)S(1)} %all_to_all.15) | data formatting | bytes 1572864 | tf_op jit(solution)/shard_map/all_to_all | solution.py:127
  108.3 2.1 %reshape.137 = bf16[8,16,48,64]{3,2,0,1:T(8,128)(2,1)S(1)} reshape(bf16[8,16,3072]{2,0,1:T(8,128)(2,1)} %copy.18) | data formatting | bytes 1572864 | tf_op jit(solution)/shard_map/reshape | solution.py:128
  110.3 7.5 %all-to-all-done.1 = bf16[8,16,3072]{2,1,0:T(8,128)(2,1)} async-done(((bf16[8,16,3072]{2,1,0:T(8,128)(2,1)}), bf16[8,16,3072]{2,1,0:T(8,128)(2,1)}, u32[]{:S(2)}, u32[]{:S(2)}) %all-to-all-start.1) | async-done | bytes 786464 | tf_op jit(solution)/shard_map/all_to_all | solution.py:127
  117.8 2.5 %copy.17 = bf16[8,16,3072]{2,0,1:T(8,128)(2,1)} copy(bf16[8,16,3072]{2,1,0:T(8,128)(2,1)} %all-to-all-done.1) | data formatting | bytes 1572864 | tf_op jit(solution)/shard_map/all_to_all | solution.py:127
  120.3 3.0 %reshape.136 = bf16[8,16,48,64]{3,2,0,1:T(8,128)(2,1)} reshape(bf16[8,16,3072]{2,0,1:T(8,128)(2,1)} %copy.17) | data formatting | bytes 1572864 | tf_op jit(solution)/shard_map/reshape | solution.py:128
  123.3 2.2 %convolution_bitcast_fusion.2 = bf16[16,48,512]{2,1,0:T(8,128)(2,1)S(1)} fusion(bf16[8,16,48,64]{3,2,0,1:T(8,128)(2,1)} %reshape.136, s32[8,64]{1,0:T(8,128)S(1)} %multiply_add_fusion, s32[512]{0:T(512)S(1)} %get-tuple-element.2), kind=kOutput, calls=%fused_computation.23 | convolution fusion | flops 402915328 | bytes 1576960 | tf_op jit(solution)/shard_map/dkti,cdi->ktc/dot_general | solution.py:130
  127.3 1.3 pad_maximum_fusion.1
  128.6 1.1 fusion.24
  (45 shorter events, 7.3 us)
Async XLA Ops:
  0.6 3.8 %copy-start = (bf16[32,48,512]{2,1,0:T(8,128)(2,1)S(1)}, bf16[32,48,512]{2,1,0:T(8,128)(2,1)}, u32[]{:S(2)}) copy-start(bf16[32,48,512]{2,1,0:T(8,128)(2,1)} %param.6) | copy-start | bytes 4718596
  7.8 4.0 %copy-start.2 = (s32[512]{0:T(512)S(1)}, s32[512]{0:T(512)}, u32[]{:S(2)}) copy-start(s32[512]{0:T(512)} %param.9) | copy-start | bytes 6148
  7.8 4.1 %copy-start.3 = (f32[32,128]{1,0:T(8,128)S(1)}, f32[32,128]{1,0:T(8,128)}, u32[]{:S(2)}) copy-start(f32[32,128]{1,0:T(8,128)} %param.7) | copy-start | bytes 49156
  15.0 50.4 %all-to-all-start = ((bf16[8,32,3328]{2,1,0:T(8,128)(2,1)}), bf16[8,32,3328]{2,1,0:T(8,128)(2,1)S(1)}, u32[]{:S(2)}, u32[]{:S(2)}) async-start(bf16[8,32,3328]{2,1,0:T(8,128)(2,1)} %concatenate.13), calls=%async_computation | async-start | bytes 3407872 | tf_op jit(solution)/shard_map/all_to_all | solution.py:102
  21.0 42.1 %collective-permute-start.1 = (bf16[4,256,256]{2,1,0:T(8,128)(2,1)}, bf16[4,256,256]{2,1,0:T(8,128)(2,1)}, u32[]{:S(2)}, u32[]{:S(2)}) collective-permute-start(bf16[4,256,256]{2,1,0:T(8,128)(2,1)} %param.8), channel_id=1, source_target_pairs={{8,0},{9,1},{14,2},{15,3},{12,4},{13,5},{18,6},{19,7},{16,8},{17,9... | collective-permute-start | bytes 1572872 | tf_op jit(solution)/shard_map/ppermute | solution.py:54
  29.0 34.1 %collective-permute-start = (bf16[4,256,256]{2,1,0:T(8,128)(2,1)}, bf16[4,256,256]{2,1,0:T(8,128)(2,1)}, u32[]{:S(2)}, u32[]{:S(2)}) collective-permute-start(bf16[4,256,256]{2,1,0:T(8,128)(2,1)} %param.8), channel_id=1, source_target_pairs={{0,0},{1,1},{6,2},{7,3},{4,4},{5,5},{10,6},{11,7},{8,8},{9,9},{14,... | collective-permute-start | bytes 1572872 | tf_op jit(solution)/shard_map/ppermute | solution.py:54
  65.4 3.0 %collective-permute-start.2 = (bf16[2,4,256,256]{3,2,1,0:T(8,128)(2,1)}, bf16[2,4,256,256]{3,2,1,0:T(8,128)(2,1)}, u32[]{:S(2)}, u32[]{:S(2)}) collective-permute-start(bf16[2,4,256,256]{3,2,1,0:T(8,128)(2,1)} %pad_maximum_fusion.2), channel_id=1, source_target_pairs={{0,1},{1,0},{2,3},{3,2},{4,5},{5,4},{6,7},{7,6},{8,9},{9,8},{10,11... | collective-permute-start | bytes 3145736 | tf_op jit(solution)/shard_map/ppermute | solution.py:57
  78.2 27.4 %copy-start.4 = (s32[128]{0:T(128)S(1)}, s32[128]{0:T(128)}, u32[]{:S(2)}) copy-start(s32[128]{0:T(128)} %param.11) | copy-start | bytes 1540
  101.2 16.7 %all-to-all-start.1 = ((bf16[8,16,3072]{2,1,0:T(8,128)(2,1)}), bf16[8,16,3072]{2,1,0:T(8,128)(2,1)}, u32[]{:S(2)}, u32[]{:S(2)}) async-start(bf16[8,16,3072]{2,1,0:T(8,128)(2,1)} %get-tuple-element.4), calls=%async_computation.1 | async-start | bytes 1572864 | tf_op jit(solution)/shard_map/all_to_all | solution.py:127
  123.3 2.2 %copy-start.1 = (bf16[8,16,48,64]{3,2,0,1:T(8,128)(2,1)S(1)}, bf16[8,16,48,64]{3,2,0,1:T(8,128)(2,1)}, u32[]{:S(2)}) copy-start(bf16[8,16,48,64]{3,2,0,1:T(8,128)(2,1)} %reshape.136) | copy-start | bytes 2359300
  127.3 1.3 copy-start.5

commit v11 on v8

--- a/solution.py
+++ b/solution.py
@@ -52,10 +52,7 @@
                 perm.append((m * n_space + src, m * n_space + s))
         assert len({src for src, _ in perm}) == len(perm)
         own.append(lax.ppermute(weights, ("member", "space"), perm))
-    own = jnp.stack(own)
     sib_perm = [(m * n_space + s, m * n_space + (s ^ 1)) for m in range(n_member) for s in range(n_space)]
-    sib = lax.ppermute(own, ("member", "space"), sib_perm)
-    w_all = jnp.concatenate([own, sib], axis=0).reshape(n_slot, members, members)
 
     group = region_ids // reg_count
     offset = (group // 2 - chip) % n_chip
@@ -99,6 +96,10 @@
     pad = jnp.zeros((n_member, local_members, spare), jnp.bfloat16)
     payload = jnp.concatenate([main, hi, mid, lo, pad], axis=2)
 
+    payload, near = lax.optimization_barrier((payload, own[0]))
+    own = jnp.stack([near] + own[1:])
+    sib = lax.ppermute(own, ("member", "space"), sib_perm)
+    w_all = jnp.concatenate([own, sib], axis=0).reshape(n_slot, members, members)
     received = lax.all_to_all(payload, "member", split_axis=0, concat_axis=0, tiled=True)
     received = received.reshape(members, payload.shape[2])
     ens32 = received[:, :flat].astype(jnp.float32)

time: 125 us -> 120 us (0.960)
  waiting for transfers between devices: 44.8 us -> 35.7 us
  starting transfers between devices: 34.8 us -> 38.9 us
    ppermute x2, waiting for transfers between devices: 22 us -> 1.18 us  [local(): own.append(lax.ppermute(weights, ('member', 'space'), perm))]
    all_to_all x1, waiting for transfers between devices: 0.01 us -> 12.7 us  [local(): lax.all_to_all(payload, 'member', split_axis=0, concat_axis=0, tiled=True)]
    all_to_all x1, starting transfers between devices: 7.48 us -> 19.6 us  [local(): lax.all_to_all(payload, 'member', split_axis=0, concat_axis=0, tiled=True)]
    ppermute x1, starting transfers between devices: 6.6 us -> 1.21 us  [local(): sib = lax.ppermute(own, ('member', 'space'), sib_perm)]
    all_to_all x1, starting transfers between devices: 8.4 us -> 3.89 us  [local(): lax.all_to_all(result, 'member', split_axis=0, concat_axis=0, tiled=True)]
    all_to_all x1, waiting for transfers between devices: 22.1 us -> 19.8 us  [local(): lax.all_to_all(result, 'member', split_axis=0, concat_axis=0, tiled=True)]
    ppermute x2, starting transfers between devices: 12.4 us -> 14.2 us  [local(): own.append(lax.ppermute(weights, ('member', 'space'), perm))]
    concatenate x1, other arithmetic: 1.72 us -> 3.07 us  [local(): jnp.concatenate([own, sib], axis=0).reshape(n_slot, members, members)]
  transfers between devices with their start and end apart: 5 -> 5, of which waited for: 3 -> 4; matrix products, arithmetic and copies ran while one was open for 5% -> 17% of each run, Pallas kernels for 0% -> 0%
where the time goes in v11:
time: 120 us; the launch traced here: 118 us
  starting transfers between devices  38.9 us (32%)
  waiting for transfers between devices  35.7 us (30%)
  matrix products  20.1 us (17%)
  local copies, waits for them, and re-layouts  14.7 us (12%)
  other arithmetic  7.93 us (7%)
    all_to_all x1, waiting for transfers between devices, local(): lax.all_to_all(result, 'member', split_axis=0, concat_axis=0, tiled=True)  19.8 us
    all_to_all x1, starting transfers between devices, local(): lax.all_to_all(payload, 'member', split_axis=0, concat_axis=0, tiled=True)  19.6 us
    ppermute x2, starting transfers between devices, local(): own.append(lax.ppermute(weights, ('member', 'space'), perm))  14.2 us
    all_to_all x1, waiting for transfers between devices, local(): lax.all_to_all(payload, 'member', split_axis=0, concat_axis=0, tiled=True)  12.7 us
    dot_general x1, matrix products, local(): jnp.einsum('rjk,rjx->kx', w_all, masked, preferred_element_type=jnp.float32)  7.82 us
    reshape x1, local copies, waits for them, and re-layouts, local(): returned = returned.reshape(n_member, local_members, tracers, own_cols)  4.86 us
    dot_general x1, matrix products, local(): jnp.einsum('dkti,cdi->ktc', returned, perm_mat, preferred_element_type=jn...  4.31 us
    reshape x1, local copies, waits for them, and re-layouts, local(): main = main.reshape(n_member, local_members, flat)  4.03 us
  transfers between devices with their start and end apart: 5, of which 4 were waited for; matrix products, arithmetic and copies ran while one was open for 17% of the time, Pallas kernels for 0%

profile of v11, /device:TPU:1, one launch (start us, length us, event | category | flops | bytes accessed | tf_op | source)
XLA Modules:
  0.0 118.2 jit_solution(10207977928037435077)
XLA Ops:
  0.6 5.5 %collective-permute-start = (bf16[4,256,256]{2,1,0:T(8,128)(2,1)}, bf16[4,256,256]{2,1,0:T(8,128)(2,1)}, u32[]{:S(2)}, u32[]{:S(2)}) collective-permute-start(bf16[4,256,256]{2,1,0:T(8,128)(2,1)} %param.8), channel_id=1, source_target_pairs={{0,0},{1,1},{6,2},{7,3},{4,4},{5,5},{10,6},{11,7},{8,8},{9,9},{14,... | collective-permute-start | bytes 1572872 | tf_op jit(solution)/shard_map/ppermute | solution.py:54
  6.1 8.8 %collective-permute-start.1 = (bf16[4,256,256]{2,1,0:T(8,128)(2,1)}, bf16[4,256,256]{2,1,0:T(8,128)(2,1)}, u32[]{:S(2)}, u32[]{:S(2)}) collective-permute-start(bf16[4,256,256]{2,1,0:T(8,128)(2,1)} %param.8), channel_id=1, source_target_pairs={{8,0},{9,1},{14,2},{15,3},{12,4},{13,5},{18,6},{19,7},{16,8},{17,9... | collective-permute-start | bytes 1572872 | tf_op jit(solution)/shard_map/ppermute | solution.py:54
  15.6 1.2 reduce-window.6
  17.2 3.4 %convolution_bitcast_fusion = bf16[8,32,48,64]{3,2,1,0:T(8,128)(2,1)} fusion(bf16[32,48,512]{2,1,0:T(8,128)(2,1)S(1)} %copy-done, s32[8,64]{1,0:T(8,128)S(1)} %multiply_add_fusion, s32[512]{0:T(512)S(1)} %fusion.52), kind=kOutput, calls=%fused_computation.15 | convolution fusion | flops 805568512 | bytes 3149824 | tf_op jit(solution)/shard_map/jtc,cdi->djti/dot_general | solution.py:92
  20.6 4.0 %reshape.126 = bf16[8,32,3072]{2,1,0:T(8,128)(2,1)S(1)} reshape(bf16[8,32,48,64]{3,2,1,0:T(8,128)(2,1)} %convolution_bitcast_fusion) | data formatting | bytes 3145728 | tf_op jit(solution)/shard_map/reshape | solution.py:93
  24.8 0.9 fusion.33
  25.7 2.0 %concatenate.7 = bf16[8,32,3328]{2,1,0:T(8,128)(2,1)} concatenate(bf16[8,32,3072]{2,1,0:T(8,128)(2,1)S(1)} %reshape.126, bf16[8,32,64]{2,1,0:T(8,128)(2,1)S(1)} %get-tuple-element.11, bf16[8,32,64]{2,1,0:T(8,128)(2,1)S(1)} %get-tuple-element.10, bf16[8,32,64]{2,1,0:T(8,128)(2,1)S(1)} %get-tuple-element.9, bf16[8,32,64]{2,1,0:T(8,128)(2,1)S(1)} %broadcast_in_dim.44), dimensions={2} | concatenate | bytes 3407872 | tf_op jit(solution)/shard_map/concatenate | solution.py:97
  27.7 19.6 %all-to-all-start = ((bf16[8,32,3328]{2,1,0:T(8,128)(2,1)}), bf16[8,32,3328]{2,1,0:T(8,128)(2,1)S(1)}, u32[]{:S(2)}, u32[]{:S(2)}) async-start(bf16[8,32,3328]{2,1,0:T(8,128)(2,1)} %concatenate.7), calls=%async_computation | async-start | bytes 3407872 | tf_op jit(solution)/shard_map/all_to_all | solution.py:103
  47.3 1.2 collective-permute-done.1
  48.5 2.3 %pad_maximum_fusion.1 = bf16[2,4,256,256]{3,2,1,0:T(8,128)(2,1)} fusion(bf16[1,4,256,256]{3,2,1,0:T(8,128)(2,1)} %bitcast.10, bf16[1,4,256,256]{3,2,1,0:T(8,128)(2,1)} %bitcast.9), kind=kLoop, calls=%fused_computation.25 | loop fusion | flops 524288 | bytes 2097152 | tf_op jit(solution)/shard_map/stack | solution.py:100
  50.8 1.2 %collective-permute-start.2 = (bf16[2,4,256,256]{3,2,1,0:T(8,128)(2,1)}, bf16[2,4,256,256]{3,2,1,0:T(8,128)(2,1)}, u32[]{:S(2)}, u32[]{:S(2)}) collective-permute-start(bf16[2,4,256,256]{3,2,1,0:T(8,128)(2,1)} %pad_maximum_fusion.1), channel_id=1, source_target_pairs={{0,1},{1,0},{2,3},{3,2},{4,5},{5,4},{6,7},{7,6},{8,9},{9,8},{10,11... | collective-permute-start | bytes 3145736 | tf_op jit(solution)/shard_map/ppermute | solution.py:101
  52.5 2.1 %collective-permute-done.2 = bf16[2,4,256,256]{3,2,1,0:T(8,128)(2,1)} collective-permute-done((bf16[2,4,256,256]{3,2,1,0:T(8,128)(2,1)}, bf16[2,4,256,256]{3,2,1,0:T(8,128)(2,1)}, u32[]{:S(2)}, u32[]{:S(2)}) %collective-permute-start.2) | collective-permute-done | bytes 1048608 | tf_op jit(solution)/shard_map/ppermute | solution.py:101
  54.6 3.1 %pad_maximum_fusion = bf16[4,4,256,256]{3,2,1,0:T(8,128)(2,1)} fusion(bf16[2,4,256,256]{3,2,1,0:T(8,128)(2,1)} %collective-permute-done.2, bf16[1,4,256,256]{3,2,1,0:T(8,128)(2,1)} %bitcast.10, bf16[1,4,256,256]{3,2,1,0:T(8,128)(2,1)} %bitcast.9), kind=kLoop, calls=%fused_computation.14 | loop fusion | flops 2097152 | bytes 4194304 | tf_op jit(solution)/shard_map/concatenate | solution.py:102
  57.7 12.7 %all-to-all-done = bf16[8,32,3328]{2,1,0:T(8,128)(2,1)S(1)} async-done(((bf16[8,32,3328]{2,1,0:T(8,128)(2,1)}), bf16[8,32,3328]{2,1,0:T(8,128)(2,1)S(1)}, u32[]{:S(2)}, u32[]{:S(2)}) %all-to-all-start) | async-done | bytes 1703968 | tf_op jit(solution)/shard_map/all_to_all | solution.py:103
  70.7 1.6 %fusion.17 = bf16[256,3072]{1,0:T(8,128)(2,1)S(1)} fusion(f32[3072]{0:T(1024)S(1)} %broadcast_multiply_fusion, bf16[256,3328]{1,0:T(8,128)(2,1)S(1)} %bitcast.78, s32[3072]{0:T(1024)S(1)} %add_select_fusion, f32[256,256]{1,0:T(8,128)S(1)} %slice_convert_fusion), kind=kOutput, calls=%fused_computation.13 | convolution fusion | flops 607354880 | bytes 3563520 | tf_op jit(solution)/shard_map/dot_general | solution.py:110
  72.3 7.8 %fusion.14 = bf16[256,3072]{1,0:T(8,128)(2,1)} fusion(bf16[16,256,256]{2,1,0:T(8,128)(2,1)S(1)} %bitcast.79, pred[16,3072]{1,0:T(8,128)(4,1)S(1)} %tile.9, bf16[256,3072]{1,0:T(8,128)(2,1)S(1)} %fusion.17, f32[3072]{0:T(1024)S(1)} %broadcast_multiply_fusion), kind=kOutput, calls=%fused_computation.12 | convolution fusion | flops 6457393152 | bytes 5304320 | tf_op jit(solution)/shard_map/rjk,rjx->kx/dot_general | solution.py:116
  80.1 3.9 %all-to-all-start.1 = ((bf16[8,32,3072]{2,1,0:T(8,128)(2,1)}), bf16[8,32,3072]{2,1,0:T(8,128)(2,1)S(1)}, u32[]{:S(2)}, u32[]{:S(2)}) async-start(bf16[8,32,3072]{2,1,0:T(8,128)(2,1)} %bitcast.80), calls=%async_computation.1 | async-start | bytes 3145728 | tf_op jit(solution)/shard_map/all_to_all | solution.py:120
  84.0 1.3 %gather_fusion = s32[128]{0:T(128)S(1)} fusion(s32[512]{0:T(512)S(1)} %fusion.52, s32[1024]{0:T(1024)S(1)} %pad_clamp_fusion), kind=kCustom, calls=%fused_computation | custom fusion | bytes 1536 | tf_op jit(solution)/shard_map/jit(_take)/gather | solution.py:125
  85.3 19.8 %all-to-all-done.1 = bf16[8,32,3072]{2,1,0:T(8,128)(2,1)S(1)} async-done(((bf16[8,32,3072]{2,1,0:T(8,128)(2,1)}), bf16[8,32,3072]{2,1,0:T(8,128)(2,1)S(1)}, u32[]{:S(2)}, u32[]{:S(2)}) %all-to-all-start.1) | async-done | bytes 1572896 | tf_op jit(solution)/shard_map/all_to_all | solution.py:120
  105.1 2.0 %copy.15 = bf16[8,32,3072]{2,0,1:T(8,128)(2,1)} copy(bf16[8,32,3072]{2,1,0:T(8,128)(2,1)S(1)} %all-to-all-done.1) | data formatting | bytes 3145728 | tf_op jit(solution)/shard_map/all_to_all | solution.py:120
  107.1 4.9 %reshape.131 = bf16[8,32,48,64]{3,2,0,1:T(8,128)(2,1)} reshape(bf16[8,32,3072]{2,0,1:T(8,128)(2,1)} %copy.15) | data formatting | bytes 3145728 | tf_op jit(solution)/shard_map/reshape | solution.py:121
  111.9 4.3 %convolution_bitcast_fusion.1 = bf16[32,48,512]{2,1,0:T(8,128)(2,1)} fusion(bf16[8,32,48,64]{3,2,0,1:T(8,128)(2,1)} %reshape.131, s32[8,64]{1,0:T(8,128)S(1)} %multiply_add_fusion, s32[512]{0:T(512)S(1)} %fusion.52), kind=kOutput, calls=%fused_computation.21 | convolution fusion | flops 805568512 | bytes 3149824 | tf_op jit(solution)/shard_map/dkti,cdi->ktc/dot_general | solution.py:122
  116.3 0.8 convolution_bitcast_fusion.2
  117.1 1.1 fusion.59
  (38 shorter events, 2.2 us)
Async XLA Ops:
  0.6 16.6 %copy-start = (bf16[32,48,512]{2,1,0:T(8,128)(2,1)S(1)}, bf16[32,48,512]{2,1,0:T(8,128)(2,1)}, u32[]{:S(2)}) copy-start(bf16[32,48,512]{2,1,0:T(8,128)(2,1)} %param.6) | copy-start | bytes 4718596
  0.6 27.1 %collective-permute-start = (bf16[4,256,256]{2,1,0:T(8,128)(2,1)}, bf16[4,256,256]{2,1,0:T(8,128)(2,1)}, u32[]{:S(2)}, u32[]{:S(2)}) collective-permute-start(bf16[4,256,256]{2,1,0:T(8,128)(2,1)} %param.8), channel_id=1, source_target_pairs={{0,0},{1,1},{6,2},{7,3},{4,4},{5,5},{10,6},{11,7},{8,8},{9,9},{14,... | collective-permute-start | bytes 1572872 | tf_op jit(solution)/shard_map/ppermute | solution.py:54
  6.1 42.4 %collective-permute-start.1 = (bf16[4,256,256]{2,1,0:T(8,128)(2,1)}, bf16[4,256,256]{2,1,0:T(8,128)(2,1)}, u32[]{:S(2)}, u32[]{:S(2)}) collective-permute-start(bf16[4,256,256]{2,1,0:T(8,128)(2,1)} %param.8), channel_id=1, source_target_pairs={{8,0},{9,1},{14,2},{15,3},{12,4},{13,5},{18,6},{19,7},{16,8},{17,9... | collective-permute-start | bytes 1572872 | tf_op jit(solution)/shard_map/ppermute | solution.py:54
  20.6 4.0 %copy-start.3 = (f32[32,128]{1,0:T(8,128)S(1)}, f32[32,128]{1,0:T(8,128)}, u32[]{:S(2)}) copy-start(f32[32,128]{1,0:T(8,128)} %param.7) | copy-start | bytes 49156
  20.6 4.1 %copy-start.4 = (s32[512]{0:T(512)S(1)}, s32[512]{0:T(512)}, u32[]{:S(2)}) copy-start(s32[512]{0:T(512)} %param.9) | copy-start | bytes 6148
  27.7 42.7 %all-to-all-start = ((bf16[8,32,3328]{2,1,0:T(8,128)(2,1)}), bf16[8,32,3328]{2,1,0:T(8,128)(2,1)S(1)}, u32[]{:S(2)}, u32[]{:S(2)}) async-start(bf16[8,32,3328]{2,1,0:T(8,128)(2,1)} %concatenate.7), calls=%async_computation | async-start | bytes 3407872 | tf_op jit(solution)/shard_map/all_to_all | solution.py:103
  50.8 3.8 %collective-permute-start.2 = (bf16[2,4,256,256]{3,2,1,0:T(8,128)(2,1)}, bf16[2,4,256,256]{3,2,1,0:T(8,128)(2,1)}, u32[]{:S(2)}, u32[]{:S(2)}) collective-permute-start(bf16[2,4,256,256]{3,2,1,0:T(8,128)(2,1)} %pad_maximum_fusion.1), channel_id=1, source_target_pairs={{0,1},{1,0},{2,3},{3,2},{4,5},{5,4},{6,7},{7,6},{8,9},{9,8},{10,11... | collective-permute-start | bytes 3145736 | tf_op jit(solution)/shard_map/ppermute | solution.py:101
  70.6 1.6 %copy-start.2 = (bf16[4,4,256,256]{3,2,1,0:T(8,128)(2,1)S(1)}, bf16[4,4,256,256]{3,2,1,0:T(8,128)(2,1)}, u32[]{:S(2)}) copy-start(bf16[4,4,256,256]{3,2,1,0:T(8,128)(2,1)} %pad_maximum_fusion) | copy-start | bytes 6291460
  80.1 3.9 %copy-start.5 = (s32[128]{0:T(128)S(1)}, s32[128]{0:T(128)}, u32[]{:S(2)}) copy-start(s32[128]{0:T(128)} %param.11) | copy-start | bytes 1540
  80.1 25.0 %all-to-all-start.1 = ((bf16[8,32,3072]{2,1,0:T(8,128)(2,1)}), bf16[8,32,3072]{2,1,0:T(8,128)(2,1)S(1)}, u32[]{:S(2)}, u32[]{:S(2)}) async-start(bf16[8,32,3072]{2,1,0:T(8,128)(2,1)} %bitcast.80), calls=%async_computation.1 | async-start | bytes 3145728 | tf_op jit(solution)/shard_map/all_to_all | solution.py:120
  111.9 4.3 %copy-start.1 = (bf16[8,32,48,64]{3,2,0,1:T(8,128)(2,1)S(1)}, bf16[8,32,48,64]{3,2,0,1:T(8,128)(2,1)}, u32[]{:S(2)}) copy-start(bf16[8,32,48,64]{3,2,0,1:T(8,128)(2,1)} %reshape.131) | copy-start | bytes 4718596
  116.3 0.8 copy-start.6

commit v12 on v11

--- a/solution.py
+++ b/solution.py
@@ -51,7 +51,13 @@
                 src = 2 * ((p + pairs_of[p % 2][m][a]) % n_chip) + s % 2
                 perm.append((m * n_space + src, m * n_space + s))
         assert len({src for src, _ in perm}) == len(perm)
-        own.append(lax.ppermute(weights, ("member", "space"), perm))
+        if a == 0:
+            half_reg = reg_count // 2
+            first = lax.ppermute(weights[:half_reg], ("member", "space"), perm)
+            rest = lax.ppermute(weights[half_reg:], ("member", "space"), perm)
+            own.append(None)
+        else:
+            own.append(lax.ppermute(weights, ("member", "space"), perm))
     sib_perm = [(m * n_space + s, m * n_space + (s ^ 1)) for m in range(n_member) for s in range(n_space)]
 
     group = region_ids // reg_count
@@ -96,8 +102,8 @@
     pad = jnp.zeros((n_member, local_members, spare), jnp.bfloat16)
     payload = jnp.concatenate([main, hi, mid, lo, pad], axis=2)
 
-    payload, near = lax.optimization_barrier((payload, own[0]))
-    own = jnp.stack([near] + own[1:])
+    payload, first = lax.optimization_barrier((payload, first))
+    own = jnp.stack([jnp.concatenate([first, rest], axis=0)] + own[1:])
     sib = lax.ppermute(own, ("member", "space"), sib_perm)
     w_all = jnp.concatenate([own, sib], axis=0).reshape(n_slot, members, members)
     received = lax.all_to_all(payload, "member", split_axis=0, concat_axis=0, tiled=True)

time: 120 us -> 119 us (level)
  starting transfers between devices: 38.9 us -> 31 us
  local copies, waits for them, and re-layouts: 14.7 us -> 18.6 us
  waiting for transfers between devices: 35.7 us -> 37 us
    all_to_all x1, starting transfers between devices: 19.6 us -> 12.2 us  [local(): lax.all_to_all(payload, 'member', split_axis=0, concat_axis=0, tiled=True)]
    ppermute x2 -> x1, starting transfers between devices: 14.2 us -> 8.83 us  [local(): own.append(lax.ppermute(weights, ('member', 'space'), perm))]
    ppermute x0 -> x2, starting transfers between devices: none -> 5.17 us  [the longest x1 3.58 us: local(): rest = lax.ppermute(weights[half_reg:], ('member', 'space'), perm)]
    slice x1 -> x2, local copies, waits for them, and re-layouts: 0.22 us -> 2.07 us  [the longest x1 1.85 us: local(): first = lax.ppermute(weights[:half_reg], ('member', 'space'), perm)]
    all_to_all x1, waiting for transfers between devices: 12.7 us -> 14.2 us  [local(): lax.all_to_all(payload, 'member', split_axis=0, concat_axis=0, tiled=True)]
    concatenate x1, local copies, waits for them, and re-layouts: 1.96 us -> 3.22 us  [local(): payload = jnp.concatenate([main, hi, mid, lo, pad], axis=2)]
    another operation x3 -> x4, other arithmetic: 3.47 us -> 4.31 us  [the longest x2 3.11 us: local(): own = jnp.stack([jnp.concatenate([first, rest], axis=0)] + own[1:])]
  transfers between devices with their start and end apart: 5 -> 6, of which waited for: 4 -> 3; matrix products, arithmetic and copies ran while one was open for 17% -> 21% of each run, Pallas kernels for 0% -> 0%
where the time goes in v12:
time: 119 us; the launch traced here: 117 us
  waiting for transfers between devices  37 us (31%)
  starting transfers between devices  31 us (26%)
  matrix products  20.7 us (17%)
  local copies, waits for them, and re-layouts  18.6 us (16%)
  other arithmetic  8.76 us (7%)
    all_to_all x1, waiting for transfers between devices, local(): lax.all_to_all(result, 'member', split_axis=0, concat_axis=0, tiled=True)  20.7 us
    all_to_all x1, waiting for transfers between devices, local(): lax.all_to_all(payload, 'member', split_axis=0, concat_axis=0, tiled=True)  14.2 us
    all_to_all x1, starting transfers between devices, local(): lax.all_to_all(payload, 'member', split_axis=0, concat_axis=0, tiled=True)  12.2 us
    ppermute x1, starting transfers between devices, local(): own.append(lax.ppermute(weights, ('member', 'space'), perm))  8.83 us
    dot_general x1, matrix products, local(): jnp.einsum('rjk,rjx->kx', w_all, masked, preferred_element_type=jnp.float32)  7.81 us
    reshape x1, local copies, waits for them, and re-layouts, local(): returned = returned.reshape(n_member, local_members, tracers, own_cols)  4.85 us
    dot_general x1, matrix products, local(): jnp.einsum('dkti,cdi->ktc', returned, perm_mat, preferred_element_type=jn...  4.31 us
    reshape x1, local copies, waits for them, and re-layouts, local(): main = main.reshape(n_member, local_members, flat)  4.01 us
  transfers between devices with their start and end apart: 6, of which 3 were waited for; matrix products, arithmetic and copies ran while one was open for 21% of the time, Pallas kernels for 0%

profile of v12, /device:TPU:1, one launch (start us, length us, event | category | flops | bytes accessed | tf_op | source)
XLA Modules:
  0.0 116.9 jit_solution(10400516102230086528)
XLA Ops:
  0.6 8.8 %collective-permute-start.2 = (bf16[4,256,256]{2,1,0:T(8,128)(2,1)}, bf16[4,256,256]{2,1,0:T(8,128)(2,1)}, u32[]{:S(2)}, u32[]{:S(2)}) collective-permute-start(bf16[4,256,256]{2,1,0:T(8,128)(2,1)} %param.8), channel_id=1, source_target_pairs={{8,0},{9,1},{14,2},{15,3},{12,4},{13,5},{18,6},{19,7},{16,8},{17,9... | collective-permute-start | bytes 1572872 | tf_op jit(solution)/shard_map/ppermute | solution.py:60
  9.5 1.8 %fusion.62 = (bf16[2,256,256]{2,1,0:T(8,128)(2,1)}, bf16[2,256,256]{2,1,0:T(8,128)(2,1)}) fusion(bf16[4,256,256]{2,1,0:T(8,128)(2,1)} %param.8), kind=kLoop, calls=%fused_computation.115 | loop fusion | bytes 1048576 | tf_op jit(solution)/shard_map/slice | solution.py:56
  11.3 1.6 %collective-permute-start = (bf16[2,256,256]{2,1,0:T(8,128)(2,1)}, bf16[2,256,256]{2,1,0:T(8,128)(2,1)S(1)}, u32[]{:S(2)}, u32[]{:S(2)}) collective-permute-start(bf16[2,256,256]{2,1,0:T(8,128)(2,1)} %get-tuple-element.9), channel_id=1, source_target_pairs={{0,0},{1,1},{6,2},{7,3},{4,4},{5,5},{10,6},{11,7},{8,8},{9,9},{14,... | collective-permute-start | bytes 786440 | tf_op jit(solution)/shard_map/ppermute | solution.py:56
  12.9 3.6 %collective-permute-start.1 = (bf16[2,256,256]{2,1,0:T(8,128)(2,1)}, bf16[2,256,256]{2,1,0:T(8,128)(2,1)}, u32[]{:S(2)}, u32[]{:S(2)}) collective-permute-start(bf16[2,256,256]{2,1,0:T(8,128)(2,1)} %get-tuple-element.10), channel_id=1, source_target_pairs={{0,0},{1,1},{6,2},{7,3},{4,4},{5,5},{10,6},{11,7},{8,8},{9,9},{14,... | collective-permute-start | bytes 786440 | tf_op jit(solution)/shard_map/ppermute | solution.py:57
  17.2 1.2 reduce-window.6
  18.8 3.4 %convolution_bitcast_fusion = bf16[8,32,48,64]{3,2,1,0:T(8,128)(2,1)} fusion(bf16[32,48,512]{2,1,0:T(8,128)(2,1)S(1)} %copy-done, s32[8,64]{1,0:T(8,128)S(1)} %multiply_add_fusion, s32[512]{0:T(512)S(1)} %fusion.52), kind=kOutput, calls=%fused_computation.15 | convolution fusion | flops 805568512 | bytes 3149824 | tf_op jit(solution)/shard_map/jtc,cdi->djti/dot_general | solution.py:98
  22.4 4.0 %reshape.126 = bf16[8,32,3072]{2,1,0:T(8,128)(2,1)S(1)} reshape(bf16[8,32,48,64]{3,2,1,0:T(8,128)(2,1)} %convolution_bitcast_fusion) | data formatting | bytes 3145728 | tf_op jit(solution)/shard_map/reshape | solution.py:99
  26.4 1.5 %fusion.33 = (bf16[8,32,64]{2,1,0:T(8,128)(2,1)S(1)}, bf16[8,32,64]{2,1,0:T(8,128)(2,1)}, bf16[8,32,64]{2,1,0:T(8,128)(2,1)}) fusion(f32[512,32,1]{0,1,2:T(8,128)S(1)} %convolution_bitcast_fusion.3, s32[8,64]{1,0:T(8,128)S(1)} %multiply_add_fusion, s32[512]{0:T(512)S(1)} %fusion.52), kind=kOutput, calls=%fused_computation.44 | convolution fusion | flops 101040128 | bytes 167936 | tf_op jit(solution)/shard_map/jc,cdi->dji/dot_general | solution.py:94
  28.0 3.2 %concatenate.10 = bf16[8,32,3328]{2,1,0:T(8,128)(2,1)} concatenate(bf16[8,32,3072]{2,1,0:T(8,128)(2,1)S(1)} %reshape.126, bf16[8,32,64]{2,1,0:T(8,128)(2,1)} %get-tuple-element.13, bf16[8,32,64]{2,1,0:T(8,128)(2,1)} %get-tuple-element.12, bf16[8,32,64]{2,1,0:T(8,128)(2,1)S(1)} %get-tuple-element.11, bf16[8,32,64]{2,1,0:T(8,128)(2,1)S(1)} %broadcast_in_dim.44), dimensions={2} | concatenate | bytes 3407872 | tf_op jit(solution)/shard_map/concatenate | solution.py:103
  31.2 12.2 %all-to-all-start = ((bf16[8,32,3328]{2,1,0:T(8,128)(2,1)}), bf16[8,32,3328]{2,1,0:T(8,128)(2,1)S(1)}, u32[]{:S(2)}, u32[]{:S(2)}) async-start(bf16[8,32,3328]{2,1,0:T(8,128)(2,1)} %concatenate.10), calls=%async_computation | async-start | bytes 3407872 | tf_op jit(solution)/shard_map/all_to_all | solution.py:109
  43.4 1.0 maximum_bitcast_fusion
  45.2 2.1 %pad_maximum_fusion.1 = bf16[2,4,256,256]{3,2,1,0:T(8,128)(2,1)} fusion(bf16[1,4,256,256]{3,2,1,0:T(8,128)(2,1)} %bitcast.10, bf16[1,4,256,256]{3,2,1,0:T(8,128)(2,1)S(1)} %maximum_bitcast_fusion), kind=kLoop, calls=%fused_computation.25 | loop fusion | flops 524288 | bytes 2097152 | tf_op jit(solution)/shard_map/stack | solution.py:106
  48.8 2.1 %collective-permute-done.3 = bf16[2,4,256,256]{3,2,1,0:T(8,128)(2,1)} collective-permute-done((bf16[2,4,256,256]{3,2,1,0:T(8,128)(2,1)}, bf16[2,4,256,256]{3,2,1,0:T(8,128)(2,1)}, u32[]{:S(2)}, u32[]{:S(2)}) %collective-permute-start.3) | collective-permute-done | bytes 1048608 | tf_op jit(solution)/shard_map/ppermute | solution.py:107
  50.9 3.1 %pad_maximum_fusion = bf16[4,4,256,256]{3,2,1,0:T(8,128)(2,1)} fusion(bf16[2,4,256,256]{3,2,1,0:T(8,128)(2,1)} %collective-permute-done.3, bf16[1,4,256,256]{3,2,1,0:T(8,128)(2,1)} %bitcast.10, bf16[1,4,256,256]{3,2,1,0:T(8,128)(2,1)} %copy-done.2), kind=kLoop, calls=%fused_computation.14 | loop fusion | flops 2097152 | bytes 4194304 | tf_op jit(solution)/shard_map/concatenate | solution.py:108
  53.9 14.2 %all-to-all-done = bf16[8,32,3328]{2,1,0:T(8,128)(2,1)S(1)} async-done(((bf16[8,32,3328]{2,1,0:T(8,128)(2,1)}), bf16[8,32,3328]{2,1,0:T(8,128)(2,1)S(1)}, u32[]{:S(2)}, u32[]{:S(2)}) %all-to-all-start) | async-done | bytes 1703968 | tf_op jit(solution)/shard_map/all_to_all | solution.py:109
  68.5 1.6 %fusion.17 = bf16[256,3072]{1,0:T(8,128)(2,1)S(1)} fusion(f32[3072]{0:T(1024)S(1)} %broadcast_multiply_fusion, bf16[256,3328]{1,0:T(8,128)(2,1)S(1)} %bitcast.79, s32[3072]{0:T(1024)S(1)} %add_select_fusion, f32[256,256]{1,0:T(8,128)S(1)} %slice_convert_fusion), kind=kOutput, calls=%fused_computation.13 | convolution fusion | flops 607354880 | bytes 3563520 | tf_op jit(solution)/shard_map/dot_general | solution.py:116
  70.1 7.8 %fusion.14 = bf16[256,3072]{1,0:T(8,128)(2,1)} fusion(bf16[16,256,256]{2,1,0:T(8,128)(2,1)S(1)} %bitcast.80, pred[16,3072]{1,0:T(8,128)(4,1)S(1)} %tile.9, bf16[256,3072]{1,0:T(8,128)(2,1)S(1)} %fusion.17, f32[3072]{0:T(1024)S(1)} %broadcast_multiply_fusion), kind=kOutput, calls=%fused_computation.12 | convolution fusion | flops 6457393152 | bytes 5304320 | tf_op jit(solution)/shard_map/rjk,rjx->kx/dot_general | solution.py:122
  77.9 3.9 %all-to-all-start.1 = ((bf16[8,32,3072]{2,1,0:T(8,128)(2,1)}), bf16[8,32,3072]{2,1,0:T(8,128)(2,1)S(1)}, u32[]{:S(2)}, u32[]{:S(2)}) async-start(bf16[8,32,3072]{2,1,0:T(8,128)(2,1)} %bitcast.81), calls=%async_computation.1 | async-start | bytes 3145728 | tf_op jit(solution)/shard_map/all_to_all | solution.py:126
  81.8 1.3 %gather_fusion = s32[128]{0:T(128)S(1)} fusion(s32[512]{0:T(512)S(1)} %fusion.52, s32[1024]{0:T(1024)S(1)} %pad_clamp_fusion), kind=kCustom, calls=%fused_computation | custom fusion | bytes 1536 | tf_op jit(solution)/shard_map/jit(_take)/gather | solution.py:131
  83.1 20.7 %all-to-all-done.1 = bf16[8,32,3072]{2,1,0:T(8,128)(2,1)S(1)} async-done(((bf16[8,32,3072]{2,1,0:T(8,128)(2,1)}), bf16[8,32,3072]{2,1,0:T(8,128)(2,1)S(1)}, u32[]{:S(2)}, u32[]{:S(2)}) %all-to-all-start.1) | async-done | bytes 1572896 | tf_op jit(solution)/shard_map/all_to_all | solution.py:126
  103.8 2.0 %copy.15 = bf16[8,32,3072]{2,0,1:T(8,128)(2,1)} copy(bf16[8,32,3072]{2,1,0:T(8,128)(2,1)S(1)} %all-to-all-done.1) | data formatting | bytes 3145728 | tf_op jit(solution)/shard_map/all_to_all | solution.py:126
  105.8 4.9 %reshape.131 = bf16[8,32,48,64]{3,2,0,1:T(8,128)(2,1)} reshape(bf16[8,32,3072]{2,0,1:T(8,128)(2,1)} %copy.15) | data formatting | bytes 3145728 | tf_op jit(solution)/shard_map/reshape | solution.py:127
  110.6 4.3 %convolution_bitcast_fusion.1 = bf16[32,48,512]{2,1,0:T(8,128)(2,1)} fusion(bf16[8,32,48,64]{3,2,0,1:T(8,128)(2,1)} %reshape.131, s32[8,64]{1,0:T(8,128)S(1)} %multiply_add_fusion, s32[512]{0:T(512)S(1)} %fusion.52), kind=kOutput, calls=%fused_computation.21 | convolution fusion | flops 805568512 | bytes 3149824 | tf_op jit(solution)/shard_map/dkti,cdi->ktc/dot_general | solution.py:128
  115.8 1.1 fusion.59
  (44 shorter events, 4.8 us)
Async XLA Ops:
  0.6 18.2 %copy-start = (bf16[32,48,512]{2,1,0:T(8,128)(2,1)S(1)}, bf16[32,48,512]{2,1,0:T(8,128)(2,1)}, u32[]{:S(2)}) copy-start(bf16[32,48,512]{2,1,0:T(8,128)(2,1)} %param.6) | copy-start | bytes 4718596
  0.6 43.7 %collective-permute-start.2 = (bf16[4,256,256]{2,1,0:T(8,128)(2,1)}, bf16[4,256,256]{2,1,0:T(8,128)(2,1)}, u32[]{:S(2)}, u32[]{:S(2)}) collective-permute-start(bf16[4,256,256]{2,1,0:T(8,128)(2,1)} %param.8), channel_id=1, source_target_pairs={{8,0},{9,1},{14,2},{15,3},{12,4},{13,5},{18,6},{19,7},{16,8},{17,9... | collective-permute-start | bytes 1572872 | tf_op jit(solution)/shard_map/ppermute | solution.py:60
  11.3 19.9 %collective-permute-start = (bf16[2,256,256]{2,1,0:T(8,128)(2,1)}, bf16[2,256,256]{2,1,0:T(8,128)(2,1)S(1)}, u32[]{:S(2)}, u32[]{:S(2)}) collective-permute-start(bf16[2,256,256]{2,1,0:T(8,128)(2,1)} %get-tuple-element.9), channel_id=1, source_target_pairs={{0,0},{1,1},{6,2},{7,3},{4,4},{5,5},{10,6},{11,7},{8,8},{9,9},{14,... | collective-permute-start | bytes 786440 | tf_op jit(solution)/shard_map/ppermute | solution.py:56
  12.9 30.4 %collective-permute-start.1 = (bf16[2,256,256]{2,1,0:T(8,128)(2,1)}, bf16[2,256,256]{2,1,0:T(8,128)(2,1)}, u32[]{:S(2)}, u32[]{:S(2)}) collective-permute-start(bf16[2,256,256]{2,1,0:T(8,128)(2,1)} %get-tuple-element.10), channel_id=1, source_target_pairs={{0,0},{1,1},{6,2},{7,3},{4,4},{5,5},{10,6},{11,7},{8,8},{9,9},{14,... | collective-permute-start | bytes 786440 | tf_op jit(solution)/shard_map/ppermute | solution.py:57
  18.8 3.4 %copy-start.4 = (f32[32,128]{1,0:T(8,128)S(1)}, f32[32,128]{1,0:T(8,128)}, u32[]{:S(2)}) copy-start(f32[32,128]{1,0:T(8,128)} %param.7) | copy-start | bytes 49156
  18.8 3.4 %copy-start.5 = (s32[512]{0:T(512)S(1)}, s32[512]{0:T(512)}, u32[]{:S(2)}) copy-start(s32[512]{0:T(512)} %param.9) | copy-start | bytes 6148
  31.2 37.0 %all-to-all-start = ((bf16[8,32,3328]{2,1,0:T(8,128)(2,1)}), bf16[8,32,3328]{2,1,0:T(8,128)(2,1)S(1)}, u32[]{:S(2)}, u32[]{:S(2)}) async-start(bf16[8,32,3328]{2,1,0:T(8,128)(2,1)} %concatenate.10), calls=%async_computation | async-start | bytes 3407872 | tf_op jit(solution)/shard_map/all_to_all | solution.py:109
  44.4 0.8 copy-start.2
  47.3 3.6 %collective-permute-start.3 = (bf16[2,4,256,256]{3,2,1,0:T(8,128)(2,1)}, bf16[2,4,256,256]{3,2,1,0:T(8,128)(2,1)}, u32[]{:S(2)}, u32[]{:S(2)}) collective-permute-start(bf16[2,4,256,256]{3,2,1,0:T(8,128)(2,1)} %pad_maximum_fusion.1), channel_id=1, source_target_pairs={{0,1},{1,0},{2,3},{3,2},{4,5},{5,4},{6,7},{7,6},{8,9},{9,8},{10,11... | collective-permute-start | bytes 3145736 | tf_op jit(solution)/shard_map/ppermute | solution.py:107
  68.4 1.6 %copy-start.3 = (bf16[4,4,256,256]{3,2,1,0:T(8,128)(2,1)S(1)}, bf16[4,4,256,256]{3,2,1,0:T(8,128)(2,1)}, u32[]{:S(2)}) copy-start(bf16[4,4,256,256]{3,2,1,0:T(8,128)(2,1)} %pad_maximum_fusion) | copy-start | bytes 6291460
  77.9 3.9 %copy-start.6 = (s32[128]{0:T(128)S(1)}, s32[128]{0:T(128)}, u32[]{:S(2)}) copy-start(s32[128]{0:T(128)} %param.11) | copy-start | bytes 1540
  77.9 25.9 %all-to-all-start.1 = ((bf16[8,32,3072]{2,1,0:T(8,128)(2,1)}), bf16[8,32,3072]{2,1,0:T(8,128)(2,1)S(1)}, u32[]{:S(2)}, u32[]{:S(2)}) async-start(bf16[8,32,3072]{2,1,0:T(8,128)(2,1)} %bitcast.81), calls=%async_computation.1 | async-start | bytes 3145728 | tf_op jit(solution)/shard_map/all_to_all | solution.py:126
  110.6 4.3 %copy-start.1 = (bf16[8,32,48,64]{3,2,0,1:T(8,128)(2,1)S(1)}, bf16[8,32,48,64]{3,2,0,1:T(8,128)(2,1)}, u32[]{:S(2)}) copy-start(bf16[8,32,48,64]{3,2,0,1:T(8,128)(2,1)} %reshape.131) | copy-start | bytes 4718596
  115.0 0.8 copy-start.7

commit v13 on v12

--- a/solution.py
+++ b/solution.py
@@ -125,13 +125,16 @@
     result = result.reshape(n_member, local_members, flat)
     returned = lax.all_to_all(result, "member", split_axis=0, concat_axis=0, tiled=True)
     returned = returned.reshape(n_member, local_members, tracers, own_cols)
-    analysis = jnp.einsum("dkti,cdi->ktc", returned, perm_mat, preferred_element_type=jnp.bfloat16)
+    rows = returned.reshape(n_member, local_members * tracers, own_cols)
+    analysis = jnp.einsum("dni,cdi->nc", rows, perm_mat, preferred_element_type=jnp.bfloat16)
+    analysis = analysis.reshape(local_members, tracers, columns)
 
     local_index = obs_cols - me_space * columns
     obs_pos = jnp.take(position, local_index)
     obs_mat = (pos_iota[:, None] == obs_pos[None, :]).astype(jnp.bfloat16)
     obs_mat = obs_mat.reshape(n_member, own_cols, obs_cols.shape[0])
-    picked = jnp.einsum("dkti,dio->kto", returned, obs_mat, preferred_element_type=jnp.float32)
+    picked = jnp.einsum("dni,dio->no", rows, obs_mat, preferred_element_type=jnp.float32)
+    picked = picked.reshape(local_members, tracers, obs_cols.shape[0])
     obs_analysis = jnp.einsum("t,kto->ko", extinction, picked, precision=lax.Precision.HIGHEST)
     return (analysis, obs_analysis)
 

time: 119 us -> 115 us (0.966)
  local copies, waits for them, and re-layouts: 18.6 us -> 15 us
    reshape x1 -> x0, local copies, waits for them, and re-layouts: 4.85 us -> none  [local(): returned = returned.reshape(n_member, local_members, tracers, own_cols)]
    another operation x1 -> x2, local copies, waits for them, and re-layouts: 0.01 us -> 3.28 us  [the longest x1 3.27 us: local(): rows = returned.reshape(n_member, local_members * tracers, own_cols)]
    all_to_all x1 -> x0, local copies, waits for them, and re-layouts: 2.01 us -> none  [local(): lax.all_to_all(result, 'member', split_axis=0, concat_axis=0, tiled=True)]
  transfers between devices with their start and end apart: 6 -> 6, of which waited for: 3 -> 3; matrix products, arithmetic and copies ran while one was open for 21% -> 22% of each run, Pallas kernels for 0% -> 0%
where the time goes in v13:
time: 115 us; the launch traced here: 113 us
  waiting for transfers between devices  37 us (32%)
  starting transfers between devices  31 us (27%)
  matrix products  20.7 us (18%)
  local copies, waits for them, and re-layouts  15 us (13%)
  other arithmetic  8.76 us (8%)
    all_to_all x1, waiting for transfers between devices, local(): lax.all_to_all(result, 'member', split_axis=0, concat_axis=0, tiled=True)  20.7 us
    all_to_all x1, waiting for transfers between devices, local(): lax.all_to_all(payload, 'member', split_axis=0, concat_axis=0, tiled=True)  14.2 us
    all_to_all x1, starting transfers between devices, local(): lax.all_to_all(payload, 'member', split_axis=0, concat_axis=0, tiled=True)  12.2 us
    ppermute x1, starting transfers between devices, local(): own.append(lax.ppermute(weights, ('member', 'space'), perm))  8.83 us
    dot_general x1, matrix products, local(): jnp.einsum('rjk,rjx->kx', w_all, masked, preferred_element_type=jnp.float32)  7.81 us
    dot_general x1, matrix products, local(): jnp.einsum('dni,cdi->nc', rows, perm_mat, preferred_element_type=jnp.bflo...  4.31 us
    reshape x1, local copies, waits for them, and re-layouts, local(): main = main.reshape(n_member, local_members, flat)  4.01 us
    all_to_all x1, starting transfers between devices, local(): lax.all_to_all(result, 'member', split_axis=0, concat_axis=0, tiled=True)  3.89 us
  transfers between devices with their start and end apart: 6, of which 3 were waited for; matrix products, arithmetic and copies ran while one was open for 22% of the time, Pallas kernels for 0%

profile of v13, /device:TPU:1, one launch (start us, length us, event | category | flops | bytes accessed | tf_op | source)
XLA Modules:
  0.0 113.3 jit_solution(1752070500437996995)
XLA Ops:
  0.6 8.8 %collective-permute-start.2 = (bf16[4,256,256]{2,1,0:T(8,128)(2,1)}, bf16[4,256,256]{2,1,0:T(8,128)(2,1)}, u32[]{:S(2)}, u32[]{:S(2)}) collective-permute-start(bf16[4,256,256]{2,1,0:T(8,128)(2,1)} %param.8), channel_id=1, source_target_pairs={{8,0},{9,1},{14,2},{15,3},{12,4},{13,5},{18,6},{19,7},{16,8},{17,9... | collective-permute-start | bytes 1572872 | tf_op jit(solution)/shard_map/ppermute | solution.py:60
  9.5 1.8 %fusion.62 = (bf16[2,256,256]{2,1,0:T(8,128)(2,1)}, bf16[2,256,256]{2,1,0:T(8,128)(2,1)}) fusion(bf16[4,256,256]{2,1,0:T(8,128)(2,1)} %param.8), kind=kLoop, calls=%fused_computation.114 | loop fusion | bytes 1048576 | tf_op jit(solution)/shard_map/slice | solution.py:56
  11.3 1.6 %collective-permute-start = (bf16[2,256,256]{2,1,0:T(8,128)(2,1)}, bf16[2,256,256]{2,1,0:T(8,128)(2,1)S(1)}, u32[]{:S(2)}, u32[]{:S(2)}) collective-permute-start(bf16[2,256,256]{2,1,0:T(8,128)(2,1)} %get-tuple-element.9), channel_id=1, source_target_pairs={{0,0},{1,1},{6,2},{7,3},{4,4},{5,5},{10,6},{11,7},{8,8},{9,9},{14,... | collective-permute-start | bytes 786440 | tf_op jit(solution)/shard_map/ppermute | solution.py:56
  12.9 3.6 %collective-permute-start.1 = (bf16[2,256,256]{2,1,0:T(8,128)(2,1)}, bf16[2,256,256]{2,1,0:T(8,128)(2,1)}, u32[]{:S(2)}, u32[]{:S(2)}) collective-permute-start(bf16[2,256,256]{2,1,0:T(8,128)(2,1)} %get-tuple-element.10), channel_id=1, source_target_pairs={{0,0},{1,1},{6,2},{7,3},{4,4},{5,5},{10,6},{11,7},{8,8},{9,9},{14,... | collective-permute-start | bytes 786440 | tf_op jit(solution)/shard_map/ppermute | solution.py:57
  17.2 1.2 %reduce-window.6 = s32[32,4,128]{2,0,1:T(8,128)S(1)} reduce-window(s32[32,4,128]{2,0,1:T(8,128)S(1)} %fusion.41, s32[]{:T(128)} %constant.139.clone.1), window={size=1x1x128 pad=0_0x0_0x127_0}, to_apply=%region_0.1 | reduce-window | flops 2080768 | bytes 131076 | tf_op jit(solution)/shard_map/reduce-window
  18.8 3.4 %convolution_bitcast_fusion = bf16[8,32,48,64]{3,2,1,0:T(8,128)(2,1)} fusion(bf16[32,48,512]{2,1,0:T(8,128)(2,1)S(1)} %copy-done, s32[8,64]{1,0:T(8,128)S(1)} %multiply_add_fusion, s32[512]{0:T(512)S(1)} %fusion.52), kind=kOutput, calls=%fused_computation.15 | convolution fusion | flops 805568512 | bytes 3149824 | tf_op jit(solution)/shard_map/jtc,cdi->djti/dot_general | solution.py:98
  22.4 4.0 %reshape.127 = bf16[8,32,3072]{2,1,0:T(8,128)(2,1)S(1)} reshape(bf16[8,32,48,64]{3,2,1,0:T(8,128)(2,1)} %convolution_bitcast_fusion) | data formatting | bytes 3145728 | tf_op jit(solution)/shard_map/reshape | solution.py:99
  26.4 1.5 %fusion.33 = (bf16[8,32,64]{2,1,0:T(8,128)(2,1)S(1)}, bf16[8,32,64]{2,1,0:T(8,128)(2,1)}, bf16[8,32,64]{2,1,0:T(8,128)(2,1)}) fusion(f32[512,32,1]{0,1,2:T(8,128)S(1)} %convolution_bitcast_fusion.3, s32[8,64]{1,0:T(8,128)S(1)} %multiply_add_fusion, s32[512]{0:T(512)S(1)} %fusion.52), kind=kOutput, calls=%fused_computation.43 | convolution fusion | flops 101040128 | bytes 167936 | tf_op jit(solution)/shard_map/jc,cdi->dji/dot_general | solution.py:94
  28.0 3.2 %concatenate.10 = bf16[8,32,3328]{2,1,0:T(8,128)(2,1)} concatenate(bf16[8,32,3072]{2,1,0:T(8,128)(2,1)S(1)} %reshape.127, bf16[8,32,64]{2,1,0:T(8,128)(2,1)} %get-tuple-element.13, bf16[8,32,64]{2,1,0:T(8,128)(2,1)} %get-tuple-element.12, bf16[8,32,64]{2,1,0:T(8,128)(2,1)S(1)} %get-tuple-element.11, bf16[8,32,64]{2,1,0:T(8,128)(2,1)S(1)} %broadcast_in_dim.44), dimensions={2} | concatenate | bytes 3407872 | tf_op jit(solution)/shard_map/concatenate | solution.py:103
  31.2 12.2 %all-to-all-start = ((bf16[8,32,3328]{2,1,0:T(8,128)(2,1)}), bf16[8,32,3328]{2,1,0:T(8,128)(2,1)S(1)}, u32[]{:S(2)}, u32[]{:S(2)}) async-start(bf16[8,32,3328]{2,1,0:T(8,128)(2,1)} %concatenate.10), calls=%async_computation | async-start | bytes 3407872 | tf_op jit(solution)/shard_map/all_to_all | solution.py:109
  43.4 1.0 maximum_bitcast_fusion
  45.2 2.1 %pad_maximum_fusion.1 = bf16[2,4,256,256]{3,2,1,0:T(8,128)(2,1)} fusion(bf16[1,4,256,256]{3,2,1,0:T(8,128)(2,1)} %bitcast.10, bf16[1,4,256,256]{3,2,1,0:T(8,128)(2,1)S(1)} %maximum_bitcast_fusion), kind=kLoop, calls=%fused_computation.24 | loop fusion | flops 524288 | bytes 2097152 | tf_op jit(solution)/shard_map/stack | solution.py:106
  47.3 1.0 collective-permute-start.3
  48.8 2.1 %collective-permute-done.3 = bf16[2,4,256,256]{3,2,1,0:T(8,128)(2,1)} collective-permute-done((bf16[2,4,256,256]{3,2,1,0:T(8,128)(2,1)}, bf16[2,4,256,256]{3,2,1,0:T(8,128)(2,1)}, u32[]{:S(2)}, u32[]{:S(2)}) %collective-permute-start.3) | collective-permute-done | bytes 1048608 | tf_op jit(solution)/shard_map/ppermute | solution.py:107
  50.9 3.1 %pad_maximum_fusion = bf16[4,4,256,256]{3,2,1,0:T(8,128)(2,1)} fusion(bf16[2,4,256,256]{3,2,1,0:T(8,128)(2,1)} %collective-permute-done.3, bf16[1,4,256,256]{3,2,1,0:T(8,128)(2,1)} %bitcast.10, bf16[1,4,256,256]{3,2,1,0:T(8,128)(2,1)} %copy-done.2), kind=kLoop, calls=%fused_computation.14 | loop fusion | flops 2097152 | bytes 4194304 | tf_op jit(solution)/shard_map/concatenate | solution.py:108
  53.9 14.2 %all-to-all-done = bf16[8,32,3328]{2,1,0:T(8,128)(2,1)S(1)} async-done(((bf16[8,32,3328]{2,1,0:T(8,128)(2,1)}), bf16[8,32,3328]{2,1,0:T(8,128)(2,1)S(1)}, u32[]{:S(2)}, u32[]{:S(2)}) %all-to-all-start) | async-done | bytes 1703968 | tf_op jit(solution)/shard_map/all_to_all | solution.py:109
  68.5 1.6 %fusion.17 = bf16[256,3072]{1,0:T(8,128)(2,1)S(1)} fusion(f32[3072]{0:T(1024)S(1)} %broadcast_multiply_fusion, bf16[256,3328]{1,0:T(8,128)(2,1)S(1)} %bitcast.89, s32[3072]{0:T(1024)S(1)} %add_select_fusion, f32[256,256]{1,0:T(8,128)S(1)} %slice_convert_fusion), kind=kOutput, calls=%fused_computation.13 | convolution fusion | flops 607354880 | bytes 3563520 | tf_op jit(solution)/shard_map/dot_general | solution.py:116
  70.1 7.8 %fusion.14 = bf16[256,3072]{1,0:T(8,128)(2,1)} fusion(bf16[16,256,256]{2,1,0:T(8,128)(2,1)S(1)} %bitcast.90, pred[16,3072]{1,0:T(8,128)(4,1)S(1)} %tile.9, bf16[256,3072]{1,0:T(8,128)(2,1)S(1)} %fusion.17, f32[3072]{0:T(1024)S(1)} %broadcast_multiply_fusion), kind=kOutput, calls=%fused_computation.12 | convolution fusion | flops 6457393152 | bytes 5304320 | tf_op jit(solution)/shard_map/rjk,rjx->kx/dot_general | solution.py:122
  77.9 3.9 %all-to-all-start.1 = ((bf16[8,32,3072]{2,1,0:T(8,128)(2,1)}), bf16[8,32,3072]{2,1,0:T(8,128)(2,1)S(1)}, u32[]{:S(2)}, u32[]{:S(2)}) async-start(bf16[8,32,3072]{2,1,0:T(8,128)(2,1)} %bitcast.91), calls=%async_computation.1 | async-start | bytes 3145728 | tf_op jit(solution)/shard_map/all_to_all | solution.py:126
  81.8 1.3 %gather_fusion = s32[128]{0:T(128)S(1)} fusion(s32[512]{0:T(512)S(1)} %fusion.52, s32[1024]{0:T(1024)S(1)} %pad_clamp_fusion), kind=kCustom, calls=%fused_computation | custom fusion | bytes 1536 | tf_op jit(solution)/shard_map/jit(_take)/gather | solution.py:133
  83.1 20.7 %all-to-all-done.1 = bf16[8,32,3072]{2,1,0:T(8,128)(2,1)S(1)} async-done(((bf16[8,32,3072]{2,1,0:T(8,128)(2,1)}), bf16[8,32,3072]{2,1,0:T(8,128)(2,1)S(1)}, u32[]{:S(2)}, u32[]{:S(2)}) %all-to-all-start.1) | async-done | bytes 1572896 | tf_op jit(solution)/shard_map/all_to_all | solution.py:126
  103.8 3.3 %reshape_reshape.3 = bf16[8,1536,64]{2,1,0:T(8,128)(2,1)} reshape(bf16[8,32,3072]{2,1,0:T(8,128)(2,1)S(1)} %all-to-all-done.1) | data formatting | bytes 3145728 | tf_op jit(solution)/shard_map/reshape;reshape | solution.py:128
  107.1 4.3 %convolution_bitcast_fusion.1 = bf16[32,48,512]{2,1,0:T(8,128)(2,1)} fusion(bf16[32,48,8,64]{3,1,0,2:T(8,128)(2,1)} %bitcast.85, s32[8,64]{1,0:T(8,128)S(1)} %multiply_add_fusion, s32[512]{0:T(512)S(1)} %fusion.52), kind=kOutput, calls=%fused_computation.17 | convolution fusion | flops 805568512 | bytes 3149824 | tf_op jit(solution)/shard_map/dni,cdi->nc/dot_general | solution.py:129
  112.2 1.1 fusion.59
  (43 shorter events, 3.8 us)
Async XLA Ops:
  0.6 18.2 %copy-start = (bf16[32,48,512]{2,1,0:T(8,128)(2,1)S(1)}, bf16[32,48,512]{2,1,0:T(8,128)(2,1)}, u32[]{:S(2)}) copy-start(bf16[32,48,512]{2,1,0:T(8,128)(2,1)} %param.6) | copy-start | bytes 4718596
  0.6 43.7 %collective-permute-start.2 = (bf16[4,256,256]{2,1,0:T(8,128)(2,1)}, bf16[4,256,256]{2,1,0:T(8,128)(2,1)}, u32[]{:S(2)}, u32[]{:S(2)}) collective-permute-start(bf16[4,256,256]{2,1,0:T(8,128)(2,1)} %param.8), channel_id=1, source_target_pairs={{8,0},{9,1},{14,2},{15,3},{12,4},{13,5},{18,6},{19,7},{16,8},{17,9... | collective-permute-start | bytes 1572872 | tf_op jit(solution)/shard_map/ppermute | solution.py:60
  11.3 19.9 %collective-permute-start = (bf16[2,256,256]{2,1,0:T(8,128)(2,1)}, bf16[2,256,256]{2,1,0:T(8,128)(2,1)S(1)}, u32[]{:S(2)}, u32[]{:S(2)}) collective-permute-start(bf16[2,256,256]{2,1,0:T(8,128)(2,1)} %get-tuple-element.9), channel_id=1, source_target_pairs={{0,0},{1,1},{6,2},{7,3},{4,4},{5,5},{10,6},{11,7},{8,8},{9,9},{14,... | collective-permute-start | bytes 786440 | tf_op jit(solution)/shard_map/ppermute | solution.py:56
  12.9 30.4 %collective-permute-start.1 = (bf16[2,256,256]{2,1,0:T(8,128)(2,1)}, bf16[2,256,256]{2,1,0:T(8,128)(2,1)}, u32[]{:S(2)}, u32[]{:S(2)}) collective-permute-start(bf16[2,256,256]{2,1,0:T(8,128)(2,1)} %get-tuple-element.10), channel_id=1, source_target_pairs={{0,0},{1,1},{6,2},{7,3},{4,4},{5,5},{10,6},{11,7},{8,8},{9,9},{14,... | collective-permute-start | bytes 786440 | tf_op jit(solution)/shard_map/ppermute | solution.py:57
  18.8 3.4 %copy-start.4 = (f32[32,128]{1,0:T(8,128)S(1)}, f32[32,128]{1,0:T(8,128)}, u32[]{:S(2)}) copy-start(f32[32,128]{1,0:T(8,128)} %param.7) | copy-start | bytes 49156
  18.8 3.4 %copy-start.5 = (s32[512]{0:T(512)S(1)}, s32[512]{0:T(512)}, u32[]{:S(2)}) copy-start(s32[512]{0:T(512)} %param.9) | copy-start | bytes 6148
  31.2 37.0 %all-to-all-start = ((bf16[8,32,3328]{2,1,0:T(8,128)(2,1)}), bf16[8,32,3328]{2,1,0:T(8,128)(2,1)S(1)}, u32[]{:S(2)}, u32[]{:S(2)}) async-start(bf16[8,32,3328]{2,1,0:T(8,128)(2,1)} %concatenate.10), calls=%async_computation | async-start | bytes 3407872 | tf_op jit(solution)/shard_map/all_to_all | solution.py:109
  44.4 0.8 copy-start.2
  47.3 3.6 %collective-permute-start.3 = (bf16[2,4,256,256]{3,2,1,0:T(8,128)(2,1)}, bf16[2,4,256,256]{3,2,1,0:T(8,128)(2,1)}, u32[]{:S(2)}, u32[]{:S(2)}) collective-permute-start(bf16[2,4,256,256]{3,2,1,0:T(8,128)(2,1)} %pad_maximum_fusion.1), channel_id=1, source_target_pairs={{0,1},{1,0},{2,3},{3,2},{4,5},{5,4},{6,7},{7,6},{8,9},{9,8},{10,11... | collective-permute-start | bytes 3145736 | tf_op jit(solution)/shard_map/ppermute | solution.py:107
  68.4 1.6 %copy-start.3 = (bf16[4,4,256,256]{3,2,1,0:T(8,128)(2,1)S(1)}, bf16[4,4,256,256]{3,2,1,0:T(8,128)(2,1)}, u32[]{:S(2)}) copy-start(bf16[4,4,256,256]{3,2,1,0:T(8,128)(2,1)} %pad_maximum_fusion) | copy-start | bytes 6291460
  77.9 3.9 %copy-start.6 = (s32[128]{0:T(128)S(1)}, s32[128]{0:T(128)}, u32[]{:S(2)}) copy-start(s32[128]{0:T(128)} %param.11) | copy-start | bytes 1540
  77.9 25.9 %all-to-all-start.1 = ((bf16[8,32,3072]{2,1,0:T(8,128)(2,1)}), bf16[8,32,3072]{2,1,0:T(8,128)(2,1)S(1)}, u32[]{:S(2)}, u32[]{:S(2)}) async-start(bf16[8,32,3072]{2,1,0:T(8,128)(2,1)} %bitcast.91), calls=%async_computation.1 | async-start | bytes 3145728 | tf_op jit(solution)/shard_map/all_to_all | solution.py:126
  107.1 4.3 %copy-start.1 = (bf16[8,1536,64]{2,1,0:T(8,128)(2,1)S(1)}, bf16[8,1536,64]{2,1,0:T(8,128)(2,1)}, u32[]{:S(2)}) copy-start(bf16[8,1536,64]{2,1,0:T(8,128)(2,1)} %reshape_reshape.3) | copy-start | bytes 4718596
  111.4 0.8 copy-start.7

commit v14 on v13

--- a/solution.py
+++ b/solution.py
@@ -52,7 +52,7 @@
                 perm.append((m * n_space + src, m * n_space + s))
         assert len({src for src, _ in perm}) == len(perm)
         if a == 0:
-            half_reg = reg_count // 2
+            half_reg = 1
             first = lax.ppermute(weights[:half_reg], ("member", "space"), perm)
             rest = lax.ppermute(weights[half_reg:], ("member", "space"), perm)
             own.append(None)

time: 115 us -> 115 us (level)
  starting transfers between devices: 31 us -> 26.9 us
  waiting for transfers between devices: 37 us -> 40.7 us
    all_to_all x1, starting transfers between devices: 12.2 us -> 7.4 us  [local(): lax.all_to_all(payload, 'member', split_axis=0, concat_axis=0, tiled=True)]
    all_to_all x1, waiting for transfers between devices: 14.2 us -> 17.7 us  [local(): lax.all_to_all(payload, 'member', split_axis=0, concat_axis=0, tiled=True)]
    slice x1 -> x2, local copies, waits for them, and re-layouts: 0.22 us -> 1.99 us  [the longest x1 1.77 us: local(): rest = lax.ppermute(weights[half_reg:], ('member', 'space'), perm)]
where the time goes in v14:
time: 115 us; the launch traced here: 114 us
  waiting for transfers between devices  40.7 us (35%)
  starting transfers between devices  26.9 us (23%)
  matrix products  20.7 us (18%)
  local copies, waits for them, and re-layouts  15.9 us (14%)
  other arithmetic  8.81 us (8%)
    all_to_all x1, waiting for transfers between devices, local(): lax.all_to_all(result, 'member', split_axis=0, concat_axis=0, tiled=True)  20.8 us
    all_to_all x1, waiting for transfers between devices, local(): lax.all_to_all(payload, 'member', split_axis=0, concat_axis=0, tiled=True)  17.7 us
    ppermute x1, starting transfers between devices, local(): own.append(lax.ppermute(weights, ('member', 'space'), perm))  8.83 us
    dot_general x1, matrix products, local(): jnp.einsum('rjk,rjx->kx', w_all, masked, preferred_element_type=jnp.float32)  7.81 us
    all_to_all x1, starting transfers between devices, local(): lax.all_to_all(payload, 'member', split_axis=0, concat_axis=0, tiled=True)  7.4 us
    ppermute x1, starting transfers between devices, local(): rest = lax.ppermute(weights[half_reg:], ('member', 'space'), perm)  4.47 us
    dot_general x1, matrix products, local(): jnp.einsum('dni,cdi->nc', rows, perm_mat, preferred_element_type=jnp.bflo...  4.31 us
    reshape x1, local copies, waits for them, and re-layouts, local(): main = main.reshape(n_member, local_members, flat)  4.03 us
  transfers between devices with their start and end apart: 6, of which 3 were waited for; matrix products, arithmetic and copies ran while one was open for 22% of the time, Pallas kernels for 0%

profile of v14, /device:TPU:1, one launch (start us, length us, event | category | flops | bytes accessed | tf_op | source)
XLA Modules:
  0.0 113.9 jit_solution(5070638891695468489)
XLA Ops:
  0.6 8.8 %collective-permute-start.2 = (bf16[4,256,256]{2,1,0:T(8,128)(2,1)}, bf16[4,256,256]{2,1,0:T(8,128)(2,1)}, u32[]{:S(2)}, u32[]{:S(2)}) collective-permute-start(bf16[4,256,256]{2,1,0:T(8,128)(2,1)} %param.8), channel_id=1, source_target_pairs={{8,0},{9,1},{14,2},{15,3},{12,4},{13,5},{18,6},{19,7},{16,8},{17,9... | collective-permute-start | bytes 1572872 | tf_op jit(solution)/shard_map/ppermute | solution.py:60
  9.5 0.9 slice.29
  11.1 1.8 %slice.31 = bf16[3,256,256]{2,1,0:T(8,128)(2,1)} slice(bf16[4,256,256]{2,1,0:T(8,128)(2,1)} %param.8), slice={[1:4], [0:256], [0:256]} | slice | bytes 786432 | tf_op jit(solution)/shard_map/slice | solution.py:57
  12.9 4.5 %collective-permute-start.1 = (bf16[3,256,256]{2,1,0:T(8,128)(2,1)}, bf16[3,256,256]{2,1,0:T(8,128)(2,1)}, u32[]{:S(2)}, u32[]{:S(2)}) collective-permute-start(bf16[3,256,256]{2,1,0:T(8,128)(2,1)} %slice.31), channel_id=1, source_target_pairs={{0,0},{1,1},{6,2},{7,3},{4,4},{5,5},{10,6},{11,7},{8,8},{9,9},{14,... | collective-permute-start | bytes 1179656 | tf_op jit(solution)/shard_map/ppermute | solution.py:57
  18.1 1.2 %reduce-window.6 = s32[32,4,128]{2,0,1:T(8,128)S(1)} reduce-window(s32[32,4,128]{2,0,1:T(8,128)S(1)} %fusion.41, s32[]{:T(128)} %constant.139.clone.1), window={size=1x1x128 pad=0_0x0_0x127_0}, to_apply=%region_0.1 | reduce-window | flops 2080768 | bytes 131076 | tf_op jit(solution)/shard_map/reduce-window
  19.7 3.4 %convolution_bitcast_fusion = bf16[8,32,48,64]{3,2,1,0:T(8,128)(2,1)} fusion(bf16[32,48,512]{2,1,0:T(8,128)(2,1)S(1)} %copy-done, s32[8,64]{1,0:T(8,128)S(1)} %multiply_add_fusion, s32[512]{0:T(512)S(1)} %fusion.52), kind=kOutput, calls=%fused_computation.15 | convolution fusion | flops 805568512 | bytes 3149824 | tf_op jit(solution)/shard_map/jtc,cdi->djti/dot_general | solution.py:98
  23.0 4.0 %reshape.127 = bf16[8,32,3072]{2,1,0:T(8,128)(2,1)S(1)} reshape(bf16[8,32,48,64]{3,2,1,0:T(8,128)(2,1)} %convolution_bitcast_fusion) | data formatting | bytes 3145728 | tf_op jit(solution)/shard_map/reshape | solution.py:99
  27.3 1.5 %fusion.33 = (bf16[8,32,64]{2,1,0:T(8,128)(2,1)S(1)}, bf16[8,32,64]{2,1,0:T(8,128)(2,1)}, bf16[8,32,64]{2,1,0:T(8,128)(2,1)}) fusion(f32[512,32,1]{0,1,2:T(8,128)S(1)} %convolution_bitcast_fusion.3, s32[8,64]{1,0:T(8,128)S(1)} %multiply_add_fusion, s32[512]{0:T(512)S(1)} %fusion.52), kind=kOutput, calls=%fused_computation.43 | convolution fusion | flops 101040128 | bytes 167936 | tf_op jit(solution)/shard_map/jc,cdi->dji/dot_general | solution.py:94
  28.9 3.2 %concatenate.10 = bf16[8,32,3328]{2,1,0:T(8,128)(2,1)} concatenate(bf16[8,32,3072]{2,1,0:T(8,128)(2,1)S(1)} %reshape.127, bf16[8,32,64]{2,1,0:T(8,128)(2,1)} %get-tuple-element.11, bf16[8,32,64]{2,1,0:T(8,128)(2,1)} %get-tuple-element.10, bf16[8,32,64]{2,1,0:T(8,128)(2,1)S(1)} %get-tuple-element.9, bf16[8,32,64]{2,1,0:T(8,128)(2,1)S(1)} %broadcast_in_dim.44), dimensions={2} | concatenate | bytes 3407872 | tf_op jit(solution)/shard_map/concatenate | solution.py:103
  32.1 7.4 %all-to-all-start = ((bf16[8,32,3328]{2,1,0:T(8,128)(2,1)}), bf16[8,32,3328]{2,1,0:T(8,128)(2,1)S(1)}, u32[]{:S(2)}, u32[]{:S(2)}) async-start(bf16[8,32,3328]{2,1,0:T(8,128)(2,1)} %concatenate.10), calls=%async_computation | async-start | bytes 3407872 | tf_op jit(solution)/shard_map/all_to_all | solution.py:109
  39.5 1.0 maximum_bitcast_fusion
  41.4 2.1 %pad_maximum_fusion.1 = bf16[2,4,256,256]{3,2,1,0:T(8,128)(2,1)} fusion(bf16[1,4,256,256]{3,2,1,0:T(8,128)(2,1)} %bitcast.10, bf16[1,4,256,256]{3,2,1,0:T(8,128)(2,1)S(1)} %maximum_bitcast_fusion), kind=kLoop, calls=%fused_computation.24 | loop fusion | flops 524288 | bytes 2097152 | tf_op jit(solution)/shard_map/stack | solution.py:106
  43.5 1.6 %collective-permute-start.3 = (bf16[2,4,256,256]{3,2,1,0:T(8,128)(2,1)}, bf16[2,4,256,256]{3,2,1,0:T(8,128)(2,1)}, u32[]{:S(2)}, u32[]{:S(2)}) collective-permute-start(bf16[2,4,256,256]{3,2,1,0:T(8,128)(2,1)} %pad_maximum_fusion.1), channel_id=1, source_target_pairs={{0,1},{1,0},{2,3},{3,2},{4,5},{5,4},{6,7},{7,6},{8,9},{9,8},{10,11... | collective-permute-start | bytes 3145736 | tf_op jit(solution)/shard_map/ppermute | solution.py:107
  45.6 2.1 %collective-permute-done.3 = bf16[2,4,256,256]{3,2,1,0:T(8,128)(2,1)} collective-permute-done((bf16[2,4,256,256]{3,2,1,0:T(8,128)(2,1)}, bf16[2,4,256,256]{3,2,1,0:T(8,128)(2,1)}, u32[]{:S(2)}, u32[]{:S(2)}) %collective-permute-start.3) | collective-permute-done | bytes 1048608 | tf_op jit(solution)/shard_map/ppermute | solution.py:107
  47.7 3.1 %pad_maximum_fusion = bf16[4,4,256,256]{3,2,1,0:T(8,128)(2,1)} fusion(bf16[2,4,256,256]{3,2,1,0:T(8,128)(2,1)} %collective-permute-done.3, bf16[1,4,256,256]{3,2,1,0:T(8,128)(2,1)} %bitcast.10, bf16[1,4,256,256]{3,2,1,0:T(8,128)(2,1)} %copy-done.2), kind=kLoop, calls=%fused_computation.14 | loop fusion | flops 2097152 | bytes 4194304 | tf_op jit(solution)/shard_map/concatenate | solution.py:108
  50.8 17.7 %all-to-all-done = bf16[8,32,3328]{2,1,0:T(8,128)(2,1)S(1)} async-done(((bf16[8,32,3328]{2,1,0:T(8,128)(2,1)}), bf16[8,32,3328]{2,1,0:T(8,128)(2,1)S(1)}, u32[]{:S(2)}, u32[]{:S(2)}) %all-to-all-start) | async-done | bytes 1703968 | tf_op jit(solution)/shard_map/all_to_all | solution.py:109
  68.8 1.6 %fusion.17 = bf16[256,3072]{1,0:T(8,128)(2,1)S(1)} fusion(f32[3072]{0:T(1024)S(1)} %broadcast_multiply_fusion, bf16[256,3328]{1,0:T(8,128)(2,1)S(1)} %bitcast.89, s32[3072]{0:T(1024)S(1)} %add_select_fusion, f32[256,256]{1,0:T(8,128)S(1)} %slice_convert_fusion), kind=kOutput, calls=%fused_computation.13 | convolution fusion | flops 607354880 | bytes 3563520 | tf_op jit(solution)/shard_map/dot_general | solution.py:116
  70.4 7.8 %fusion.14 = bf16[256,3072]{1,0:T(8,128)(2,1)} fusion(bf16[16,256,256]{2,1,0:T(8,128)(2,1)S(1)} %bitcast.90, pred[16,3072]{1,0:T(8,128)(4,1)S(1)} %tile.9, bf16[256,3072]{1,0:T(8,128)(2,1)S(1)} %fusion.17, f32[3072]{0:T(1024)S(1)} %broadcast_multiply_fusion), kind=kOutput, calls=%fused_computation.12 | convolution fusion | flops 6457393152 | bytes 5304320 | tf_op jit(solution)/shard_map/rjk,rjx->kx/dot_general | solution.py:122
  78.2 3.9 %all-to-all-start.1 = ((bf16[8,32,3072]{2,1,0:T(8,128)(2,1)}), bf16[8,32,3072]{2,1,0:T(8,128)(2,1)S(1)}, u32[]{:S(2)}, u32[]{:S(2)}) async-start(bf16[8,32,3072]{2,1,0:T(8,128)(2,1)} %bitcast.91), calls=%async_computation.1 | async-start | bytes 3145728 | tf_op jit(solution)/shard_map/all_to_all | solution.py:126
  82.2 1.3 %gather_fusion = s32[128]{0:T(128)S(1)} fusion(s32[512]{0:T(512)S(1)} %fusion.52, s32[1024]{0:T(1024)S(1)} %pad_clamp_fusion), kind=kCustom, calls=%fused_computation | custom fusion | bytes 1536 | tf_op jit(solution)/shard_map/jit(_take)/gather | solution.py:133
  83.5 20.8 %all-to-all-done.1 = bf16[8,32,3072]{2,1,0:T(8,128)(2,1)S(1)} async-done(((bf16[8,32,3072]{2,1,0:T(8,128)(2,1)}), bf16[8,32,3072]{2,1,0:T(8,128)(2,1)S(1)}, u32[]{:S(2)}, u32[]{:S(2)}) %all-to-all-start.1) | async-done | bytes 1572896 | tf_op jit(solution)/shard_map/all_to_all | solution.py:126
  104.3 3.3 %reshape_reshape.3 = bf16[8,1536,64]{2,1,0:T(8,128)(2,1)} reshape(bf16[8,32,3072]{2,1,0:T(8,128)(2,1)S(1)} %all-to-all-done.1) | data formatting | bytes 3145728 | tf_op jit(solution)/shard_map/reshape;reshape | solution.py:128
  107.6 4.3 %convolution_bitcast_fusion.1 = bf16[32,48,512]{2,1,0:T(8,128)(2,1)} fusion(bf16[32,48,8,64]{3,1,0,2:T(8,128)(2,1)} %bitcast.85, s32[8,64]{1,0:T(8,128)S(1)} %multiply_add_fusion, s32[512]{0:T(512)S(1)} %fusion.52), kind=kOutput, calls=%fused_computation.17 | convolution fusion | flops 805568512 | bytes 3149824 | tf_op jit(solution)/shard_map/dni,cdi->nc/dot_general | solution.py:129
  112.7 1.1 fusion.59
  (44 shorter events, 4.5 us)
Async XLA Ops:
  0.6 19.0 %copy-start = (bf16[32,48,512]{2,1,0:T(8,128)(2,1)S(1)}, bf16[32,48,512]{2,1,0:T(8,128)(2,1)}, u32[]{:S(2)}) copy-start(bf16[32,48,512]{2,1,0:T(8,128)(2,1)} %param.6) | copy-start | bytes 4718596
  0.6 39.9 %collective-permute-start.2 = (bf16[4,256,256]{2,1,0:T(8,128)(2,1)}, bf16[4,256,256]{2,1,0:T(8,128)(2,1)}, u32[]{:S(2)}, u32[]{:S(2)}) collective-permute-start(bf16[4,256,256]{2,1,0:T(8,128)(2,1)} %param.8), channel_id=1, source_target_pairs={{8,0},{9,1},{14,2},{15,3},{12,4},{13,5},{18,6},{19,7},{16,8},{17,9... | collective-permute-start | bytes 1572872 | tf_op jit(solution)/shard_map/ppermute | solution.py:60
  10.4 21.7 %collective-permute-start = (bf16[1,256,256]{2,1,0:T(8,128)(2,1)S(1)}, bf16[1,256,256]{2,1,0:T(8,128)(2,1)S(1)}, u32[]{:S(2)}, u32[]{:S(2)}) collective-permute-start(bf16[1,256,256]{2,1,0:T(8,128)(2,1)S(1)} %slice.29), channel_id=1, source_target_pairs={{0,0},{1,1},{6,2},{7,3},{4,4},{5,5},{10,6},{11,7},{8,8},{9,9},{14,... | collective-permute-start | bytes 393224 | tf_op jit(solution)/shard_map/ppermute | solution.py:56
  12.9 26.6 %collective-permute-start.1 = (bf16[3,256,256]{2,1,0:T(8,128)(2,1)}, bf16[3,256,256]{2,1,0:T(8,128)(2,1)}, u32[]{:S(2)}, u32[]{:S(2)}) collective-permute-start(bf16[3,256,256]{2,1,0:T(8,128)(2,1)} %slice.31), channel_id=1, source_target_pairs={{0,0},{1,1},{6,2},{7,3},{4,4},{5,5},{10,6},{11,7},{8,8},{9,9},{14,... | collective-permute-start | bytes 1179656 | tf_op jit(solution)/shard_map/ppermute | solution.py:57
  23.0 4.0 %copy-start.4 = (f32[32,128]{1,0:T(8,128)S(1)}, f32[32,128]{1,0:T(8,128)}, u32[]{:S(2)}) copy-start(f32[32,128]{1,0:T(8,128)} %param.7) | copy-start | bytes 49156
  23.0 4.1 %copy-start.5 = (s32[512]{0:T(512)S(1)}, s32[512]{0:T(512)}, u32[]{:S(2)}) copy-start(s32[512]{0:T(512)} %param.9) | copy-start | bytes 6148
  32.1 36.4 %all-to-all-start = ((bf16[8,32,3328]{2,1,0:T(8,128)(2,1)}), bf16[8,32,3328]{2,1,0:T(8,128)(2,1)S(1)}, u32[]{:S(2)}, u32[]{:S(2)}) async-start(bf16[8,32,3328]{2,1,0:T(8,128)(2,1)} %concatenate.10), calls=%async_computation | async-start | bytes 3407872 | tf_op jit(solution)/shard_map/all_to_all | solution.py:109
  40.6 0.8 copy-start.2
  43.5 4.2 %collective-permute-start.3 = (bf16[2,4,256,256]{3,2,1,0:T(8,128)(2,1)}, bf16[2,4,256,256]{3,2,1,0:T(8,128)(2,1)}, u32[]{:S(2)}, u32[]{:S(2)}) collective-permute-start(bf16[2,4,256,256]{3,2,1,0:T(8,128)(2,1)} %pad_maximum_fusion.1), channel_id=1, source_target_pairs={{0,1},{1,0},{2,3},{3,2},{4,5},{5,4},{6,7},{7,6},{8,9},{9,8},{10,11... | collective-permute-start | bytes 3145736 | tf_op jit(solution)/shard_map/ppermute | solution.py:107
  68.8 1.6 %copy-start.3 = (bf16[4,4,256,256]{3,2,1,0:T(8,128)(2,1)S(1)}, bf16[4,4,256,256]{3,2,1,0:T(8,128)(2,1)}, u32[]{:S(2)}) copy-start(bf16[4,4,256,256]{3,2,1,0:T(8,128)(2,1)} %pad_maximum_fusion) | copy-start | bytes 6291460
  78.2 3.9 %copy-start.6 = (s32[128]{0:T(128)S(1)}, s32[128]{0:T(128)}, u32[]{:S(2)}) copy-start(s32[128]{0:T(128)} %param.11) | copy-start | bytes 1540
  78.2 26.1 %all-to-all-start.1 = ((bf16[8,32,3072]{2,1,0:T(8,128)(2,1)}), bf16[8,32,3072]{2,1,0:T(8,128)(2,1)S(1)}, u32[]{:S(2)}, u32[]{:S(2)}) async-start(bf16[8,32,3072]{2,1,0:T(8,128)(2,1)} %bitcast.91), calls=%async_computation.1 | async-start | bytes 3145728 | tf_op jit(solution)/shard_map/all_to_all | solution.py:126
  107.6 4.3 %copy-start.1 = (bf16[8,1536,64]{2,1,0:T(8,128)(2,1)S(1)}, bf16[8,1536,64]{2,1,0:T(8,128)(2,1)}, u32[]{:S(2)}) copy-start(bf16[8,1536,64]{2,1,0:T(8,128)(2,1)} %reshape_reshape.3) | copy-start | bytes 4718596
  111.9 0.8 copy-start.7
